TPU v7x, 512 devices: a whole 4x4x16 slice. The times are simulated.
512 devices in a mesh: ctx: 64 (over x, z_lo, core), head: 8 (over y, z_hi).
Axes of the slice: x: 4, y: 4, z: 16 (z_hi: 2, z_lo: 8; z = z_hi * 8 + z_lo), core: 2. Of those that a mesh axis runs over, the one named last changes fastest.
Arguments:
- queries: bfloat16 [16384, 2048], P('ctx', 'head'), may hold values from -40 to 40
- keys: bfloat16 [16384, 2048], P('ctx', 'head'), may hold values from -4 to 4
- values: bfloat16 [16384, 2048], P('ctx', 'head'), may hold values from -5 to 5
- selected: int32 [16, 512, 3], P('head', 'ctx'), may hold values from 0 to 63, as said below
- out_weight: bfloat16 [2048, 2048], P(None, 'head'), may hold values from -0.125 to 0.125
Outputs:
- projected: bfloat16 [16384, 2048], P('ctx', 'head')
Inputs may be any that keep to these rules, and one draw needn't show every extreme that they name: `selected`: entry 0 of a tile's selection is its own block; entries 1 and 2 are two different earlier blocks, or both the own block where no earlier block is chosen for the tile (one earlier block and the own block in the second key block). For each head, the tiles of one key block name any one other block at most 2 times, and exactly 2 times for every block they name, from the third key block on.
All inputs are finite; a program needn't handle non-finite values.
Results may differ from a plain program's by a relative error of at most 0.0054.
Values may be sent and summed in bfloat16 or wider, within the bound.
No kernel may reach another device: no remote copies, remote signals or barrier semaphores. Data moves between devices by JAX's collectives and lax.ppermute only.
A program may use at most 64 MiB of HBM per device.

v0:
```python
import math

import jax
import jax.numpy as jnp
from jax import lax
from jax.sharding import PartitionSpec as P

CAP = 2


def owner_block(group, keys_three, vals_three, scale):
    scores = (
        jnp.einsum("gchtd,khd->gchtk", group, keys_three, preferred_element_type=jnp.float32)
        * scale
    )
    top = jnp.max(scores, axis=-1)
    prob = jnp.exp(scores - top[..., None])
    total = jnp.sum(prob, axis=-1)
    part = jnp.einsum(
        "gchtk,khd->gchtd",
        prob.astype(jnp.bfloat16),
        vals_three,
        preferred_element_type=jnp.float32,
    )
    return (part / total[..., None], top + jnp.log(total))


def partials_back(outputs, sums):
    return (
        lax.all_to_all(outputs, "ctx", split_axis=0, concat_axis=0, tiled=True),
        lax.all_to_all(sums, "ctx", split_axis=0, concat_axis=0, tiled=True),
    )


def group_size(sources, rows_each):
    size = max(1, 512 // rows_each)
    size = min(size, sources)
    while sources % size != 0:
        size = size - 1
    return size


def local(queries, keys, values, selected, out_weight):
    heads_loc = selected.shape[0]
    tiles = selected.shape[1]
    tokens_here = queries.shape[0]
    width = queries.shape[1] // heads_loc
    tile_rows = tokens_here // tiles
    sources = lax.axis_size("ctx")
    mine = lax.axis_index("ctx")
    scale = width ** (-0.5)
    quer_three = queries.reshape(tokens_here, heads_loc, width)
    keys_three = keys.reshape(tokens_here, heads_loc, width)
    vals_three = values.reshape(tokens_here, heads_loc, width)
    rows_blk = math.gcd(tokens_here, 512)
    row_groups = tokens_here // rows_blk
    key_pos = jnp.arange(tokens_here, dtype=jnp.int32)

    def own_rows(args):
        query_rows, start = args
        scores = (
            jnp.einsum("rhd,khd->hrk", query_rows, keys_three, preferred_element_type=jnp.float32)
            * scale
        )
        allowed = (start + jnp.arange(rows_blk, dtype=jnp.int32))[:, None] >= key_pos[None, :]
        scores = jnp.where(allowed[None], scores, jnp.float32(-1e30))
        top = jnp.max(scores, axis=-1)
        prob = jnp.exp(scores - top[..., None])
        total = jnp.sum(prob, axis=-1)
        part = jnp.einsum(
            "hrk,khd->hrd",
            prob.astype(jnp.bfloat16),
            vals_three,
            preferred_element_type=jnp.float32,
        )
        return (part / total[..., None], top + jnp.log(total))

    own_out, own_lse = lax.map(
        own_rows,
        (
            quer_three.reshape(row_groups, rows_blk, heads_loc, width),
            jnp.arange(row_groups, dtype=jnp.int32) * rows_blk,
        ),
    )
    own_out = jnp.transpose(own_out, (1, 0, 2, 3)).reshape(heads_loc, tiles, tile_rows, width)
    own_lse = jnp.transpose(own_lse, (1, 0, 2)).reshape(heads_loc, tiles, tile_rows)
    picks = selected[:, :, 1:]
    valid = picks != mine
    target = jnp.where(valid, picks, sources)
    onehot = (target[..., None] == jnp.arange(sources, dtype=jnp.int32)).astype(jnp.int32)
    flat_hot = onehot.reshape(heads_loc, tiles * 2, sources)
    before = jnp.cumsum(flat_hot, axis=1) - flat_hot
    slot = jnp.sum(before * flat_hot, axis=-1).reshape(heads_loc, tiles, 2)
    head_idx = jnp.broadcast_to(
        jnp.arange(heads_loc, dtype=jnp.int32)[:, None, None], (heads_loc, tiles, 2)
    )
    query_src = jnp.transpose(quer_three.reshape(tiles, tile_rows, heads_loc, width), (2, 0, 1, 3))
    query_pairs = jnp.broadcast_to(query_src[:, :, None], (heads_loc, tiles, 2, tile_rows, width))
    send_q = jnp.zeros((sources, CAP, heads_loc, tile_rows, width), jnp.bfloat16)
    send_q = send_q.at[target, slot, head_idx].set(query_pairs, mode="drop")
    got_rows = lax.all_to_all(send_q, "ctx", split_axis=0, concat_axis=0, tiled=True)
    count = got_rows.shape[1]
    group_count = group_size(sources, count * heads_loc * tile_rows)
    query_groups = got_rows.reshape(
        sources // group_count, group_count, count, heads_loc, tile_rows, width
    )

    def one_group(group):
        return owner_block(group, keys_three, vals_three, scale)

    outputs, sums = lax.map(one_group, query_groups)
    got_out, got_lse = partials_back(
        outputs.reshape(sources, count, heads_loc, tile_rows, width),
        sums.reshape(sources, count, heads_loc, tile_rows),
    )
    clipped = jnp.clip(target, 0, sources - 1)
    pick_out = got_out[clipped, slot, head_idx]
    pick_lse = got_lse[clipped, slot, head_idx]
    keep = valid[..., None]
    top = jnp.maximum(own_lse, jnp.max(jnp.where(keep, pick_lse, own_lse[:, :, None]), axis=2))
    own_w = jnp.exp(own_lse - top)
    pick_w = jnp.exp(jnp.where(keep, pick_lse - top[:, :, None], jnp.float32(-1e30)))
    numer = own_w[..., None] * own_out + jnp.sum(pick_w[..., None] * pick_out, axis=2)
    denom = own_w + jnp.sum(pick_w, axis=2)
    attention = jnp.transpose(numer / denom[..., None], (1, 2, 0, 3)).reshape(
        tokens_here, heads_loc * width
    )
    attention = attention.astype(jnp.bfloat16)
    projected = jnp.dot(
        lax.all_gather(attention, "head", axis=1, tiled=True),
        out_weight,
        preferred_element_type=jnp.float32,
    )
    return projected.astype(jnp.bfloat16)


def solution(mesh):
    return jax.shard_map(
        local,
        mesh=mesh,
        in_specs=(
            P("ctx", "head"),
            P("ctx", "head"),
            P("ctx", "head"),
            P("head", "ctx", None),
            P(None, "head"),
        ),
        out_specs=P("ctx", "head"),
        check_vma=False,
    )
```

profile of v0, /device:TPU:6, one launch (start us, length us, event | category | flops | bytes accessed | tf_op | source)
XLA Modules:
  0.0 489.6 jit_solution(11999929789895695316)
XLA Ops:
  9.2 1.9 broadcast_in_dim.120
  11.1 4.2 scatter_fusion
  15.2 16.2 %all-to-all-start = ((bf16[64,2,2,32,128]{4,3,2,1,0:T(8,128)(2,1)}), bf16[64,2,2,32,128]{4,3,2,1,0:T(8,128)(2,1)S(1)}, u32[]{:S(2)}, u32[]{:S(2)}) async-start(bf16[64,2,2,32,128]{4,3,2,1,0:T(8,128)(2,1)} %scatter_fusion), calls=%async_computation | async-start | bytes 4194304 | tf_op jit(solution)/shard_map/all_to_all | solution.py:101
  33.5 92.6 %all-to-all-done = bf16[64,2,2,32,128]{4,3,2,1,0:T(8,128)(2,1)S(1)} async-done(((bf16[64,2,2,32,128]{4,3,2,1,0:T(8,128)(2,1)}), bf16[64,2,2,32,128]{4,3,2,1,0:T(8,128)(2,1)S(1)}, u32[]{:S(2)}, u32[]{:S(2)}) %all-to-all-start) | async-done | bytes 2097184 | tf_op jit(solution)/shard_map/all_to_all | solution.py:101
  126.0 50.5 %while.2 = (s32[]{:T(128)}, f32[16,4,2,2,32,128]{5,4,3,2,1,0:T(8,128)}, f32[16,4,2,2,32]{4,3,2,1,0:T(2,128)}, bf16[16,4,2,2,32,128]{5,4,3,2,1,0:T(8,128)(2,1)S(1...) while((s32[]{:T(128)}, f32[16,4,2,2,32,128]{5,4,3,2,1,0:T(8,128)}, ...), condition=%wide.region_8.9_spmd, body=%wide.region_5.8_spmd.sunk | while | flops 67960320 | bytes 2779233 | solution.py:111
  126.6 1.2 fusion.42
  129.8 1.2 fusion.42
  132.9 1.2 fusion.42
  136.1 1.2 fusion.42
  139.2 1.2 fusion.42
  142.4 1.2 fusion.42
  145.6 1.2 fusion.42
  148.7 1.2 fusion.42
  151.9 1.2 fusion.42
  158.2 1.2 fusion.42
  164.5 1.2 fusion.42
  170.9 1.2 fusion.42
  174.0 1.2 fusion.42
  177.6 20.1 %all_to_all.15 = f32[64,1,128]{2,1,0:T(1,128)S(1)} all-to-all(f32[64,1,128]{2,1,0:T(1,128)S(1)} %reshape.180), channel_id=1, replica_groups=mesh['ctx'=64,'head'=8] {'ctx'}, dimensions={0} | all-to-all | bytes 65536 | tf_op jit(solution)/shard_map/all_to_all | solution.py:31
  197.7 7.7 %all-to-all-start.2 = ((f32[64,2,2,32,128]{4,3,2,1,0:T(8,128)}), f32[64,2,2,32,128]{4,3,2,1,0:T(8,128)}, u32[]{:S(2)}, u32[]{:S(2)}) async-start(f32[64,2,2,32,128]{4,3,2,1,0:T(8,128)} %bitcast.87), calls=%async_computation.2 | async-start | bytes 8388608 | tf_op jit(solution)/shard_map/all_to_all | solution.py:30
  208.9 178.8 %all-to-all-done.2 = f32[64,2,2,32,128]{4,3,2,1,0:T(8,128)} async-done(((f32[64,2,2,32,128]{4,3,2,1,0:T(8,128)}), f32[64,2,2,32,128]{4,3,2,1,0:T(8,128)}, u32[]{:S(2)}, u32[]{:S(2)}) %all-to-all-start.2) | async-done | bytes 4194336 | tf_op jit(solution)/shard_map/all_to_all | solution.py:30
  387.7 2.8 gather_fusion.1
  391.9 88.6 %all-gather.2.cloned.1.call-done = bf16[256,2048]{1,0:T(8,128)(2,1)} async-done(((bf16[256,256]{1,0:T(8,128)(2,1)}), bf16[256,2048]{1,0:T(8,128)(2,1)}) %all-gather.2.cloned.1.call-update) | async-done | bytes 1048592 | tf_op jit(solution)/shard_map/all_gather | solution.py:130
  480.5 2.3 convolution_convert_fusion
  (134 shorter events, 45.0 us)
Async XLA Ops:
  6.5 473.9 %copy-start = (bf16[2048,256]{1,0:T(8,128)(2,1)S(1)}, bf16[2048,256]{1,0:T(8,128)(2,1)}, u32[]{:S(2)}) copy-start(bf16[2048,256]{1,0:T(8,128)(2,1)} %param.11) | copy-start | bytes 3145732
  6.5 24.9 %copy-start.2 = (bf16[256,256]{1,0:T(8,128)(2,1)S(1)}, bf16[256,256]{1,0:T(8,128)(2,1)}, u32[]{:S(2)}) copy-start(bf16[256,256]{1,0:T(8,128)(2,1)} %param.8) | copy-start | bytes 393220
  15.2 110.8 %all-to-all-start = ((bf16[64,2,2,32,128]{4,3,2,1,0:T(8,128)(2,1)}), bf16[64,2,2,32,128]{4,3,2,1,0:T(8,128)(2,1)S(1)}, u32[]{:S(2)}, u32[]{:S(2)}) async-start(bf16[64,2,2,32,128]{4,3,2,1,0:T(8,128)(2,1)} %scatter_fusion), calls=%async_computation | async-start | bytes 4194304 | tf_op jit(solution)/shard_map/all_to_all | solution.py:101
  197.7 8.0 %copy-start.1 = (bf16[256,256]{1,0:T(8,128)(2,1)S(1)}, bf16[256,256]{1,0:T(8,128)(2,1)}, u32[]{:S(2)}) copy-start(bf16[256,256]{1,0:T(8,128)(2,1)} %param.7) | copy-start | bytes 393220
  197.7 190.0 %all-to-all-start.2 = ((f32[64,2,2,32,128]{4,3,2,1,0:T(8,128)}), f32[64,2,2,32,128]{4,3,2,1,0:T(8,128)}, u32[]{:S(2)}, u32[]{:S(2)}) async-start(f32[64,2,2,32,128]{4,3,2,1,0:T(8,128)} %bitcast.87), calls=%async_computation.2 | async-start | bytes 8388608 | tf_op jit(solution)/shard_map/all_to_all | solution.py:30
  205.4 275.0 %all-gather.2.cloned.1.call-start = ((), (), s32[]{:S(2)}) async-start(), calls=%async_computation.3 | async-start | bytes 1179648 | tf_op jit(solution)/shard_map/all_gather | solution.py:130
Sparse Core Ops, SparseCore 0:
  392.0 88.4 all-gather.1
where the time goes:
time: 491 us; the launch traced here: 490 us
  waiting for transfers between devices  360 us (73%)
  local copies, waits for them, and re-layouts  37.3 us (8%)
  matrix products  26.9 us (5%)
  starting transfers between devices  23.9 us (5%)
  blocking collectives  20.1 us (4%)
  between operations  13.6 us (3%)
  other arithmetic  7.41 us (2%)
    all_to_all x1, waiting for transfers between devices, partials_back(): lax.all_to_all(outputs, 'ctx', split_axis=0, concat_axis=0, tiled=True)  179 us
    all_to_all x1, waiting for transfers between devices, local(): lax.all_to_all(send_q, 'ctx', split_axis=0, concat_axis=0, tiled=True)  92.6 us
    all_gather x1, waiting for transfers between devices, local(): lax.all_gather(attention, 'head', axis=1, tiled=True)  88.6 us
    dynamic_update_slice x32, local copies, waits for them, and re-layouts, local(): outputs, sums = lax.map(one_group, query_groups)  21.3 us
    all_to_all x1, blocking collectives, partials_back(): lax.all_to_all(sums, 'ctx', split_axis=0, concat_axis=0, tiled=True)  20.1 us
    dot_general x16, matrix products, owner_block(): jnp.einsum('gchtk,khd->gchtd', prob.astype(jnp.bfloat16), vals_three, pre...  19.1 us
    all_to_all x1, starting transfers between devices, local(): lax.all_to_all(send_q, 'ctx', split_axis=0, concat_axis=0, tiled=True)  16.2 us
  transfers between devices with their start and end apart: 3, of which 3 were waited for; matrix products, arithmetic and copies ran while one was open for 1% of the time, Pallas kernels for 0%

commit v1 on v0

v1 whole, which is shorter than its diff:
```python
import jax
import jax.numpy as jnp
from jax import lax
from jax.sharding import PartitionSpec as P

CAP = 2
LSE_ROWS = 16


def split_bf16(x):
    hi = lax.reduce_precision(x, exponent_bits=8, mantissa_bits=7)
    rest = x - hi
    mid = lax.reduce_precision(rest, exponent_bits=8, mantissa_bits=7)
    lo = rest - mid
    return jnp.stack([hi, mid, lo]).astype(jnp.bfloat16)


def join_bf16(parts):
    parts = parts.astype(jnp.float32)
    return parts[0] + (parts[1] + parts[2])


def softmax_pv(scores, vals):
    top = jnp.max(scores, axis=-1)
    prob = jnp.exp(scores - top[..., None])
    total = jnp.sum(prob, axis=-1)
    part = jnp.einsum(
        "hrk,khd->hrd", prob.astype(jnp.bfloat16), vals, preferred_element_type=jnp.float32
    )
    return part / total[..., None], top + jnp.log(total)


def local(queries, keys, values, selected, out_weight):
    heads_loc = selected.shape[0]
    tiles = selected.shape[1]
    tokens_here = queries.shape[0]
    width = queries.shape[1] // heads_loc
    tile_rows = tokens_here // tiles
    sources = lax.axis_size("ctx")
    mine = lax.axis_index("ctx")
    scale = width ** (-0.5)
    quer_three = queries.reshape(tokens_here, heads_loc, width)
    keys_three = keys.reshape(tokens_here, heads_loc, width)
    vals_three = values.reshape(tokens_here, heads_loc, width)

    pos = jnp.arange(tokens_here, dtype=jnp.int32)
    own_scores = (
        jnp.einsum("rhd,khd->hrk", quer_three, keys_three, preferred_element_type=jnp.float32)
        * scale
    )
    own_scores = jnp.where((pos[:, None] >= pos[None, :])[None], own_scores, jnp.float32(-1e30))
    own_out, own_lse = softmax_pv(own_scores, vals_three)
    own_out = own_out.reshape(heads_loc, tiles, tile_rows, width)
    own_lse = own_lse.reshape(heads_loc, tiles, tile_rows)

    picks = selected[:, :, 1:]
    valid = picks != mine
    target = jnp.where(valid, picks, sources)
    onehot = (target[..., None] == jnp.arange(sources, dtype=jnp.int32)).astype(jnp.int32)
    flat_hot = onehot.reshape(heads_loc, tiles * 2, sources)
    before = jnp.cumsum(flat_hot, axis=1) - flat_hot
    slot = jnp.sum(before * flat_hot, axis=-1).reshape(heads_loc, tiles, 2)
    head_idx = jnp.broadcast_to(
        jnp.arange(heads_loc, dtype=jnp.int32)[:, None, None], (heads_loc, tiles, 2)
    )
    query_src = jnp.transpose(quer_three.reshape(tiles, tile_rows, heads_loc, width), (2, 0, 1, 3))
    query_pairs = jnp.broadcast_to(query_src[:, :, None], (heads_loc, tiles, 2, tile_rows, width))
    send_q = jnp.zeros((sources, CAP, heads_loc, tile_rows, width), jnp.bfloat16)
    send_q = send_q.at[target, slot, head_idx].set(query_pairs, mode="drop")
    got_rows = lax.all_to_all(send_q, "ctx", split_axis=0, concat_axis=0, tiled=True)

    got_q = jnp.transpose(got_rows, (2, 0, 1, 3, 4)).reshape(
        heads_loc, sources * CAP * tile_rows, width
    )
    got_scores = (
        jnp.einsum("hrd,khd->hrk", got_q, keys_three, preferred_element_type=jnp.float32) * scale
    )
    part, lse = softmax_pv(got_scores, vals_three)
    part = jnp.transpose(
        part.reshape(heads_loc, sources, CAP, tile_rows, width), (1, 2, 0, 3, 4)
    ).reshape(sources, CAP * heads_loc * tile_rows, width)
    lse = jnp.transpose(lse.reshape(heads_loc, sources, CAP, tile_rows), (1, 2, 0, 3)).reshape(
        sources, CAP * heads_loc * tile_rows
    )
    lse_parts = jnp.transpose(split_bf16(lse), (1, 0, 2)).reshape(sources, -1, width)
    pad = -lse_parts.shape[1] % LSE_ROWS
    back = jnp.concatenate(
        [
            part.astype(jnp.bfloat16),
            lse_parts,
            jnp.zeros((sources, pad, width), jnp.bfloat16),
        ],
        axis=1,
    )
    got_back = lax.all_to_all(back, "ctx", split_axis=0, concat_axis=0, tiled=True)
    rows_part = CAP * heads_loc * tile_rows
    got_out = got_back[:, :rows_part].reshape(sources, CAP, heads_loc, tile_rows, width)
    got_lse = join_bf16(
        jnp.transpose(
            got_back[:, rows_part : rows_part + lse_parts.shape[1]].reshape(sources, 3, rows_part),
            (1, 0, 2),
        )
    ).reshape(sources, CAP, heads_loc, tile_rows)

    clipped = jnp.clip(target, 0, sources - 1)
    pick_out = got_out[clipped, slot, head_idx].astype(jnp.float32)
    pick_lse = got_lse[clipped, slot, head_idx]
    keep = valid[..., None]
    top = jnp.maximum(own_lse, jnp.max(jnp.where(keep, pick_lse, own_lse[:, :, None]), axis=2))
    own_w = jnp.exp(own_lse - top)
    pick_w = jnp.exp(jnp.where(keep, pick_lse - top[:, :, None], jnp.float32(-1e30)))
    numer = own_w[..., None] * own_out + jnp.sum(pick_w[..., None] * pick_out, axis=2)
    denom = own_w + jnp.sum(pick_w, axis=2)
    attention = jnp.transpose(numer / denom[..., None], (1, 2, 0, 3)).reshape(
        tokens_here, heads_loc * width
    )
    attention = attention.astype(jnp.bfloat16)
    projected = jnp.dot(
        lax.all_gather(attention, "head", axis=1, tiled=True),
        out_weight,
        preferred_element_type=jnp.float32,
    )
    return projected.astype(jnp.bfloat16)


def solution(mesh):
    return jax.shard_map(
        local,
        mesh=mesh,
        in_specs=(
            P("ctx", "head"),
            P("ctx", "head"),
            P("ctx", "head"),
            P("head", "ctx", None),
            P(None, "head"),
        ),
        out_specs=P("ctx", "head"),
        check_vma=False,
    )
```

time: 491 us -> 361 us (0.74)
  waiting for transfers between devices: 360 us -> 282 us
  blocking collectives: 20.1 us -> 0 us
  local copies, waits for them, and re-layouts: 37.3 us -> 19.9 us
  matrix products: 26.9 us -> 11.8 us
    all_to_all x1, waiting for transfers between devices: 179 us -> 100 us  [local(): lax.all_to_all(back, 'ctx', split_axis=0, concat_axis=0, tiled=True)]
    dynamic_update_slice x32 -> x0, local copies, waits for them, and re-layouts: 21.3 us -> none  [local(): outputs, sums = lax.map(one_group, query_groups)]
    all_to_all x1 -> x0, blocking collectives: 20.1 us -> none  [partials_back(): lax.all_to_all(sums, 'ctx', split_axis=0, concat_axis=0, tiled=True)]
    dot_general x34 -> x4, matrix products: 24.6 us -> 9.52 us  [the longest x2 7.1 us: softmax_pv(): jnp.einsum('hrk,khd->hrd', prob.astype(jnp.bfloat16), vals, preferred_ele...]
where the time goes in v1:
time: 361 us; the launch traced here: 360 us
  waiting for transfers between devices  282 us (78%)
  starting transfers between devices  26.2 us (7%)
  local copies, waits for them, and re-layouts  19.9 us (6%)
  between operations  13.7 us (4%)
  matrix products  11.8 us (3%)
  other arithmetic  6.85 us (2%)
    all_to_all x1, waiting for transfers between devices, local(): lax.all_to_all(back, 'ctx', split_axis=0, concat_axis=0, tiled=True)  100 us
    all_to_all x1, waiting for transfers between devices, local(): lax.all_to_all(send_q, 'ctx', split_axis=0, concat_axis=0, tiled=True)  94.5 us
    all_gather x1, waiting for transfers between devices, local(): lax.all_gather(attention, 'head', axis=1, tiled=True)  86.8 us
    all_to_all x1, starting transfers between devices, local(): lax.all_to_all(send_q, 'ctx', split_axis=0, concat_axis=0, tiled=True)  16.4 us
    all_to_all x1, starting transfers between devices, local(): lax.all_to_all(back, 'ctx', split_axis=0, concat_axis=0, tiled=True)  9.78 us
  transfers between devices with their start and end apart: 3, of which 3 were waited for; matrix products, arithmetic and copies ran while one was open for 1% of the time, Pallas kernels for 0%

profile of v1, /device:TPU:6, one launch (start us, length us, event | category | flops | bytes accessed | tf_op | source)
XLA Modules:
  0.0 360.1 jit_solution(8766354204228165098)
XLA Ops:
  6.5 1.3 fusion.32
  8.7 0.9 reshape_reshape.3
  9.7 1.9 broadcast_in_dim.55
  11.6 4.2 %scatter_fusion = bf16[64,2,2,32,128]{4,3,2,1,0:T(8,128)(2,1)} fusion(bf16[64,2,2,32,128]{4,3,2,1,0:T(8,128)(2,1)} %broadcast_in_dim.55, s32[32]{0:T(128)S(1)} %reshape.202, bf16[32,32,128]{2,1,0:T(8,128)(2,1)S(1)} %bitcast.87), kind=kCustom, calls=%fused_computation.2 | custom fusion | bytes 786816 | tf_op jit(solution)/shard_map/scatter | solution.py:69
  15.7 16.4 %all-to-all-start = ((bf16[64,2,2,32,128]{4,3,2,1,0:T(8,128)(2,1)}), bf16[64,2,2,32,128]{4,3,2,1,0:T(8,128)(2,1)S(1)}, u32[]{:S(2)}, u32[]{:S(2)}) async-start(bf16[64,2,2,32,128]{4,3,2,1,0:T(8,128)(2,1)} %scatter_fusion), calls=%async_computation | async-start | bytes 4194304 | tf_op jit(solution)/shard_map/all_to_all | solution.py:70
  32.2 94.5 %all-to-all-done = bf16[64,2,2,32,128]{4,3,2,1,0:T(8,128)(2,1)S(1)} async-done(((bf16[64,2,2,32,128]{4,3,2,1,0:T(8,128)(2,1)}), bf16[64,2,2,32,128]{4,3,2,1,0:T(8,128)(2,1)S(1)}, u32[]{:S(2)}, u32[]{:S(2)}) %all-to-all-start) | async-done | bytes 2097184 | tf_op jit(solution)/shard_map/all_to_all | solution.py:70
  127.4 1.3 multiply_reduce_fusion
  128.7 1.4 fusion
  130.1 1.8 copy-done.1
  132.4 5.0 %fusion.2 = bf16[2,4096,128]{2,1,0:T(8,128)(2,1)S(1)} fusion(f32[2,4096,256]{1,2,0:T(8,128)} %copy-done.1, f32[2,4096]{1,0:T(2,128)S(1)} %get-tuple-element.17, f32[2,4096]{1,0:T(2,128)S(1)} %fusion, bf16[256,256]{1,0:T(8,128)(2,1)S(1)} %copy-done.6), kind=kOutput, calls=%fused_computation.8 | convolution fusion | flops 545259520 | bytes 10682368 | tf_op jit(solution)/shard_map/hrk,khd->hrd/dot_general | solution.py:27
  138.0 1.9 maximum_maximum_fusion
  139.9 9.8 %all-to-all-start.1 = ((bf16[64,144,128]{2,1,0:T(8,128)(2,1)}), bf16[64,144,128]{2,1,0:T(8,128)(2,1)S(1)}, u32[]{:S(2)}, u32[]{:S(2)}) async-start(bf16[64,144,128]{2,1,0:T(8,128)(2,1)} %maximum_maximum_fusion), calls=%async_computation.1 | async-start | bytes 4718592 | tf_op jit(solution)/shard_map/all_to_all | solution.py:95
  150.0 1.1 fusion.36
  151.1 0.8 copy-done.2
  152.8 2.1 convolution_divide_fusion.1
  154.9 100.3 %all-to-all-done.1 = bf16[64,144,128]{2,1,0:T(8,128)(2,1)S(1)} async-done(((bf16[64,144,128]{2,1,0:T(8,128)(2,1)}), bf16[64,144,128]{2,1,0:T(8,128)(2,1)S(1)}, u32[]{:S(2)}, u32[]{:S(2)}) %all-to-all-start.1) | async-done | bytes 2359328 | tf_op jit(solution)/shard_map/all_to_all | solution.py:95
  255.3 0.7 copy.97
  256.1 1.0 copy.100
  257.0 1.6 slice.37
  258.7 2.3 gather_fusion.1
  261.0 0.7 gather_fusion
  262.1 1.2 fusion.19
  264.1 86.8 %all-gather.2.cloned.1.call-done = bf16[256,2048]{1,0:T(8,128)(2,1)} async-done(((bf16[256,256]{1,0:T(8,128)(2,1)}), bf16[256,2048]{1,0:T(8,128)(2,1)}) %all-gather.2.cloned.1.call-update) | async-done | bytes 1048592 | tf_op jit(solution)/shard_map/all_gather | solution.py:119
  350.9 2.3 convolution_convert_fusion
  (54 shorter events, 5.1 us)
Async XLA Ops:
  6.5 344.4 %copy-start = (bf16[2048,256]{1,0:T(8,128)(2,1)S(1)}, bf16[2048,256]{1,0:T(8,128)(2,1)}, u32[]{:S(2)}) copy-start(bf16[2048,256]{1,0:T(8,128)(2,1)} %param.9) | copy-start | bytes 3145732
  15.7 111.6 %copy-start.4 = (bf16[256,256]{1,0:T(8,128)(2,1)S(1)}, bf16[256,256]{1,0:T(8,128)(2,1)}, u32[]{:S(2)}) copy-start(bf16[256,256]{1,0:T(8,128)(2,1)} %param.6) | copy-start | bytes 393220
  15.7 110.9 %all-to-all-start = ((bf16[64,2,2,32,128]{4,3,2,1,0:T(8,128)(2,1)}), bf16[64,2,2,32,128]{4,3,2,1,0:T(8,128)(2,1)S(1)}, u32[]{:S(2)}, u32[]{:S(2)}) async-start(bf16[64,2,2,32,128]{4,3,2,1,0:T(8,128)(2,1)} %scatter_fusion), calls=%async_computation | async-start | bytes 4194304 | tf_op jit(solution)/shard_map/all_to_all | solution.py:70
  128.7 3.2 copy-start.1
  128.7 3.7 %copy-start.6 = (bf16[256,256]{1,0:T(8,128)(2,1)S(1)}, bf16[256,256]{1,0:T(8,128)(2,1)}, u32[]{:S(2)}) copy-start(bf16[256,256]{1,0:T(8,128)(2,1)} %param.7) | copy-start | bytes 393220
  137.9 12.0 %copy-start.3 = (bf16[256,256]{1,0:T(8,128)(2,1)S(1)}, bf16[256,256]{1,0:T(8,128)(2,1)}, u32[]{:S(2)}) copy-start(bf16[256,256]{1,0:T(8,128)(2,1)} %param.5) | copy-start | bytes 393220
  139.9 115.3 %all-to-all-start.1 = ((bf16[64,144,128]{2,1,0:T(8,128)(2,1)}), bf16[64,144,128]{2,1,0:T(8,128)(2,1)S(1)}, u32[]{:S(2)}, u32[]{:S(2)}) async-start(bf16[64,144,128]{2,1,0:T(8,128)(2,1)} %maximum_maximum_fusion), calls=%async_computation.1 | async-start | bytes 4718592 | tf_op jit(solution)/shard_map/all_to_all | solution.py:95
  149.7 201.2 %all-gather.2.cloned.1.call-start = ((), (), s32[]{:S(2)}) async-start(), calls=%async_computation.2 | async-start | bytes 1179648 | tf_op jit(solution)/shard_map/all_gather | solution.py:119
  151.1 0.8 copy-start.2
  151.1 0.9 copy-start.5
Sparse Core Ops, SparseCore 0:
  264.2 86.6 all-gather.1

commit v2 on v1

--- a/solution.py
+++ b/solution.py
@@ -1,7 +1,7 @@
 import jax
 import jax.numpy as jnp
 from jax import lax
-from jax.sharding import PartitionSpec as P
+from jax.sharding import Mesh, PartitionSpec as P
 
 CAP = 2
 LSE_ROWS = 16
@@ -115,8 +115,10 @@
         tokens_here, heads_loc * width
     )
     attention = attention.astype(jnp.bfloat16)
+    gathered = lax.all_gather(attention, "zh", axis=1, tiled=True)
+    gathered = lax.all_gather(gathered, "y", axis=1, tiled=True)
     projected = jnp.dot(
-        lax.all_gather(attention, "head", axis=1, tiled=True),
+        gathered,
         out_weight,
         preferred_element_type=jnp.float32,
     )
@@ -124,16 +126,19 @@
 
 
 def solution(mesh):
+    ctx_n, head_n = mesh.devices.shape
+    split = Mesh(mesh.devices.reshape(ctx_n, head_n // 2, 2), ("ctx", "y", "zh"))
+    head = ("y", "zh")
     return jax.shard_map(
         local,
-        mesh=mesh,
+        mesh=split,
         in_specs=(
-            P("ctx", "head"),
-            P("ctx", "head"),
-            P("ctx", "head"),
-            P("head", "ctx", None),
-            P(None, "head"),
+            P("ctx", head),
+            P("ctx", head),
+            P("ctx", head),
+            P(head, "ctx", None),
+            P(None, head),
         ),
-        out_specs=P("ctx", "head"),
+        out_specs=P("ctx", head),
         check_vma=False,
     )

time: 361 us -> 325 us (0.900)
  waiting for transfers between devices: 282 us -> 223 us
  blocking collectives: 0 us -> 23.7 us
    all_gather x1, waiting for transfers between devices: 86.8 us -> 28 us  [local(): gathered = lax.all_gather(gathered, 'y', axis=1, tiled=True)]
    all_gather x0 -> x1, blocking collectives: none -> 23.7 us  [local(): gathered = lax.all_gather(attention, 'zh', axis=1, tiled=True)]
where the time goes in v2:
time: 325 us; the launch traced here: 324 us
  waiting for transfers between devices  223 us (69%)
  starting transfers between devices  26.2 us (8%)
  blocking collectives  23.7 us (7%)
  local copies, waits for them, and re-layouts  19.3 us (6%)
  between operations  13.7 us (4%)
  matrix products  11.8 us (4%)
  other arithmetic  6.85 us (2%)
    all_to_all x1, waiting for transfers between devices, local(): lax.all_to_all(back, 'ctx', split_axis=0, concat_axis=0, tiled=True)  100 us
    all_to_all x1, waiting for transfers between devices, local(): lax.all_to_all(send_q, 'ctx', split_axis=0, concat_axis=0, tiled=True)  94.5 us
    all_gather x1, waiting for transfers between devices, local(): gathered = lax.all_gather(gathered, 'y', axis=1, tiled=True)  28 us
    all_gather x1, blocking collectives, local(): gathered = lax.all_gather(attention, 'zh', axis=1, tiled=True)  23.7 us
    all_to_all x1, starting transfers between devices, local(): lax.all_to_all(send_q, 'ctx', split_axis=0, concat_axis=0, tiled=True)  16.3 us
    all_to_all x1, starting transfers between devices, local(): lax.all_to_all(back, 'ctx', split_axis=0, concat_axis=0, tiled=True)  9.78 us
    dot_general x2, matrix products, softmax_pv(): jnp.einsum('hrk,khd->hrd', prob.astype(jnp.bfloat16), vals, preferred_ele...  7.1 us
  transfers between devices with their start and end apart: 3, of which 3 were waited for; matrix products, arithmetic and copies ran while one was open for 1% of the time, Pallas kernels for 0%

profile of v2, /device:TPU:6, one launch (start us, length us, event | category | flops | bytes accessed | tf_op | source)
XLA Modules:
  0.0 324.3 jit_solution(3656303859149430648)
XLA Ops:
  6.5 1.3 fusion.32
  8.7 0.9 reshape_reshape.3
  9.7 1.9 broadcast_in_dim.55
  11.6 4.2 %scatter_fusion = bf16[64,2,2,32,128]{4,3,2,1,0:T(8,128)(2,1)} fusion(bf16[64,2,2,32,128]{4,3,2,1,0:T(8,128)(2,1)} %broadcast_in_dim.55, s32[32]{0:T(128)S(1)} %reshape.202, bf16[32,32,128]{2,1,0:T(8,128)(2,1)S(1)} %bitcast.87), kind=kCustom, calls=%fused_computation.2 | custom fusion | bytes 786816 | tf_op jit(solution)/shard_map/scatter | solution.py:69
  15.8 16.3 %all-to-all-start = ((bf16[64,2,2,32,128]{4,3,2,1,0:T(8,128)(2,1)}), bf16[64,2,2,32,128]{4,3,2,1,0:T(8,128)(2,1)S(1)}, u32[]{:S(2)}, u32[]{:S(2)}) async-start(bf16[64,2,2,32,128]{4,3,2,1,0:T(8,128)(2,1)} %scatter_fusion), calls=%async_computation | async-start | bytes 4194304 | tf_op jit(solution)/shard_map/all_to_all | solution.py:70
  32.2 94.5 %all-to-all-done = bf16[64,2,2,32,128]{4,3,2,1,0:T(8,128)(2,1)S(1)} async-done(((bf16[64,2,2,32,128]{4,3,2,1,0:T(8,128)(2,1)}), bf16[64,2,2,32,128]{4,3,2,1,0:T(8,128)(2,1)S(1)}, u32[]{:S(2)}, u32[]{:S(2)}) %all-to-all-start) | async-done | bytes 2097184 | tf_op jit(solution)/shard_map/all_to_all | solution.py:70
  127.4 1.3 multiply_reduce_fusion
  128.7 1.4 fusion
  130.1 1.8 copy-done.1
  132.4 5.0 %fusion.2 = bf16[2,4096,128]{2,1,0:T(8,128)(2,1)S(1)} fusion(f32[2,4096,256]{1,2,0:T(8,128)} %copy-done.1, f32[2,4096]{1,0:T(2,128)S(1)} %get-tuple-element.17, f32[2,4096]{1,0:T(2,128)S(1)} %fusion, bf16[256,256]{1,0:T(8,128)(2,1)S(1)} %copy-done.6), kind=kOutput, calls=%fused_computation.8 | convolution fusion | flops 545259520 | bytes 10682368 | tf_op jit(solution)/shard_map/hrk,khd->hrd/dot_general | solution.py:27
  137.9 1.9 maximum_maximum_fusion
  139.9 9.8 %all-to-all-start.1 = ((bf16[64,144,128]{2,1,0:T(8,128)(2,1)}), bf16[64,144,128]{2,1,0:T(8,128)(2,1)S(1)}, u32[]{:S(2)}, u32[]{:S(2)}) async-start(bf16[64,144,128]{2,1,0:T(8,128)(2,1)} %maximum_maximum_fusion), calls=%async_computation.1 | async-start | bytes 4718592 | tf_op jit(solution)/shard_map/all_to_all | solution.py:95
  149.9 1.1 fusion.36
  151.1 0.8 copy-done.2
  152.8 2.1 convolution_divide_fusion.1
  154.9 100.3 %all-to-all-done.1 = bf16[64,144,128]{2,1,0:T(8,128)(2,1)S(1)} async-done(((bf16[64,144,128]{2,1,0:T(8,128)(2,1)}), bf16[64,144,128]{2,1,0:T(8,128)(2,1)S(1)}, u32[]{:S(2)}, u32[]{:S(2)}) %all-to-all-start.1) | async-done | bytes 2359328 | tf_op jit(solution)/shard_map/all_to_all | solution.py:95
  255.3 0.7 copy.97
  256.0 1.0 copy.100
  257.0 1.6 slice.37
  258.6 2.3 gather_fusion.1
  262.1 1.2 fusion.19
  263.4 23.7 %all_gather.6 = bf16[256,512]{1,0:T(8,128)(2,1)} all-gather(bf16[256,256]{1,0:T(8,128)(2,1)S(1)} %bitcast.89), channel_id=1, replica_groups=mesh['ctx'=64,'y'=4,'zh'=2] {'zh'}, dimensions={1}, use_global_device_ids=true | all-gather | bytes 393216 | tf_op jit(solution)/shard_map/all_gather | solution.py:118
  287.1 28.0 %all-gather.2.cloned.1.call-done = bf16[256,2048]{1,0:T(8,128)(2,1)} async-done(((bf16[256,512]{1,0:T(8,128)(2,1)}), bf16[256,2048]{1,0:T(8,128)(2,1)}) %all-gather.2.cloned.1.call-update) | async-done | bytes 1048592 | tf_op jit(solution)/shard_map/all_gather | solution.py:119
  315.2 2.3 convolution_convert_fusion
  (55 shorter events, 5.2 us)
Async XLA Ops:
  6.5 308.6 %copy-start = (bf16[2048,256]{1,0:T(8,128)(2,1)S(1)}, bf16[2048,256]{1,0:T(8,128)(2,1)}, u32[]{:S(2)}) copy-start(bf16[2048,256]{1,0:T(8,128)(2,1)} %param.9) | copy-start | bytes 3145732
  15.8 111.6 %copy-start.4 = (bf16[256,256]{1,0:T(8,128)(2,1)S(1)}, bf16[256,256]{1,0:T(8,128)(2,1)}, u32[]{:S(2)}) copy-start(bf16[256,256]{1,0:T(8,128)(2,1)} %param.6) | copy-start | bytes 393220
  15.8 110.9 %all-to-all-start = ((bf16[64,2,2,32,128]{4,3,2,1,0:T(8,128)(2,1)}), bf16[64,2,2,32,128]{4,3,2,1,0:T(8,128)(2,1)S(1)}, u32[]{:S(2)}, u32[]{:S(2)}) async-start(bf16[64,2,2,32,128]{4,3,2,1,0:T(8,128)(2,1)} %scatter_fusion), calls=%async_computation | async-start | bytes 4194304 | tf_op jit(solution)/shard_map/all_to_all | solution.py:70
  128.6 3.2 copy-start.1
  128.7 3.7 %copy-start.6 = (bf16[256,256]{1,0:T(8,128)(2,1)S(1)}, bf16[256,256]{1,0:T(8,128)(2,1)}, u32[]{:S(2)}) copy-start(bf16[256,256]{1,0:T(8,128)(2,1)} %param.7) | copy-start | bytes 393220
  137.9 12.0 %copy-start.3 = (bf16[256,256]{1,0:T(8,128)(2,1)S(1)}, bf16[256,256]{1,0:T(8,128)(2,1)}, u32[]{:S(2)}) copy-start(bf16[256,256]{1,0:T(8,128)(2,1)} %param.5) | copy-start | bytes 393220
  139.9 115.3 %all-to-all-start.1 = ((bf16[64,144,128]{2,1,0:T(8,128)(2,1)}), bf16[64,144,128]{2,1,0:T(8,128)(2,1)S(1)}, u32[]{:S(2)}, u32[]{:S(2)}) async-start(bf16[64,144,128]{2,1,0:T(8,128)(2,1)} %maximum_maximum_fusion), calls=%async_computation.1 | async-start | bytes 4718592 | tf_op jit(solution)/shard_map/all_to_all | solution.py:95
  149.7 165.5 %all-gather.2.cloned.1.call-start = ((), (), s32[]{:S(2)}) async-start(), calls=%async_computation.2 | async-start | bytes 1310720 | tf_op jit(solution)/shard_map/all_gather | solution.py:119
  151.1 0.8 copy-start.2
  151.1 0.9 copy-start.5
Sparse Core Ops, SparseCore 0:
  287.3 27.8 all-gather.1

commit v3 on v2

--- a/solution.py
+++ b/solution.py
@@ -65,9 +65,18 @@
     )
     query_src = jnp.transpose(quer_three.reshape(tiles, tile_rows, heads_loc, width), (2, 0, 1, 3))
     query_pairs = jnp.broadcast_to(query_src[:, :, None], (heads_loc, tiles, 2, tile_rows, width))
+    shift = jnp.where(valid, mine - picks, 0)
     send_q = jnp.zeros((sources, CAP, heads_loc, tile_rows, width), jnp.bfloat16)
-    send_q = send_q.at[target, slot, head_idx].set(query_pairs, mode="drop")
-    got_rows = lax.all_to_all(send_q, "ctx", split_axis=0, concat_axis=0, tiled=True)
+    send_q = send_q.at[jnp.where(valid, shift, sources), slot, head_idx].set(
+        query_pairs, mode="drop"
+    )
+    got_rows = jnp.stack(
+        [jnp.zeros_like(send_q[0])]
+        + [
+            lax.ppermute(send_q[s], "ctx", [(b, b - s) for b in range(s, sources)])
+            for s in range(1, sources)
+        ]
+    )
 
     got_q = jnp.transpose(got_rows, (2, 0, 1, 3, 4)).reshape(
         heads_loc, sources * CAP * tile_rows, width
@@ -92,7 +101,13 @@
         ],
         axis=1,
     )
-    got_back = lax.all_to_all(back, "ctx", split_axis=0, concat_axis=0, tiled=True)
+    got_back = jnp.stack(
+        [jnp.zeros_like(back[0])]
+        + [
+            lax.ppermute(back[s], "ctx", [(d, d + s) for d in range(0, sources - s)])
+            for s in range(1, sources)
+        ]
+    )
     rows_part = CAP * heads_loc * tile_rows
     got_out = got_back[:, :rows_part].reshape(sources, CAP, heads_loc, tile_rows, width)
     got_lse = join_bf16(
@@ -102,9 +117,8 @@
         )
     ).reshape(sources, CAP, heads_loc, tile_rows)
 
-    clipped = jnp.clip(target, 0, sources - 1)
-    pick_out = got_out[clipped, slot, head_idx].astype(jnp.float32)
-    pick_lse = got_lse[clipped, slot, head_idx]
+    pick_out = got_out[shift, slot, head_idx].astype(jnp.float32)
+    pick_lse = got_lse[shift, slot, head_idx]
     keep = valid[..., None]
     top = jnp.maximum(own_lse, jnp.max(jnp.where(keep, pick_lse, own_lse[:, :, None]), axis=2))
     own_w = jnp.exp(own_lse - top)

time: 325 us -> 1920 us (5.91)
  starting transfers between devices: 26.2 us -> 1780 us
  waiting for transfers between devices: 223 us -> 72.1 us
    ppermute x0 -> x126, starting transfers between devices: none -> 1780 us  [the longest x63 891 us: local(): lax.ppermute(back[s], 'ctx', [(d, d + s) for d in range(0, sources - s)])]
    all_to_all x2 -> x0, waiting for transfers between devices: 195 us -> none  [the longest x1 100 us: local(): lax.all_to_all(back, 'ctx', split_axis=0, concat_axis=0, tiled=True)]
    all_gather x1, waiting for transfers between devices: 28 us -> 59.2 us  [local(): gathered = lax.all_gather(gathered, 'y', axis=1, tiled=True)]
    all_to_all x2 -> x0, starting transfers between devices: 26.1 us -> none  [the longest x1 16.3 us: local(): lax.all_to_all(send_q, 'ctx', split_axis=0, concat_axis=0, tiled=True)]
  transfers between devices with their start and end apart: 3 -> 127, of which waited for: 3 -> 4; matrix products, arithmetic and copies ran while one was open for 1% -> 1% of each run, Pallas kernels for 0% -> 0%
where the time goes in v3:
time: 1920 us
  starting transfers between devices  1780 us (93%)
  waiting for transfers between devices  72.1 us (4%)
  local copies, waits for them, and re-layouts  19.5 us (1%)
    ppermute x63, starting transfers between devices, local(): lax.ppermute(back[s], 'ctx', [(d, d + s) for d in range(0, sources - s)])  891 us
    ppermute x63, starting transfers between devices, local(): lax.ppermute(send_q[s], 'ctx', [(b, b - s) for b in range(s, sources)])  889 us
    all_gather x1, waiting for transfers between devices, local(): gathered = lax.all_gather(gathered, 'y', axis=1, tiled=True)  59.2 us
  transfers between devices with their start and end apart: 127, of which 4 were waited for; matrix products, arithmetic and copies ran while one was open for 1% of the time, Pallas kernels for 0%

profile of v3, /device:TPU:6, one launch (start us, length us, event | category | flops | bytes accessed | tf_op | source)
XLA Modules:
  0.0 1918.0 jit_solution(1472618239134992338)
XLA Ops:
  13.9 20.7 %collective-permute-start = (bf16[2,2,32,128]{3,2,1,0:T(8,128)(2,1)}, bf16[2,2,32,128]{3,2,1,0:T(8,128)(2,1)}, u32[]{:S(2)}, u32[]{:S(2)}) collective-permute-start(bf16[2,2,32,128]{3,2,1,0:T(8,128)(2,1)} %get-tuple-element.136), channel_id=1, source_target_pairs={{8,0},{16,8},{24,16},{32,24},{40,32},{48,40},{56,48},{64,56},{72,6... | collective-permute-start | bytes 98312 | tf_op jit(solution)/shard_map/ppermute | solution.py:76
  34.5 19.0 collective-permute-start.1
  53.5 19.0 collective-permute-start.2
  72.6 19.0 collective-permute-start.3
  91.6 19.1 collective-permute-start.4
  925.2 49.6 %collective-permute-start.63 = (bf16[144,128]{1,0:T(8,128)(2,1)S(1)}, bf16[144,128]{1,0:T(8,128)(2,1)S(1)}, u32[]{:S(2)}, u32[]{:S(2)}) collective-permute-start(bf16[144,128]{1,0:T(8,128)(2,1)S(1)} %get-tuple-element.73), channel_id=1, source_target_pairs={{0,8},{8,16},{16,24},{24,32},{32,40},{40,48},{48,56},{56,64},{64,7... | collective-permute-start | bytes 110600 | tf_op jit(solution)/shard_map/ppermute | solution.py:107
  1012.8 19.0 collective-permute-start.66
  1259.7 19.0 collective-permute-start.79
  1278.7 19.0 collective-permute-start.80
  1297.8 19.0 collective-permute-start.81
  1316.8 19.0 collective-permute-start.82
  1335.8 19.0 collective-permute-start.83
  1354.9 19.0 collective-permute-start.84
  1373.9 19.0 collective-permute-start.85
  1393.0 19.0 collective-permute-start.86
  1412.0 19.0 collective-permute-start.87
  1431.0 19.0 collective-permute-start.88
  1450.1 19.0 collective-permute-start.89
  1469.1 19.0 collective-permute-start.90
  1488.2 19.0 collective-permute-start.91
  1507.2 19.0 collective-permute-start.92
  1526.2 19.0 collective-permute-start.93
  1545.3 19.0 collective-permute-start.94
  1849.7 59.2 %all-gather.2.cloned.1.call-done = bf16[256,2048]{1,0:T(8,128)(2,1)} async-done(((bf16[256,512]{1,0:T(8,128)(2,1)}), bf16[256,2048]{1,0:T(8,128)(2,1)}) %all-gather.2.cloned.1.call-update) | async-done | bytes 1048592 | tf_op jit(solution)/shard_map/all_gather | solution.py:133
  (481 shorter events, 1373.0 us)
Async XLA Ops:
  6.5 1902.3 %all-gather.2.cloned.1.call-start = ((), (), s32[]{:S(2)}) async-start(), calls=%async_computation | async-start | bytes 1310720 | tf_op jit(solution)/shard_map/all_gather | solution.py:133
  13.9 104.7 %collective-permute-start = (bf16[2,2,32,128]{3,2,1,0:T(8,128)(2,1)}, bf16[2,2,32,128]{3,2,1,0:T(8,128)(2,1)}, u32[]{:S(2)}, u32[]{:S(2)}) collective-permute-start(bf16[2,2,32,128]{3,2,1,0:T(8,128)(2,1)} %get-tuple-element.136), channel_id=1, source_target_pairs={{8,0},{16,8},{24,16},{32,24},{40,32},{48,40},{56,48},{64,56},{72,6... | collective-permute-start | bytes 98312 | tf_op jit(solution)/shard_map/ppermute | solution.py:76
  34.5 103.8 %collective-permute-start.1 = (bf16[2,2,32,128]{3,2,1,0:T(8,128)(2,1)}, bf16[2,2,32,128]{3,2,1,0:T(8,128)(2,1)}, u32[]{:S(2)}, u32[]{:S(2)}) collective-permute-start(bf16[2,2,32,128]{3,2,1,0:T(8,128)(2,1)} %get-tuple-element.135), channel_id=1, source_target_pairs={{16,0},{24,8},{32,16},{40,24},{48,32},{56,40},{64,48},{72,56},{80,... | collective-permute-start | bytes 98312 | tf_op jit(solution)/shard_map/ppermute | solution.py:76
  53.5 104.5 %collective-permute-start.2 = (bf16[2,2,32,128]{3,2,1,0:T(8,128)(2,1)}, bf16[2,2,32,128]{3,2,1,0:T(8,128)(2,1)}, u32[]{:S(2)}, u32[]{:S(2)}) collective-permute-start(bf16[2,2,32,128]{3,2,1,0:T(8,128)(2,1)} %get-tuple-element.134), channel_id=1, source_target_pairs={{24,0},{32,8},{40,16},{48,24},{56,32},{64,40},{72,48},{80,56},{88,... | collective-permute-start | bytes 98312 | tf_op jit(solution)/shard_map/ppermute | solution.py:76
  72.6 105.3 %collective-permute-start.3 = (bf16[2,2,32,128]{3,2,1,0:T(8,128)(2,1)}, bf16[2,2,32,128]{3,2,1,0:T(8,128)(2,1)}, u32[]{:S(2)}, u32[]{:S(2)}) collective-permute-start(bf16[2,2,32,128]{3,2,1,0:T(8,128)(2,1)} %get-tuple-element.133), channel_id=1, source_target_pairs={{32,0},{40,8},{48,16},{56,24},{64,32},{72,40},{80,48},{88,56},{96,... | collective-permute-start | bytes 98312 | tf_op jit(solution)/shard_map/ppermute | solution.py:76
  91.6 106.0 %collective-permute-start.4 = (bf16[2,2,32,128]{3,2,1,0:T(8,128)(2,1)}, bf16[2,2,32,128]{3,2,1,0:T(8,128)(2,1)}, u32[]{:S(2)}, u32[]{:S(2)}) collective-permute-start(bf16[2,2,32,128]{3,2,1,0:T(8,128)(2,1)} %get-tuple-element.132), channel_id=1, source_target_pairs={{40,0},{48,8},{56,16},{64,24},{72,32},{80,40},{88,48},{96,56},{104... | collective-permute-start | bytes 98312 | tf_op jit(solution)/shard_map/ppermute | solution.py:76
  118.5 98.9 %collective-permute-start.5 = (bf16[2,2,32,128]{3,2,1,0:T(8,128)(2,1)}, bf16[2,2,32,128]{3,2,1,0:T(8,128)(2,1)S(1)}, u32[]{:S(2)}, u32[]{:S(2)}) collective-permute-start(bf16[2,2,32,128]{3,2,1,0:T(8,128)(2,1)} %get-tuple-element.131), channel_id=1, source_target_pairs={{48,0},{56,8},{64,16},{72,24},{80,32},{88,40},{96,48},{104,56},{11... | collective-permute-start | bytes 98312 | tf_op jit(solution)/shard_map/ppermute | solution.py:76
  138.3 98.1 %collective-permute-start.6 = (bf16[2,2,32,128]{3,2,1,0:T(8,128)(2,1)}, bf16[2,2,32,128]{3,2,1,0:T(8,128)(2,1)S(1)}, u32[]{:S(2)}, u32[]{:S(2)}) collective-permute-start(bf16[2,2,32,128]{3,2,1,0:T(8,128)(2,1)} %get-tuple-element.130), channel_id=1, source_target_pairs={{56,0},{64,8},{72,16},{80,24},{88,32},{96,40},{104,48},{112,56},{1... | collective-permute-start | bytes 98312 | tf_op jit(solution)/shard_map/ppermute | solution.py:76
  158.1 97.4 %collective-permute-start.7 = (bf16[2,2,32,128]{3,2,1,0:T(8,128)(2,1)}, bf16[2,2,32,128]{3,2,1,0:T(8,128)(2,1)S(1)}, u32[]{:S(2)}, u32[]{:S(2)}) collective-permute-start(bf16[2,2,32,128]{3,2,1,0:T(8,128)(2,1)} %get-tuple-element.129), channel_id=1, source_target_pairs={{64,0},{72,8},{80,16},{88,24},{96,32},{104,40},{112,48},{120,56},{... | collective-permute-start | bytes 98312 | tf_op jit(solution)/shard_map/ppermute | solution.py:76
  177.9 96.7 %collective-permute-start.8 = (bf16[2,2,32,128]{3,2,1,0:T(8,128)(2,1)}, bf16[2,2,32,128]{3,2,1,0:T(8,128)(2,1)S(1)}, u32[]{:S(2)}, u32[]{:S(2)}) collective-permute-start(bf16[2,2,32,128]{3,2,1,0:T(8,128)(2,1)} %get-tuple-element.128), channel_id=1, source_target_pairs={{72,0},{80,8},{88,16},{96,24},{104,32},{112,40},{120,48},{128,56},... | collective-permute-start | bytes 98312 | tf_op jit(solution)/shard_map/ppermute | solution.py:76
  197.6 95.9 %collective-permute-start.9 = (bf16[2,2,32,128]{3,2,1,0:T(8,128)(2,1)}, bf16[2,2,32,128]{3,2,1,0:T(8,128)(2,1)S(1)}, u32[]{:S(2)}, u32[]{:S(2)}) collective-permute-start(bf16[2,2,32,128]{3,2,1,0:T(8,128)(2,1)} %get-tuple-element.127), channel_id=1, source_target_pairs={{80,0},{88,8},{96,16},{104,24},{112,32},{120,40},{128,48},{136,56}... | collective-permute-start | bytes 98312 | tf_op jit(solution)/shard_map/ppermute | solution.py:76
  925.2 125.7 %collective-permute-start.63 = (bf16[144,128]{1,0:T(8,128)(2,1)S(1)}, bf16[144,128]{1,0:T(8,128)(2,1)S(1)}, u32[]{:S(2)}, u32[]{:S(2)}) collective-permute-start(bf16[144,128]{1,0:T(8,128)(2,1)S(1)} %get-tuple-element.73), channel_id=1, source_target_pairs={{0,8},{8,16},{16,24},{24,32},{32,40},{40,48},{48,56},{56,64},{64,7... | collective-permute-start | bytes 110600 | tf_op jit(solution)/shard_map/ppermute | solution.py:107
  1050.9 95.2 %collective-permute-start.68 = (bf16[144,128]{1,0:T(8,128)(2,1)S(1)}, bf16[144,128]{1,0:T(8,128)(2,1)S(1)}, u32[]{:S(2)}, u32[]{:S(2)}) collective-permute-start(bf16[144,128]{1,0:T(8,128)(2,1)S(1)} %get-tuple-element.68), channel_id=1, source_target_pairs={{0,48},{8,56},{16,64},{24,72},{32,80},{40,88},{48,96},{56,104},{64... | collective-permute-start | bytes 110600 | tf_op jit(solution)/shard_map/ppermute | solution.py:107
  1259.7 95.2 %collective-permute-start.79 = (bf16[144,128]{1,0:T(8,128)(2,1)S(1)}, bf16[144,128]{1,0:T(8,128)(2,1)S(1)}, u32[]{:S(2)}, u32[]{:S(2)}) collective-permute-start(bf16[144,128]{1,0:T(8,128)(2,1)S(1)} %get-tuple-element.57), channel_id=1, source_target_pairs={{0,136},{8,144},{16,152},{24,160},{32,168},{40,176},{48,184},{56,1... | collective-permute-start | bytes 110600 | tf_op jit(solution)/shard_map/ppermute | solution.py:107
  1278.7 95.2 %collective-permute-start.80 = (bf16[144,128]{1,0:T(8,128)(2,1)S(1)}, bf16[144,128]{1,0:T(8,128)(2,1)S(1)}, u32[]{:S(2)}, u32[]{:S(2)}) collective-permute-start(bf16[144,128]{1,0:T(8,128)(2,1)S(1)} %get-tuple-element.56), channel_id=1, source_target_pairs={{0,144},{8,152},{16,160},{24,168},{32,176},{40,184},{48,192},{56,2... | collective-permute-start | bytes 110600 | tf_op jit(solution)/shard_map/ppermute | solution.py:107
  1297.8 95.2 %collective-permute-start.81 = (bf16[144,128]{1,0:T(8,128)(2,1)S(1)}, bf16[144,128]{1,0:T(8,128)(2,1)S(1)}, u32[]{:S(2)}, u32[]{:S(2)}) collective-permute-start(bf16[144,128]{1,0:T(8,128)(2,1)S(1)} %get-tuple-element.55), channel_id=1, source_target_pairs={{0,152},{8,160},{16,168},{24,176},{32,184},{40,192},{48,200},{56,2... | collective-permute-start | bytes 110600 | tf_op jit(solution)/shard_map/ppermute | solution.py:107
  1316.8 95.2 %collective-permute-start.82 = (bf16[144,128]{1,0:T(8,128)(2,1)S(1)}, bf16[144,128]{1,0:T(8,128)(2,1)S(1)}, u32[]{:S(2)}, u32[]{:S(2)}) collective-permute-start(bf16[144,128]{1,0:T(8,128)(2,1)S(1)} %get-tuple-element.54), channel_id=1, source_target_pairs={{0,160},{8,168},{16,176},{24,184},{32,192},{40,200},{48,208},{56,2... | collective-permute-start | bytes 110600 | tf_op jit(solution)/shard_map/ppermute | solution.py:107
  1335.8 95.2 %collective-permute-start.83 = (bf16[144,128]{1,0:T(8,128)(2,1)S(1)}, bf16[144,128]{1,0:T(8,128)(2,1)S(1)}, u32[]{:S(2)}, u32[]{:S(2)}) collective-permute-start(bf16[144,128]{1,0:T(8,128)(2,1)S(1)} %get-tuple-element.53), channel_id=1, source_target_pairs={{0,168},{8,176},{16,184},{24,192},{32,200},{40,208},{48,216},{56,2... | collective-permute-start | bytes 110600 | tf_op jit(solution)/shard_map/ppermute | solution.py:107
  1354.9 95.2 %collective-permute-start.84 = (bf16[144,128]{1,0:T(8,128)(2,1)S(1)}, bf16[144,128]{1,0:T(8,128)(2,1)S(1)}, u32[]{:S(2)}, u32[]{:S(2)}) collective-permute-start(bf16[144,128]{1,0:T(8,128)(2,1)S(1)} %get-tuple-element.52), channel_id=1, source_target_pairs={{0,176},{8,184},{16,192},{24,200},{32,208},{40,216},{48,224},{56,2... | collective-permute-start | bytes 110600 | tf_op jit(solution)/shard_map/ppermute | solution.py:107
  1373.9 95.2 %collective-permute-start.85 = (bf16[144,128]{1,0:T(8,128)(2,1)S(1)}, bf16[144,128]{1,0:T(8,128)(2,1)S(1)}, u32[]{:S(2)}, u32[]{:S(2)}) collective-permute-start(bf16[144,128]{1,0:T(8,128)(2,1)S(1)} %get-tuple-element.51), channel_id=1, source_target_pairs={{0,184},{8,192},{16,200},{24,208},{32,216},{40,224},{48,232},{56,2... | collective-permute-start | bytes 110600 | tf_op jit(solution)/shard_map/ppermute | solution.py:107
  1393.0 95.2 %collective-permute-start.86 = (bf16[144,128]{1,0:T(8,128)(2,1)S(1)}, bf16[144,128]{1,0:T(8,128)(2,1)S(1)}, u32[]{:S(2)}, u32[]{:S(2)}) collective-permute-start(bf16[144,128]{1,0:T(8,128)(2,1)S(1)} %get-tuple-element.50), channel_id=1, source_target_pairs={{0,192},{8,200},{16,208},{24,216},{32,224},{40,232},{48,240},{56,2... | collective-permute-start | bytes 110600 | tf_op jit(solution)/shard_map/ppermute | solution.py:107
  1412.0 95.2 %collective-permute-start.87 = (bf16[144,128]{1,0:T(8,128)(2,1)S(1)}, bf16[144,128]{1,0:T(8,128)(2,1)S(1)}, u32[]{:S(2)}, u32[]{:S(2)}) collective-permute-start(bf16[144,128]{1,0:T(8,128)(2,1)S(1)} %get-tuple-element.49), channel_id=1, source_target_pairs={{0,200},{8,208},{16,216},{24,224},{32,232},{40,240},{48,248},{56,2... | collective-permute-start | bytes 110600 | tf_op jit(solution)/shard_map/ppermute | solution.py:107
  1431.0 95.2 %collective-permute-start.88 = (bf16[144,128]{1,0:T(8,128)(2,1)S(1)}, bf16[144,128]{1,0:T(8,128)(2,1)S(1)}, u32[]{:S(2)}, u32[]{:S(2)}) collective-permute-start(bf16[144,128]{1,0:T(8,128)(2,1)S(1)} %get-tuple-element.48), channel_id=1, source_target_pairs={{0,208},{8,216},{16,224},{24,232},{32,240},{40,248},{48,256},{56,2... | collective-permute-start | bytes 110600 | tf_op jit(solution)/shard_map/ppermute | solution.py:107
  1450.1 95.2 %collective-permute-start.89 = (bf16[144,128]{1,0:T(8,128)(2,1)S(1)}, bf16[144,128]{1,0:T(8,128)(2,1)S(1)}, u32[]{:S(2)}, u32[]{:S(2)}) collective-permute-start(bf16[144,128]{1,0:T(8,128)(2,1)S(1)} %get-tuple-element.47), channel_id=1, source_target_pairs={{0,216},{8,224},{16,232},{24,240},{32,248},{40,256},{48,264},{56,2... | collective-permute-start | bytes 110600 | tf_op jit(solution)/shard_map/ppermute | solution.py:107
  (131 other events, 24707.6 us)
Sparse Core Ops, SparseCore 0:
  1849.8 58.9 all-gather.1

commit v4 on v2

--- a/solution.py
+++ b/solution.py
@@ -115,8 +115,7 @@
         tokens_here, heads_loc * width
     )
     attention = attention.astype(jnp.bfloat16)
-    gathered = lax.all_gather(attention, "zh", axis=1, tiled=True)
-    gathered = lax.all_gather(gathered, "y", axis=1, tiled=True)
+    gathered = lax.all_gather(attention, ("y", "zh"), axis=1, tiled=True)
     projected = jnp.dot(
         gathered,
         out_weight,

time: 325 us -> 361 us (1.11)
  waiting for transfers between devices: 223 us -> 282 us
  blocking collectives: 23.7 us -> 0 us
    all_gather x1, waiting for transfers between devices: 28 us -> 86.8 us  [local(): gathered = lax.all_gather(attention, ('y', 'zh'), axis=1, tiled=True)]
    all_gather x1 -> x0, blocking collectives: 23.7 us -> none  [local(): gathered = lax.all_gather(attention, 'zh', axis=1, tiled=True)]
where the time goes in v4:
time: 361 us; the launch traced here: 360 us
  waiting for transfers between devices  282 us (78%)
  starting transfers between devices  26.2 us (7%)
  local copies, waits for them, and re-layouts  19.9 us (6%)
  between operations  13.7 us (4%)
  matrix products  11.8 us (3%)
  other arithmetic  6.85 us (2%)
    all_to_all x1, waiting for transfers between devices, local(): lax.all_to_all(back, 'ctx', split_axis=0, concat_axis=0, tiled=True)  100 us
    all_to_all x1, waiting for transfers between devices, local(): lax.all_to_all(send_q, 'ctx', split_axis=0, concat_axis=0, tiled=True)  94.5 us
    all_gather x1, waiting for transfers between devices, local(): gathered = lax.all_gather(attention, ('y', 'zh'), axis=1, tiled=True)  86.8 us
    all_to_all x1, starting transfers between devices, local(): lax.all_to_all(send_q, 'ctx', split_axis=0, concat_axis=0, tiled=True)  16.4 us
    all_to_all x1, starting transfers between devices, local(): lax.all_to_all(back, 'ctx', split_axis=0, concat_axis=0, tiled=True)  9.78 us
  transfers between devices with their start and end apart: 3, of which 3 were waited for; matrix products, arithmetic and copies ran while one was open for 1% of the time, Pallas kernels for 0%

profile of v4, /device:TPU:6, one launch (start us, length us, event | category | flops | bytes accessed | tf_op | source)
XLA Modules:
  0.0 360.1 jit_solution(8766354204228165098)
XLA Ops:
  6.5 1.3 fusion.32
  8.7 0.9 reshape_reshape.3
  9.7 1.9 broadcast_in_dim.55
  11.6 4.2 %scatter_fusion = bf16[64,2,2,32,128]{4,3,2,1,0:T(8,128)(2,1)} fusion(bf16[64,2,2,32,128]{4,3,2,1,0:T(8,128)(2,1)} %broadcast_in_dim.55, s32[32]{0:T(128)S(1)} %reshape.202, bf16[32,32,128]{2,1,0:T(8,128)(2,1)S(1)} %bitcast.87), kind=kCustom, calls=%fused_computation.2 | custom fusion | bytes 786816 | tf_op jit(solution)/shard_map/scatter | solution.py:69
  15.7 16.4 %all-to-all-start = ((bf16[64,2,2,32,128]{4,3,2,1,0:T(8,128)(2,1)}), bf16[64,2,2,32,128]{4,3,2,1,0:T(8,128)(2,1)S(1)}, u32[]{:S(2)}, u32[]{:S(2)}) async-start(bf16[64,2,2,32,128]{4,3,2,1,0:T(8,128)(2,1)} %scatter_fusion), calls=%async_computation | async-start | bytes 4194304 | tf_op jit(solution)/shard_map/all_to_all | solution.py:70
  32.2 94.5 %all-to-all-done = bf16[64,2,2,32,128]{4,3,2,1,0:T(8,128)(2,1)S(1)} async-done(((bf16[64,2,2,32,128]{4,3,2,1,0:T(8,128)(2,1)}), bf16[64,2,2,32,128]{4,3,2,1,0:T(8,128)(2,1)S(1)}, u32[]{:S(2)}, u32[]{:S(2)}) %all-to-all-start) | async-done | bytes 2097184 | tf_op jit(solution)/shard_map/all_to_all | solution.py:70
  127.4 1.3 multiply_reduce_fusion
  128.7 1.4 fusion
  130.1 1.8 copy-done.1
  132.4 5.0 %fusion.2 = bf16[2,4096,128]{2,1,0:T(8,128)(2,1)S(1)} fusion(f32[2,4096,256]{1,2,0:T(8,128)} %copy-done.1, f32[2,4096]{1,0:T(2,128)S(1)} %get-tuple-element.17, f32[2,4096]{1,0:T(2,128)S(1)} %fusion, bf16[256,256]{1,0:T(8,128)(2,1)S(1)} %copy-done.6), kind=kOutput, calls=%fused_computation.8 | convolution fusion | flops 545259520 | bytes 10682368 | tf_op jit(solution)/shard_map/hrk,khd->hrd/dot_general | solution.py:27
  138.0 1.9 maximum_maximum_fusion
  139.9 9.8 %all-to-all-start.1 = ((bf16[64,144,128]{2,1,0:T(8,128)(2,1)}), bf16[64,144,128]{2,1,0:T(8,128)(2,1)S(1)}, u32[]{:S(2)}, u32[]{:S(2)}) async-start(bf16[64,144,128]{2,1,0:T(8,128)(2,1)} %maximum_maximum_fusion), calls=%async_computation.1 | async-start | bytes 4718592 | tf_op jit(solution)/shard_map/all_to_all | solution.py:95
  150.0 1.1 fusion.36
  151.1 0.8 copy-done.2
  152.8 2.1 convolution_divide_fusion.1
  154.9 100.3 %all-to-all-done.1 = bf16[64,144,128]{2,1,0:T(8,128)(2,1)S(1)} async-done(((bf16[64,144,128]{2,1,0:T(8,128)(2,1)}), bf16[64,144,128]{2,1,0:T(8,128)(2,1)S(1)}, u32[]{:S(2)}, u32[]{:S(2)}) %all-to-all-start.1) | async-done | bytes 2359328 | tf_op jit(solution)/shard_map/all_to_all | solution.py:95
  255.3 0.7 copy.97
  256.1 1.0 copy.100
  257.0 1.6 slice.37
  258.7 2.3 gather_fusion.1
  261.0 0.7 gather_fusion
  262.1 1.2 fusion.19
  264.1 86.8 %all-gather.2.cloned.1.call-done = bf16[256,2048]{1,0:T(8,128)(2,1)} async-done(((bf16[256,256]{1,0:T(8,128)(2,1)}), bf16[256,2048]{1,0:T(8,128)(2,1)}) %all-gather.2.cloned.1.call-update) | async-done | bytes 1048592 | tf_op jit(solution)/shard_map/all_gather | solution.py:118
  350.9 2.3 convolution_convert_fusion
  (54 shorter events, 5.1 us)
Async XLA Ops:
  6.5 344.4 %copy-start = (bf16[2048,256]{1,0:T(8,128)(2,1)S(1)}, bf16[2048,256]{1,0:T(8,128)(2,1)}, u32[]{:S(2)}) copy-start(bf16[2048,256]{1,0:T(8,128)(2,1)} %param.9) | copy-start | bytes 3145732
  15.7 111.6 %copy-start.4 = (bf16[256,256]{1,0:T(8,128)(2,1)S(1)}, bf16[256,256]{1,0:T(8,128)(2,1)}, u32[]{:S(2)}) copy-start(bf16[256,256]{1,0:T(8,128)(2,1)} %param.6) | copy-start | bytes 393220
  15.7 110.9 %all-to-all-start = ((bf16[64,2,2,32,128]{4,3,2,1,0:T(8,128)(2,1)}), bf16[64,2,2,32,128]{4,3,2,1,0:T(8,128)(2,1)S(1)}, u32[]{:S(2)}, u32[]{:S(2)}) async-start(bf16[64,2,2,32,128]{4,3,2,1,0:T(8,128)(2,1)} %scatter_fusion), calls=%async_computation | async-start | bytes 4194304 | tf_op jit(solution)/shard_map/all_to_all | solution.py:70
  128.7 3.2 copy-start.1
  128.7 3.7 %copy-start.6 = (bf16[256,256]{1,0:T(8,128)(2,1)S(1)}, bf16[256,256]{1,0:T(8,128)(2,1)}, u32[]{:S(2)}) copy-start(bf16[256,256]{1,0:T(8,128)(2,1)} %param.7) | copy-start | bytes 393220
  138.0 12.0 %copy-start.3 = (bf16[256,256]{1,0:T(8,128)(2,1)S(1)}, bf16[256,256]{1,0:T(8,128)(2,1)}, u32[]{:S(2)}) copy-start(bf16[256,256]{1,0:T(8,128)(2,1)} %param.5) | copy-start | bytes 393220
  139.9 115.3 %all-to-all-start.1 = ((bf16[64,144,128]{2,1,0:T(8,128)(2,1)}), bf16[64,144,128]{2,1,0:T(8,128)(2,1)S(1)}, u32[]{:S(2)}, u32[]{:S(2)}) async-start(bf16[64,144,128]{2,1,0:T(8,128)(2,1)} %maximum_maximum_fusion), calls=%async_computation.1 | async-start | bytes 4718592 | tf_op jit(solution)/shard_map/all_to_all | solution.py:95
  149.7 201.2 %all-gather.2.cloned.1.call-start = ((), (), s32[]{:S(2)}) async-start(), calls=%async_computation.2 | async-start | bytes 1179648 | tf_op jit(solution)/shard_map/all_gather | solution.py:118
  151.1 0.8 copy-start.2
  151.1 0.9 copy-start.5
Sparse Core Ops, SparseCore 0:
  264.3 86.6 all-gather.1

commit v5 on v2

--- a/solution.py
+++ b/solution.py
@@ -4,7 +4,6 @@
 from jax.sharding import Mesh, PartitionSpec as P
 
 CAP = 2
-LSE_ROWS = 16
 
 
 def split_bf16(x):
@@ -60,13 +59,17 @@
     flat_hot = onehot.reshape(heads_loc, tiles * 2, sources)
     before = jnp.cumsum(flat_hot, axis=1) - flat_hot
     slot = jnp.sum(before * flat_hot, axis=-1).reshape(heads_loc, tiles, 2)
-    head_idx = jnp.broadcast_to(
-        jnp.arange(heads_loc, dtype=jnp.int32)[:, None, None], (heads_loc, tiles, 2)
-    )
-    query_src = jnp.transpose(quer_three.reshape(tiles, tile_rows, heads_loc, width), (2, 0, 1, 3))
-    query_pairs = jnp.broadcast_to(query_src[:, :, None], (heads_loc, tiles, 2, tile_rows, width))
-    send_q = jnp.zeros((sources, CAP, heads_loc, tile_rows, width), jnp.bfloat16)
-    send_q = send_q.at[target, slot, head_idx].set(query_pairs, mode="drop")
+    query_src = jnp.transpose(
+        quer_three.reshape(tiles, tile_rows, heads_loc, width), (2, 0, 1, 3)
+    ).reshape(heads_loc, tiles, tile_rows * width)
+    flat_slot = target * CAP + slot
+    route = (
+        flat_slot[..., None] == jnp.arange(sources * CAP, dtype=jnp.int32)
+    ).astype(jnp.bfloat16)
+    send_q = jnp.einsum(
+        "htep,htx->phx", route, query_src, preferred_element_type=jnp.float32
+    ).astype(jnp.bfloat16)
+    send_q = send_q.reshape(sources, CAP, heads_loc, tile_rows, width)
     got_rows = lax.all_to_all(send_q, "ctx", split_axis=0, concat_axis=0, tiled=True)
 
     got_q = jnp.transpose(got_rows, (2, 0, 1, 3, 4)).reshape(
@@ -82,29 +85,28 @@
     lse = jnp.transpose(lse.reshape(heads_loc, sources, CAP, tile_rows), (1, 2, 0, 3)).reshape(
         sources, CAP * heads_loc * tile_rows
     )
-    lse_parts = jnp.transpose(split_bf16(lse), (1, 0, 2)).reshape(sources, -1, width)
-    pad = -lse_parts.shape[1] % LSE_ROWS
+    lse_parts = jnp.transpose(split_bf16(lse), (1, 0, 2))
+    rows_part = CAP * heads_loc * tile_rows
     back = jnp.concatenate(
         [
-            part.astype(jnp.bfloat16),
-            lse_parts,
-            jnp.zeros((sources, pad, width), jnp.bfloat16),
+            part.astype(jnp.bfloat16).reshape(sources, rows_part * width),
+            lse_parts.reshape(sources, 3 * rows_part),
         ],
         axis=1,
     )
     got_back = lax.all_to_all(back, "ctx", split_axis=0, concat_axis=0, tiled=True)
-    rows_part = CAP * heads_loc * tile_rows
-    got_out = got_back[:, :rows_part].reshape(sources, CAP, heads_loc, tile_rows, width)
-    got_lse = join_bf16(
-        jnp.transpose(
-            got_back[:, rows_part : rows_part + lse_parts.shape[1]].reshape(sources, 3, rows_part),
-            (1, 0, 2),
-        )
-    ).reshape(sources, CAP, heads_loc, tile_rows)
-
-    clipped = jnp.clip(target, 0, sources - 1)
-    pick_out = got_out[clipped, slot, head_idx].astype(jnp.float32)
-    pick_lse = got_lse[clipped, slot, head_idx]
+    got_out = got_back[:, : rows_part * width].reshape(sources * CAP, heads_loc, tile_rows * width)
+    got_parts = jnp.transpose(
+        got_back[:, rows_part * width :].reshape(sources, 3, CAP, heads_loc, tile_rows),
+        (0, 2, 3, 1, 4),
+    ).reshape(sources * CAP, heads_loc, 3 * tile_rows)
+    pick_out = jnp.einsum(
+        "htep,phx->htex", route, got_out, preferred_element_type=jnp.float32
+    ).reshape(heads_loc, tiles, 2, tile_rows, width)
+    pick_parts = jnp.einsum(
+        "htep,phx->htex", route, got_parts, preferred_element_type=jnp.float32
+    ).reshape(heads_loc, tiles, 2, 3, tile_rows)
+    pick_lse = pick_parts[:, :, :, 0] + (pick_parts[:, :, :, 1] + pick_parts[:, :, :, 2])
     keep = valid[..., None]
     top = jnp.maximum(own_lse, jnp.max(jnp.where(keep, pick_lse, own_lse[:, :, None]), axis=2))
     own_w = jnp.exp(own_lse - top)

time: 325 us -> 346 us (1.065)
  blocking collectives: 23.7 us -> 135 us
  waiting for transfers between devices: 223 us -> 122 us
  local copies, waits for them, and re-layouts: 19.3 us -> 43.8 us
  starting transfers between devices: 26.2 us -> 9.83 us
    all_to_all x0 -> x1, blocking collectives: none -> 111 us  [local(): lax.all_to_all(send_q, 'ctx', split_axis=0, concat_axis=0, tiled=True)]
    all_to_all x1 -> x0, waiting for transfers between devices: 94.5 us -> none  [local(): lax.all_to_all(send_q, 'ctx', split_axis=0, concat_axis=0, tiled=True)]
    all_to_all x1 -> x0, starting transfers between devices: 16.3 us -> none  [local(): lax.all_to_all(send_q, 'ctx', split_axis=0, concat_axis=0, tiled=True)]
    unnamed x15 -> x18, local copies, waits for them, and re-layouts: 2.59 us -> 16.8 us
    all_to_all x0 -> x2, local copies, waits for them, and re-layouts: none -> 11.4 us  [local(): lax.all_to_all(back, 'ctx', split_axis=0, concat_axis=0, tiled=True)]
    slice x1 -> x4, local copies, waits for them, and re-layouts: 1.63 us -> 8.91 us  [the longest x2 7.24 us: local(): got_back[:, :rows_part * width]]
    all_to_all x1, waiting for transfers between devices: 100 us -> 94.5 us  [local(): lax.all_to_all(back, 'ctx', split_axis=0, concat_axis=0, tiled=True)]
    dot_general x0 -> x3, matrix products: none -> 4.89 us  [the longest x1 3.95 us: local(): jnp.einsum('htep,phx->htex', route, got_out, preferred_element_type=jnp.f...]
  transfers between devices with their start and end apart: 3 -> 2, of which waited for: 3 -> 2; matrix products, arithmetic and copies ran while one was open for 1% -> 1% of each run, Pallas kernels for 0% -> 0%
where the time goes in v5:
time: 346 us; the launch traced here: 345 us
  blocking collectives  135 us (39%)
  waiting for transfers between devices  122 us (35%)
  local copies, waits for them, and re-layouts  43.8 us (13%)
  matrix products  15.1 us (4%)
  between operations  13.7 us (4%)
  starting transfers between devices  9.83 us (3%)
  other arithmetic  5.53 us (2%)
    all_to_all x1, blocking collectives, local(): lax.all_to_all(send_q, 'ctx', split_axis=0, concat_axis=0, tiled=True)  111 us
    all_to_all x1, waiting for transfers between devices, local(): lax.all_to_all(back, 'ctx', split_axis=0, concat_axis=0, tiled=True)  94.5 us
    all_gather x1, waiting for transfers between devices, local(): gathered = lax.all_gather(gathered, 'y', axis=1, tiled=True)  27.7 us
    all_gather x1, blocking collectives, local(): gathered = lax.all_gather(attention, 'zh', axis=1, tiled=True)  23.9 us
    unnamed x18, local copies, waits for them, and re-layouts  16.8 us
    all_to_all x2, local copies, waits for them, and re-layouts, local(): lax.all_to_all(back, 'ctx', split_axis=0, concat_axis=0, tiled=True)  11.4 us
    all_to_all x1, starting transfers between devices, local(): lax.all_to_all(back, 'ctx', split_axis=0, concat_axis=0, tiled=True)  9.78 us
    slice x2, local copies, waits for them, and re-layouts, local(): got_back[:, :rows_part * width]  7.24 us
  transfers between devices with their start and end apart: 2, of which 2 were waited for; matrix products, arithmetic and copies ran while one was open for 1% of the time, Pallas kernels for 0%

profile of v5, /device:TPU:6, one launch (start us, length us, event | category | flops | bytes accessed | tf_op | source)
XLA Modules:
  0.0 344.8 jit_solution(17711686933998058365)
XLA Ops:
  6.5 0.8 slice.18
  8.0 1.0 reshape_reshape.3
  10.8 110.7 %all_to_all.17 = bf16[64,2,2,32,128]{4,3,1,2,0:T(8,128)(2,1)S(1)} all-to-all(bf16[64,2,2,32,128]{4,3,1,2,0:T(8,128)(2,1)S(1)} %copy.66), channel_id=1, replica_groups=mesh['ctx'=64,'y'=4,'zh'=2] {'ctx'}, dimensions={0} | all-to-all | bytes 4194304 | tf_op jit(solution)/shard_map/all_to_all | solution.py:73
  122.0 1.3 multiply_reduce_fusion
  123.4 1.4 fusion
  124.8 1.8 copy-done.1
  127.0 5.0 %fusion.2 = bf16[2,4096,128]{2,1,0:T(8,128)(2,1)S(1)} fusion(f32[2,4096,256]{1,2,0:T(8,128)} %copy-done.1, f32[2,4096]{1,0:T(2,128)S(1)} %get-tuple-element.12, f32[2,4096]{1,0:T(2,128)S(1)} %fusion, bf16[256,256]{1,0:T(8,128)(2,1)S(1)} %copy-done.5), kind=kOutput, calls=%fused_computation.6 | convolution fusion | flops 545259520 | bytes 10682368 | tf_op jit(solution)/shard_map/hrk,khd->hrd/dot_general | solution.py:26
  132.5 1.4 copy.140
  134.6 2.9 reduce.1
  137.5 4.8 %reshape.203 = bf16[64,2,8384]{2,1,0:T(2,128)(2,1)} reshape(bf16[64,16768]{1,0:T(8,128)(2,1)} %reduce.1) | data formatting | bytes 4292608
  142.3 9.8 %all-to-all-start.1 = ((bf16[64,2,8384]{2,1,0:T(2,128)(2,1)}), bf16[64,2,8384]{2,1,0:T(2,128)(2,1)S(1)}, u32[]{:S(2)}, u32[]{:S(2)}) async-start(bf16[64,2,8384]{2,1,0:T(2,128)(2,1)} %reshape.203), calls=%async_computation.1 | async-start | bytes 4325376 | tf_op jit(solution)/shard_map/all_to_all | solution.py:97
  152.5 0.8 copy-done.2
  153.5 1.4 convolution_divide_fusion.1
  154.9 94.5 %all-to-all-done.1 = bf16[64,2,8384]{2,1,0:T(2,128)(2,1)S(1)} async-done(((bf16[64,2,8384]{2,1,0:T(2,128)(2,1)}), bf16[64,2,8384]{2,1,0:T(2,128)(2,1)S(1)}, u32[]{:S(2)}, u32[]{:S(2)}) %all-to-all-start.1) | async-done | bytes 2146336 | tf_op jit(solution)/shard_map/all_to_all | solution.py:97
  249.4 7.5 %reshape.204 = bf16[64,1,16768]{2,1,0:T(2,128)(2,1)} reshape(bf16[64,2,8384]{2,1,0:T(2,128)(2,1)S(1)} %all-to-all-done.1) | data formatting | bytes 4292608
  256.9 10.9 %copy.75 = bf16[64,1,16768]{0,2,1:T(8,128)(2,1)} copy(bf16[64,1,16768]{2,1,0:T(2,128)(2,1)} %reshape.204) | data formatting | bytes 4292608 | tf_op jit(solution)/shard_map/all_to_all | solution.py:97
  267.8 3.7 %slice.28 = bf16[64,16384]{0,1:T(8,128)(2,1)} slice(bf16[64,16768]{0,1:T(8,128)(2,1)} %bitcast.106), slice={[0:64], [0:16384]} | slice | bytes 4194304 | tf_op jit(solution)/shard_map/slice | solution.py:98
  271.5 0.9 slice.24
  272.4 3.5 %copy.81 = bf16[64,16384]{1,0:T(8,128)(2,1)S(1)} copy(bf16[64,16384]{0,1:T(8,128)(2,1)} %slice.28) | data formatting | bytes 4194304 | tf_op jit(solution)/shard_map/slice | solution.py:98
  276.0 2.8 reshape.200
  279.7 4.0 %fusion.8 = f32[2,8,4096]{2,1,0:T(8,128)S(1)} fusion(bf16[128,2,4096,1]{2,1,0,3:T(2,128)(2,1)} %bitcast.114, f32[2,8,2,32]{1,3,2,0:T(8,128)S(1)} %copy.80, s32[2,8,2]{1,2,0:T(2,128)S(1)} %copy.64), kind=kOutput, calls=%fused_computation.15 | convolution fusion | flops 33755136 | bytes 2363520 | tf_op jit(solution)/shard_map/htep,phx->htex/dot_general | solution.py:103
  284.1 23.9 %all_gather.6 = bf16[256,512]{1,0:T(8,128)(2,1)} all-gather(bf16[256,256]{1,0:T(8,128)(2,1)S(1)} %bitcast.118), channel_id=1, replica_groups=mesh['ctx'=64,'y'=4,'zh'=2] {'zh'}, dimensions={1}, use_global_device_ids=true | all-gather | bytes 393216 | tf_op jit(solution)/shard_map/all_gather | solution.py:120
  308.0 27.7 %all-gather.2.cloned.1.call-done = bf16[256,2048]{1,0:T(8,128)(2,1)} async-done(((bf16[256,512]{1,0:T(8,128)(2,1)}), bf16[256,2048]{1,0:T(8,128)(2,1)}) %all-gather.2.cloned.1.call-update) | async-done | bytes 1048592 | tf_op jit(solution)/shard_map/all_gather | solution.py:121
  335.6 2.3 convolution_convert_fusion.1
  (55 shorter events, 6.5 us)
Async XLA Ops:
  6.5 329.1 %copy-start = (bf16[2048,256]{1,0:T(8,128)(2,1)S(1)}, bf16[2048,256]{1,0:T(8,128)(2,1)}, u32[]{:S(2)}) copy-start(bf16[2048,256]{1,0:T(8,128)(2,1)} %param.9) | copy-start | bytes 3145732
  10.8 111.2 %copy-start.4 = (bf16[256,256]{1,0:T(8,128)(2,1)S(1)}, bf16[256,256]{1,0:T(8,128)(2,1)}, u32[]{:S(2)}) copy-start(bf16[256,256]{1,0:T(8,128)(2,1)} %param.6) | copy-start | bytes 393220
  123.3 3.2 copy-start.1
  123.3 3.7 %copy-start.5 = (bf16[256,256]{1,0:T(8,128)(2,1)S(1)}, bf16[256,256]{1,0:T(8,128)(2,1)}, u32[]{:S(2)}) copy-start(bf16[256,256]{1,0:T(8,128)(2,1)} %param.7) | copy-start | bytes 393220
  137.5 14.7 %copy-start.3 = (bf16[256,256]{1,0:T(8,128)(2,1)S(1)}, bf16[256,256]{1,0:T(8,128)(2,1)}, u32[]{:S(2)}) copy-start(bf16[256,256]{1,0:T(8,128)(2,1)} %param.5) | copy-start | bytes 393220
  142.3 107.1 %all-to-all-start.1 = ((bf16[64,2,8384]{2,1,0:T(2,128)(2,1)}), bf16[64,2,8384]{2,1,0:T(2,128)(2,1)S(1)}, u32[]{:S(2)}, u32[]{:S(2)}) async-start(bf16[64,2,8384]{2,1,0:T(2,128)(2,1)} %reshape.203), calls=%async_computation.1 | async-start | bytes 4325376 | tf_op jit(solution)/shard_map/all_to_all | solution.py:97
  152.1 183.5 %all-gather.2.cloned.1.call-start = ((), (), s32[]{:S(2)}) async-start(), calls=%async_computation.2 | async-start | bytes 1310720 | tf_op jit(solution)/shard_map/all_gather | solution.py:121
  152.4 0.8 copy-start.2
Sparse Core Ops, SparseCore 0:
  308.1 27.5 all-gather.1

commit v6 on v5

--- a/solution.py
+++ b/solution.py
@@ -4,6 +4,7 @@
 from jax.sharding import Mesh, PartitionSpec as P
 
 CAP = 2
+LSE_ROWS = 16
 
 
 def split_bf16(x):
@@ -85,27 +86,31 @@
     lse = jnp.transpose(lse.reshape(heads_loc, sources, CAP, tile_rows), (1, 2, 0, 3)).reshape(
         sources, CAP * heads_loc * tile_rows
     )
-    lse_parts = jnp.transpose(split_bf16(lse), (1, 0, 2))
-    rows_part = CAP * heads_loc * tile_rows
+    lse_parts = jnp.transpose(split_bf16(lse), (1, 0, 2)).reshape(sources, -1, width)
+    pad = -lse_parts.shape[1] % LSE_ROWS
     back = jnp.concatenate(
         [
-            part.astype(jnp.bfloat16).reshape(sources, rows_part * width),
-            lse_parts.reshape(sources, 3 * rows_part),
+            part.astype(jnp.bfloat16),
+            lse_parts,
+            jnp.zeros((sources, pad, width), jnp.bfloat16),
         ],
         axis=1,
     )
     got_back = lax.all_to_all(back, "ctx", split_axis=0, concat_axis=0, tiled=True)
-    got_out = got_back[:, : rows_part * width].reshape(sources * CAP, heads_loc, tile_rows * width)
+    rows_part = CAP * heads_loc * tile_rows
+    got_out = got_back[:, :rows_part].reshape(sources * CAP, heads_loc, tile_rows, width)
     got_parts = jnp.transpose(
-        got_back[:, rows_part * width :].reshape(sources, 3, CAP, heads_loc, tile_rows),
+        got_back[:, rows_part : rows_part + lse_parts.shape[1]].reshape(
+            sources, 3, CAP, heads_loc, tile_rows
+        ),
         (0, 2, 3, 1, 4),
-    ).reshape(sources * CAP, heads_loc, 3 * tile_rows)
+    ).reshape(sources * CAP, heads_loc, 3, tile_rows)
     pick_out = jnp.einsum(
-        "htep,phx->htex", route, got_out, preferred_element_type=jnp.float32
-    ).reshape(heads_loc, tiles, 2, tile_rows, width)
+        "htep,phrd->hterd", route, got_out, preferred_element_type=jnp.float32
+    )
     pick_parts = jnp.einsum(
-        "htep,phx->htex", route, got_parts, preferred_element_type=jnp.float32
-    ).reshape(heads_loc, tiles, 2, 3, tile_rows)
+        "htep,phkr->htekr", route, got_parts, preferred_element_type=jnp.float32
+    )
     pick_lse = pick_parts[:, :, :, 0] + (pick_parts[:, :, :, 1] + pick_parts[:, :, :, 2])
     keep = valid[..., None]
     top = jnp.maximum(own_lse, jnp.max(jnp.where(keep, pick_lse, own_lse[:, :, None]), axis=2))

time: 346 us -> 320 us (0.925)
  blocking collectives: 135 us -> 23.7 us
  waiting for transfers between devices: 122 us -> 223 us
  local copies, waits for them, and re-layouts: 43.8 us -> 12.7 us
  starting transfers between devices: 9.83 us -> 26.4 us
    all_to_all x1 -> x0, blocking collectives: 111 us -> none  [local(): lax.all_to_all(send_q, 'ctx', split_axis=0, concat_axis=0, tiled=True)]
    all_to_all x0 -> x1, waiting for transfers between devices: none -> 94.5 us  [local(): lax.all_to_all(send_q, 'ctx', split_axis=0, concat_axis=0, tiled=True)]
    all_to_all x0 -> x1, starting transfers between devices: none -> 16.4 us  [local(): lax.all_to_all(send_q, 'ctx', split_axis=0, concat_axis=0, tiled=True)]
    unnamed x18 -> x19, local copies, waits for them, and re-layouts: 16.8 us -> 3.57 us
    all_to_all x2 -> x0, local copies, waits for them, and re-layouts: 11.4 us -> none  [local(): lax.all_to_all(back, 'ctx', split_axis=0, concat_axis=0, tiled=True)]
    all_to_all x1, waiting for transfers between devices: 94.5 us -> 101 us  [local(): lax.all_to_all(back, 'ctx', split_axis=0, concat_axis=0, tiled=True)]
    slice x3, local copies, waits for them, and re-layouts: 8.14 us -> 1.88 us  [the longest x2 1.61 us: local(): got_back[:, rows_part:rows_part + lse_parts.shape[1]]]
  transfers between devices with their start and end apart: 2 -> 3, of which waited for: 2 -> 3; matrix products, arithmetic and copies ran while one was open for 1% -> 1% of each run, Pallas kernels for 0% -> 0%
where the time goes in v6:
time: 320 us; the launch traced here: 319 us
  waiting for transfers between devices  223 us (70%)
  starting transfers between devices  26.4 us (8%)
  blocking collectives  23.7 us (7%)
  matrix products  15 us (5%)
  between operations  13.7 us (4%)
  local copies, waits for them, and re-layouts  12.7 us (4%)
  other arithmetic  4.4 us (1%)
    all_to_all x1, waiting for transfers between devices, local(): lax.all_to_all(back, 'ctx', split_axis=0, concat_axis=0, tiled=True)  101 us
    all_to_all x1, waiting for transfers between devices, local(): lax.all_to_all(send_q, 'ctx', split_axis=0, concat_axis=0, tiled=True)  94.5 us
    all_gather x1, waiting for transfers between devices, local(): gathered = lax.all_gather(gathered, 'y', axis=1, tiled=True)  28 us
    all_gather x1, blocking collectives, local(): gathered = lax.all_gather(attention, 'zh', axis=1, tiled=True)  23.7 us
    all_to_all x1, starting transfers between devices, local(): lax.all_to_all(send_q, 'ctx', split_axis=0, concat_axis=0, tiled=True)  16.4 us
    all_to_all x1, starting transfers between devices, local(): lax.all_to_all(back, 'ctx', split_axis=0, concat_axis=0, tiled=True)  9.78 us
    dot_general x2, matrix products, softmax_pv(): jnp.einsum('hrk,khd->hrd', prob.astype(jnp.bfloat16), vals, preferred_ele...  7.09 us
  transfers between devices with their start and end apart: 3, of which 3 were waited for; matrix products, arithmetic and copies ran while one was open for 1% of the time, Pallas kernels for 0%

profile of v6, /device:TPU:6, one launch (start us, length us, event | category | flops | bytes accessed | tf_op | source)
XLA Modules:
  0.0 319.2 jit_solution(9597144498097137240)
XLA Ops:
  6.5 0.8 slice.18
  8.0 1.0 reshape_reshape.3
  9.0 0.7 convolution_convert_fusion
  10.2 1.8 copy.73
  12.0 16.4 %all-to-all-start = ((bf16[64,2,2,32,128]{4,3,1,2,0:T(8,128)(2,1)}), bf16[64,2,2,32,128]{4,3,1,2,0:T(8,128)(2,1)S(1)}, u32[]{:S(2)}, u32[]{:S(2)}) async-start(bf16[64,2,2,32,128]{4,3,1,2,0:T(8,128)(2,1)} %copy.73), calls=%async_computation | async-start | bytes 4194304 | tf_op jit(solution)/shard_map/all_to_all | solution.py:74
  28.5 94.5 %all-to-all-done = bf16[64,2,2,32,128]{4,3,1,2,0:T(8,128)(2,1)S(1)} async-done(((bf16[64,2,2,32,128]{4,3,1,2,0:T(8,128)(2,1)}), bf16[64,2,2,32,128]{4,3,1,2,0:T(8,128)(2,1)S(1)}, u32[]{:S(2)}, u32[]{:S(2)}) %all-to-all-start) | async-done | bytes 2097184 | tf_op jit(solution)/shard_map/all_to_all | solution.py:74
  123.5 1.3 multiply_reduce_fusion
  124.8 1.4 fusion
  126.3 1.8 copy-done.1
  128.5 5.0 %fusion.2 = bf16[2,4096,128]{2,1,0:T(8,128)(2,1)S(1)} fusion(f32[2,4096,256]{1,2,0:T(8,128)} %copy-done.1, f32[2,4096]{1,0:T(2,128)S(1)} %get-tuple-element.14, f32[2,4096]{1,0:T(2,128)S(1)} %fusion, bf16[256,256]{1,0:T(8,128)(2,1)S(1)} %copy-done.7), kind=kOutput, calls=%fused_computation.6 | convolution fusion | flops 545259520 | bytes 10682368 | tf_op jit(solution)/shard_map/hrk,khd->hrd/dot_general | solution.py:27
  134.1 1.9 maximum_maximum_fusion
  136.0 9.8 %all-to-all-start.1 = ((bf16[64,144,128]{2,1,0:T(8,128)(2,1)}), bf16[64,144,128]{2,1,0:T(8,128)(2,1)S(1)}, u32[]{:S(2)}, u32[]{:S(2)}) async-start(bf16[64,144,128]{2,1,0:T(8,128)(2,1)} %maximum_maximum_fusion), calls=%async_computation.1 | async-start | bytes 4718592 | tf_op jit(solution)/shard_map/all_to_all | solution.py:99
  146.1 1.2 fusion.50
  147.3 0.8 copy-done.2
  148.4 2.1 convolution_divide_fusion.1
  150.4 100.9 %all-to-all-done.1 = bf16[64,144,128]{2,1,0:T(8,128)(2,1)S(1)} async-done(((bf16[64,144,128]{2,1,0:T(8,128)(2,1)}), bf16[64,144,128]{2,1,0:T(8,128)(2,1)S(1)}, u32[]{:S(2)}, u32[]{:S(2)}) %all-to-all-start.1) | async-done | bytes 2359328 | tf_op jit(solution)/shard_map/all_to_all | solution.py:99
  252.0 1.0 copy.83
  253.0 0.8 copy.84
  253.8 1.1 fusion.42
  255.1 0.7 copy.90
  256.7 1.2 fusion.12
  258.4 23.7 %all_gather.6 = bf16[256,512]{1,0:T(8,128)(2,1)} all-gather(bf16[256,256]{1,0:T(8,128)(2,1)S(1)} %bitcast.104), channel_id=1, replica_groups=mesh['ctx'=64,'y'=4,'zh'=2] {'zh'}, dimensions={1}, use_global_device_ids=true | all-gather | bytes 393216 | tf_op jit(solution)/shard_map/all_gather | solution.py:125
  282.1 28.0 %all-gather.2.cloned.1.call-done = bf16[256,2048]{1,0:T(8,128)(2,1)} async-done(((bf16[256,512]{1,0:T(8,128)(2,1)}), bf16[256,2048]{1,0:T(8,128)(2,1)}) %all-gather.2.cloned.1.call-update) | async-done | bytes 1048592 | tf_op jit(solution)/shard_map/all_gather | solution.py:126
  310.1 2.3 convolution_convert_fusion.1
  (55 shorter events, 5.4 us)
Async XLA Ops:
  6.5 303.5 %copy-start = (bf16[2048,256]{1,0:T(8,128)(2,1)S(1)}, bf16[2048,256]{1,0:T(8,128)(2,1)}, u32[]{:S(2)}) copy-start(bf16[2048,256]{1,0:T(8,128)(2,1)} %param.9) | copy-start | bytes 3145732
  12.0 111.5 %copy-start.5 = (bf16[256,256]{1,0:T(8,128)(2,1)S(1)}, bf16[256,256]{1,0:T(8,128)(2,1)}, u32[]{:S(2)}) copy-start(bf16[256,256]{1,0:T(8,128)(2,1)} %param.6) | copy-start | bytes 393220
  12.0 110.9 %all-to-all-start = ((bf16[64,2,2,32,128]{4,3,1,2,0:T(8,128)(2,1)}), bf16[64,2,2,32,128]{4,3,1,2,0:T(8,128)(2,1)S(1)}, u32[]{:S(2)}, u32[]{:S(2)}) async-start(bf16[64,2,2,32,128]{4,3,1,2,0:T(8,128)(2,1)} %copy.73), calls=%async_computation | async-start | bytes 4194304 | tf_op jit(solution)/shard_map/all_to_all | solution.py:74
  124.8 3.2 %copy-start.1 = (f32[2,4096,256]{1,2,0:T(8,128)}, f32[2,4096,256]{1,2,0:T(8,128)S(1)}, u32[]{:S(2)}) copy-start(f32[2,4096,256]{1,2,0:T(8,128)S(1)} %get-tuple-element.15) | copy-start | bytes 25165828
  124.8 3.7 %copy-start.7 = (bf16[256,256]{1,0:T(8,128)(2,1)S(1)}, bf16[256,256]{1,0:T(8,128)(2,1)}, u32[]{:S(2)}) copy-start(bf16[256,256]{1,0:T(8,128)(2,1)} %param.7) | copy-start | bytes 393220
  134.1 12.0 %copy-start.4 = (bf16[256,256]{1,0:T(8,128)(2,1)S(1)}, bf16[256,256]{1,0:T(8,128)(2,1)}, u32[]{:S(2)}) copy-start(bf16[256,256]{1,0:T(8,128)(2,1)} %param.5) | copy-start | bytes 393220
  136.0 115.3 %all-to-all-start.1 = ((bf16[64,144,128]{2,1,0:T(8,128)(2,1)}), bf16[64,144,128]{2,1,0:T(8,128)(2,1)S(1)}, u32[]{:S(2)}, u32[]{:S(2)}) async-start(bf16[64,144,128]{2,1,0:T(8,128)(2,1)} %maximum_maximum_fusion), calls=%async_computation.1 | async-start | bytes 4718592 | tf_op jit(solution)/shard_map/all_to_all | solution.py:99
  145.8 164.2 %all-gather.2.cloned.1.call-start = ((), (), s32[]{:S(2)}) async-start(), calls=%async_computation.2 | async-start | bytes 1310720 | tf_op jit(solution)/shard_map/all_gather | solution.py:126
  147.3 0.8 copy-start.2
  255.8 0.8 copy-start.6
  256.0 1.9 copy-start.3
Sparse Core Ops, SparseCore 0:
  282.2 27.8 all-gather.1

commit v7 on v6

--- a/solution.py
+++ b/solution.py
@@ -122,12 +122,18 @@
         tokens_here, heads_loc * width
     )
     attention = attention.astype(jnp.bfloat16)
-    gathered = lax.all_gather(attention, "zh", axis=1, tiled=True)
-    gathered = lax.all_gather(gathered, "y", axis=1, tiled=True)
+    pair = lax.axis_size("zh")
+    mine_zh = lax.axis_index("zh")
+    own_rows = lax.all_gather(attention, "y", axis=1, tiled=True)
+    partner = lax.ppermute(attention, "zh", [(0, 1), (1, 0)])
+    partner_rows = lax.all_gather(partner, "y", axis=1, tiled=True)
+    groups = out_weight.reshape(-1, pair, heads_loc * width, out_weight.shape[1])
+    own_w = lax.dynamic_index_in_dim(groups, mine_zh, axis=1, keepdims=False)
+    partner_w = lax.dynamic_index_in_dim(groups, 1 - mine_zh, axis=1, keepdims=False)
     projected = jnp.dot(
-        gathered,
-        out_weight,
-        preferred_element_type=jnp.float32,
+        own_rows, own_w.reshape(-1, out_weight.shape[1]), preferred_element_type=jnp.float32
+    ) + jnp.dot(
+        partner_rows, partner_w.reshape(-1, out_weight.shape[1]), preferred_element_type=jnp.float32
     )
     return projected.astype(jnp.bfloat16)
 

time: 320 us -> 312 us (0.975)
  waiting for transfers between devices: 223 us -> 209 us
  between operations: 13.7 us -> 0.3 us
  starting transfers between devices: 26.4 us -> 34.2 us
  local copies, waits for them, and re-layouts: 12.7 us -> 19.9 us
    all_gather x1 -> x0, waiting for transfers between devices: 28 us -> none  [local(): gathered = lax.all_gather(gathered, 'y', axis=1, tiled=True)]
    ppermute x0 -> x1, waiting for transfers between devices: none -> 14 us  [local(): partner = lax.ppermute(attention, 'zh', [(0, 1), (1, 0)])]
    ppermute x0 -> x1, starting transfers between devices: none -> 8.21 us  [local(): partner = lax.ppermute(attention, 'zh', [(0, 1), (1, 0)])]
    all_gather x1 -> x2, blocking collectives: 23.7 us -> 26.8 us  [the longest x1 14 us: local(): own_rows = lax.all_gather(attention, 'y', axis=1, tiled=True)]
where the time goes in v7:
time: 312 us; the launch traced here: 311 us
  waiting for transfers between devices  209 us (67%)
  starting transfers between devices  34.2 us (11%)
  blocking collectives  26.8 us (9%)
  local copies, waits for them, and re-layouts  19.9 us (6%)
  matrix products  13 us (4%)
  other arithmetic  7.54 us (2%)
    all_to_all x1, waiting for transfers between devices, local(): lax.all_to_all(back, 'ctx', split_axis=0, concat_axis=0, tiled=True)  100 us
    all_to_all x1, waiting for transfers between devices, local(): lax.all_to_all(send_q, 'ctx', split_axis=0, concat_axis=0, tiled=True)  94.5 us
    all_to_all x1, starting transfers between devices, local(): lax.all_to_all(send_q, 'ctx', split_axis=0, concat_axis=0, tiled=True)  16.2 us
    ppermute x1, waiting for transfers between devices, local(): partner = lax.ppermute(attention, 'zh', [(0, 1), (1, 0)])  14 us
    all_gather x1, blocking collectives, local(): own_rows = lax.all_gather(attention, 'y', axis=1, tiled=True)  14 us
    all_gather x1, blocking collectives, local(): partner_rows = lax.all_gather(partner, 'y', axis=1, tiled=True)  12.8 us
    all_to_all x1, starting transfers between devices, local(): lax.all_to_all(back, 'ctx', split_axis=0, concat_axis=0, tiled=True)  9.8 us
    ppermute x1, starting transfers between devices, local(): partner = lax.ppermute(attention, 'zh', [(0, 1), (1, 0)])  8.21 us
  transfers between devices with their start and end apart: 3, of which 3 were waited for; matrix products, arithmetic and copies ran while one was open for 1% of the time, Pallas kernels for 0%

profile of v7, /device:TPU:6, one launch (start us, length us, event | category | flops | bytes accessed | tf_op | source)
XLA Modules:
  0.0 310.6 jit_solution(13533782068518504216)
XLA Ops:
  4.2 1.8 copy.73
  6.0 16.2 %all-to-all-start = ((bf16[64,2,2,32,128]{4,3,1,2,0:T(8,128)(2,1)}), bf16[64,2,2,32,128]{4,3,1,2,0:T(8,128)(2,1)S(1)}, u32[]{:S(2)}, u32[]{:S(2)}) async-start(bf16[64,2,2,32,128]{4,3,1,2,0:T(8,128)(2,1)} %copy.73), calls=%async_computation | async-start | bytes 4194304 | tf_op jit(solution)/shard_map/all_to_all | solution.py:74
  22.3 94.5 %all-to-all-done = bf16[64,2,2,32,128]{4,3,1,2,0:T(8,128)(2,1)S(1)} async-done(((bf16[64,2,2,32,128]{4,3,1,2,0:T(8,128)(2,1)}), bf16[64,2,2,32,128]{4,3,1,2,0:T(8,128)(2,1)S(1)}, u32[]{:S(2)}, u32[]{:S(2)}) %all-to-all-start) | async-done | bytes 2097184 | tf_op jit(solution)/shard_map/all_to_all | solution.py:74
  117.4 1.3 multiply_reduce_fusion
  118.7 1.4 fusion
  120.1 1.8 copy-done.1
  122.3 5.0 %fusion.2 = bf16[2,4096,128]{2,1,0:T(8,128)(2,1)S(1)} fusion(f32[2,4096,256]{1,2,0:T(8,128)} %copy-done.1, f32[2,4096]{1,0:T(2,128)S(1)} %get-tuple-element.16, f32[2,4096]{1,0:T(2,128)S(1)} %fusion, bf16[256,256]{1,0:T(8,128)(2,1)S(1)} %copy-done.12), kind=kOutput, calls=%fused_computation.6 | convolution fusion | flops 545259520 | bytes 10682368 | tf_op jit(solution)/shard_map/hrk,khd->hrd/dot_general | solution.py:27
  127.9 1.9 maximum_maximum_fusion
  129.9 9.8 %all-to-all-start.1 = ((bf16[64,144,128]{2,1,0:T(8,128)(2,1)}), bf16[64,144,128]{2,1,0:T(8,128)(2,1)S(1)}, u32[]{:S(2)}, u32[]{:S(2)}) async-start(bf16[64,144,128]{2,1,0:T(8,128)(2,1)} %maximum_maximum_fusion), calls=%async_computation.1 | async-start | bytes 4718592 | tf_op jit(solution)/shard_map/all_to_all | solution.py:99
  141.5 1.3 constant_dynamic-slice_fusion.1
  142.7 2.1 convolution_divide_fusion.1
  144.9 100.4 %all-to-all-done.1 = bf16[64,144,128]{2,1,0:T(8,128)(2,1)S(1)} async-done(((bf16[64,144,128]{2,1,0:T(8,128)(2,1)}), bf16[64,144,128]{2,1,0:T(8,128)(2,1)S(1)}, u32[]{:S(2)}, u32[]{:S(2)}) %all-to-all-start.1) | async-done | bytes 2359328 | tf_op jit(solution)/shard_map/all_to_all | solution.py:99
  245.9 1.6 copy.83
  247.5 1.7 copy.84
  250.4 1.9 fusion.50
  252.3 1.4 copy.90
  253.7 1.3 fusion.49
  255.1 1.4 copy.86
  256.4 1.4 copy.92
  258.7 1.2 fusion.12
  260.3 14.0 %all_gather.6 = bf16[256,1024]{1,0:T(8,128)(2,1)S(1)} all-gather(bf16[256,256]{1,0:T(8,128)(2,1)S(1)} %bitcast.110), channel_id=1, replica_groups=mesh['ctx'=64,'y'=4,'zh'=2] {'y'}, dimensions={1}, use_global_device_ids=true | all-gather | bytes 655360 | tf_op jit(solution)/shard_map/all_gather | solution.py:127
  274.3 8.2 %collective-permute-start = (bf16[256,256]{1,0:T(8,128)(2,1)S(1)}, bf16[256,256]{1,0:T(8,128)(2,1)S(1)}, u32[]{:S(2)}, u32[]{:S(2)}) collective-permute-start(bf16[256,256]{1,0:T(8,128)(2,1)S(1)} %bitcast.111), channel_id=1, source_target_pairs={{0,1},{1,0},{2,3},{3,2},{4,5},{5,4},{6,7},{7,6},{8,9},{9,8},{10,11... | collective-permute-start | bytes 393224 | tf_op jit(solution)/shard_map/ppermute | solution.py:128
  282.9 14.0 %collective-permute-done = bf16[256,256]{1,0:T(8,128)(2,1)S(1)} collective-permute-done((bf16[256,256]{1,0:T(8,128)(2,1)S(1)}, bf16[256,256]{1,0:T(8,128)(2,1)S(1)}, u32[]{:S(2)}, u32[]{:S(2)}) %collective-permute-start) | collective-permute-done | bytes 131104 | tf_op jit(solution)/shard_map/ppermute | solution.py:128
  296.9 12.8 %all_gather.7 = bf16[256,1024]{1,0:T(8,128)(2,1)S(1)} all-gather(bf16[256,256]{1,0:T(8,128)(2,1)S(1)} %collective-permute-done), channel_id=1, replica_groups=mesh['ctx'=64,'y'=4,'zh'=2] {'y'}, dimensions={1}, use_global_device_ids=true | all-gather | bytes 655360 | tf_op jit(solution)/shard_map/all_gather | solution.py:129
  (67 shorter events, 11.8 us)
Async XLA Ops:
  0.0 117.4 %copy-start = (bf16[256,256]{1,0:T(8,128)(2,1)S(1)}, bf16[256,256]{1,0:T(8,128)(2,1)}, u32[]{:S(2)}) copy-start(bf16[256,256]{1,0:T(8,128)(2,1)} %param.6) | copy-start | bytes 393220
  1.4 0.6 copy-start.10
  6.0 110.8 %all-to-all-start = ((bf16[64,2,2,32,128]{4,3,1,2,0:T(8,128)(2,1)}), bf16[64,2,2,32,128]{4,3,1,2,0:T(8,128)(2,1)S(1)}, u32[]{:S(2)}, u32[]{:S(2)}) async-start(bf16[64,2,2,32,128]{4,3,1,2,0:T(8,128)(2,1)} %copy.73), calls=%async_computation | async-start | bytes 4194304 | tf_op jit(solution)/shard_map/all_to_all | solution.py:74
  118.6 3.2 %copy-start.1 = (f32[2,4096,256]{1,2,0:T(8,128)}, f32[2,4096,256]{1,2,0:T(8,128)S(1)}, u32[]{:S(2)}) copy-start(f32[2,4096,256]{1,2,0:T(8,128)S(1)} %get-tuple-element.17) | copy-start | bytes 25165828
  118.6 3.7 %copy-start.12 = (bf16[256,256]{1,0:T(8,128)(2,1)S(1)}, bf16[256,256]{1,0:T(8,128)(2,1)}, u32[]{:S(2)}) copy-start(bf16[256,256]{1,0:T(8,128)(2,1)} %param.7) | copy-start | bytes 393220
  127.9 11.8 %copy-start.6 = (bf16[256,256]{1,0:T(8,128)(2,1)S(1)}, bf16[256,256]{1,0:T(8,128)(2,1)}, u32[]{:S(2)}) copy-start(bf16[256,256]{1,0:T(8,128)(2,1)} %param.5) | copy-start | bytes 393220
  129.9 115.3 %all-to-all-start.1 = ((bf16[64,144,128]{2,1,0:T(8,128)(2,1)}), bf16[64,144,128]{2,1,0:T(8,128)(2,1)S(1)}, u32[]{:S(2)}, u32[]{:S(2)}) async-start(bf16[64,144,128]{2,1,0:T(8,128)(2,1)} %maximum_maximum_fusion), calls=%async_computation.1 | async-start | bytes 4718592 | tf_op jit(solution)/shard_map/all_to_all | solution.py:99
  140.0 0.8 copy-start.2
  140.9 0.6 copy-start.9
  141.1 109.2 %copy-start.8 = (pred[2,8,2]{1,2,0:T(4,128)(4,1)}, pred[2,8,2]{1,2,0:T(4,128)(4,1)S(1)}, u32[]{:S(2)}) copy-start(pred[2,8,2]{1,2,0:T(4,128)(4,1)S(1)} %copy.70) | copy-start | bytes 100
  255.1 3.1 copy-start.11
  257.8 0.8 copy-start.7
  257.8 2.1 copy-start.3
  257.8 2.1 copy-start.4
  257.8 2.1 copy-start.5
  274.3 22.6 %collective-permute-start = (bf16[256,256]{1,0:T(8,128)(2,1)S(1)}, bf16[256,256]{1,0:T(8,128)(2,1)S(1)}, u32[]{:S(2)}, u32[]{:S(2)}) collective-permute-start(bf16[256,256]{1,0:T(8,128)(2,1)S(1)} %bitcast.111), channel_id=1, source_target_pairs={{0,1},{1,0},{2,3},{3,2},{4,5},{5,4},{6,7},{7,6},{8,9},{9,8},{10,11... | collective-permute-start | bytes 393224 | tf_op jit(solution)/shard_map/ppermute | solution.py:128

commit v8 on v7

--- a/solution.py
+++ b/solution.py
@@ -4,6 +4,7 @@
 from jax.sharding import Mesh, PartitionSpec as P
 
 CAP = 2
+LANE_ROWS = 4
 LSE_ROWS = 16
 
 
@@ -83,34 +84,34 @@
     part = jnp.transpose(
         part.reshape(heads_loc, sources, CAP, tile_rows, width), (1, 2, 0, 3, 4)
     ).reshape(sources, CAP * heads_loc * tile_rows, width)
-    lse = jnp.transpose(lse.reshape(heads_loc, sources, CAP, tile_rows), (1, 2, 0, 3)).reshape(
-        sources, CAP * heads_loc * tile_rows
+    pieces = split_bf16(lse.reshape(heads_loc, sources, CAP, tile_rows))
+    pieces = jnp.concatenate(
+        [pieces, jnp.zeros((LANE_ROWS - 3,) + pieces.shape[1:], pieces.dtype)], axis=0
     )
-    lse_parts = jnp.transpose(split_bf16(lse), (1, 0, 2)).reshape(sources, -1, width)
-    pad = -lse_parts.shape[1] % LSE_ROWS
+    lse_rows = jnp.transpose(pieces, (2, 3, 1, 0, 4)).reshape(
+        sources, CAP * heads_loc, LANE_ROWS * tile_rows
+    )
+    rows_part = CAP * heads_loc * tile_rows
+    pad = -(rows_part + CAP * heads_loc) % 16
     back = jnp.concatenate(
         [
             part.astype(jnp.bfloat16),
-            lse_parts,
+            lse_rows,
             jnp.zeros((sources, pad, width), jnp.bfloat16),
         ],
         axis=1,
     )
     got_back = lax.all_to_all(back, "ctx", split_axis=0, concat_axis=0, tiled=True)
-    rows_part = CAP * heads_loc * tile_rows
     got_out = got_back[:, :rows_part].reshape(sources * CAP, heads_loc, tile_rows, width)
-    got_parts = jnp.transpose(
-        got_back[:, rows_part : rows_part + lse_parts.shape[1]].reshape(
-            sources, 3, CAP, heads_loc, tile_rows
-        ),
-        (0, 2, 3, 1, 4),
-    ).reshape(sources * CAP, heads_loc, 3, tile_rows)
+    got_lse = got_back[:, rows_part : rows_part + CAP * heads_loc].reshape(
+        sources * CAP, heads_loc, width
+    )
     pick_out = jnp.einsum(
         "htep,phrd->hterd", route, got_out, preferred_element_type=jnp.float32
     )
     pick_parts = jnp.einsum(
-        "htep,phkr->htekr", route, got_parts, preferred_element_type=jnp.float32
-    )
+        "htep,phx->htex", route, got_lse, preferred_element_type=jnp.float32
+    ).reshape(heads_loc, tiles, 2, LANE_ROWS, tile_rows)
     pick_lse = pick_parts[:, :, :, 0] + (pick_parts[:, :, :, 1] + pick_parts[:, :, :, 2])
     keep = valid[..., None]
     top = jnp.maximum(own_lse, jnp.max(jnp.where(keep, pick_lse, own_lse[:, :, None]), axis=2))

time: 312 us -> 311 us (level)
  no operation moved by 1% of the time
where the time goes in v8:
time: 311 us; the launch traced here: 310 us
  waiting for transfers between devices  209 us (67%)
  starting transfers between devices  34.2 us (11%)
  blocking collectives  26.8 us (9%)
  local copies, waits for them, and re-layouts  18.4 us (6%)
  matrix products  13.4 us (4%)
  other arithmetic  7.55 us (2%)
    all_to_all x1, waiting for transfers between devices, local(): lax.all_to_all(back, 'ctx', split_axis=0, concat_axis=0, tiled=True)  100 us
    all_to_all x1, waiting for transfers between devices, local(): lax.all_to_all(send_q, 'ctx', split_axis=0, concat_axis=0, tiled=True)  94.5 us
    all_to_all x1, starting transfers between devices, local(): lax.all_to_all(send_q, 'ctx', split_axis=0, concat_axis=0, tiled=True)  16.2 us
    ppermute x1, waiting for transfers between devices, local(): partner = lax.ppermute(attention, 'zh', [(0, 1), (1, 0)])  14 us
    all_gather x1, blocking collectives, local(): own_rows = lax.all_gather(attention, 'y', axis=1, tiled=True)  14 us
    all_gather x1, blocking collectives, local(): partner_rows = lax.all_gather(partner, 'y', axis=1, tiled=True)  12.8 us
    all_to_all x1, starting transfers between devices, local(): lax.all_to_all(back, 'ctx', split_axis=0, concat_axis=0, tiled=True)  9.8 us
    ppermute x1, starting transfers between devices, local(): partner = lax.ppermute(attention, 'zh', [(0, 1), (1, 0)])  8.2 us
  transfers between devices with their start and end apart: 3, of which 3 were waited for; matrix products, arithmetic and copies ran while one was open for 1% of the time, Pallas kernels for 0%

profile of v8, /device:TPU:6, one launch (start us, length us, event | category | flops | bytes accessed | tf_op | source)
XLA Modules:
  0.0 309.5 jit_solution(9879162235493104044)
XLA Ops:
  4.2 1.8 copy.71
  6.0 16.2 %all-to-all-start = ((bf16[64,2,2,32,128]{4,3,1,2,0:T(8,128)(2,1)}), bf16[64,2,2,32,128]{4,3,1,2,0:T(8,128)(2,1)S(1)}, u32[]{:S(2)}, u32[]{:S(2)}) async-start(bf16[64,2,2,32,128]{4,3,1,2,0:T(8,128)(2,1)} %copy.71), calls=%async_computation | async-start | bytes 4194304 | tf_op jit(solution)/shard_map/all_to_all | solution.py:75
  22.3 94.5 %all-to-all-done = bf16[64,2,2,32,128]{4,3,1,2,0:T(8,128)(2,1)S(1)} async-done(((bf16[64,2,2,32,128]{4,3,1,2,0:T(8,128)(2,1)}), bf16[64,2,2,32,128]{4,3,1,2,0:T(8,128)(2,1)S(1)}, u32[]{:S(2)}, u32[]{:S(2)}) %all-to-all-start) | async-done | bytes 2097184 | tf_op jit(solution)/shard_map/all_to_all | solution.py:75
  117.4 1.3 multiply_reduce_fusion
  118.7 1.4 fusion
  120.1 1.8 copy-done.1
  122.4 5.0 %fusion.2 = bf16[2,4096,128]{2,1,0:T(8,128)(2,1)S(1)} fusion(f32[2,4096,256]{1,2,0:T(8,128)} %copy-done.1, f32[2,4096]{1,0:T(2,128)S(1)} %get-tuple-element.17, f32[2,4096]{1,0:T(2,128)S(1)} %fusion, bf16[256,256]{1,0:T(8,128)(2,1)S(1)} %copy-done.12), kind=kOutput, calls=%fused_computation.6 | convolution fusion | flops 545259520 | bytes 10682368 | tf_op jit(solution)/shard_map/hrk,khd->hrd/dot_general | solution.py:28
  127.9 1.9 maximum_maximum_fusion
  129.9 9.8 %all-to-all-start.1 = ((bf16[64,144,128]{2,1,0:T(8,128)(2,1)}), bf16[64,144,128]{2,1,0:T(8,128)(2,1)S(1)}, u32[]{:S(2)}, u32[]{:S(2)}) async-start(bf16[64,144,128]{2,1,0:T(8,128)(2,1)} %maximum_maximum_fusion), calls=%async_computation.1 | async-start | bytes 4718592 | tf_op jit(solution)/shard_map/all_to_all | solution.py:104
  141.5 1.3 constant_dynamic-slice_fusion.1
  142.7 2.1 convolution_divide_fusion.1
  144.9 100.4 %all-to-all-done.1 = bf16[64,144,128]{2,1,0:T(8,128)(2,1)S(1)} async-done(((bf16[64,144,128]{2,1,0:T(8,128)(2,1)}), bf16[64,144,128]{2,1,0:T(8,128)(2,1)S(1)}, u32[]{:S(2)}, u32[]{:S(2)}) %all-to-all-start.1) | async-done | bytes 2359328 | tf_op jit(solution)/shard_map/all_to_all | solution.py:104
  245.3 1.4 fusion.44
  246.7 1.4 reshape.206
  249.3 1.9 fusion.57
  251.2 1.4 copy.89
  252.6 1.3 fusion.56
  253.9 1.4 copy.85
  255.3 1.4 copy.91
  257.5 1.2 fusion.12
  259.2 14.0 %all_gather.6 = bf16[256,1024]{1,0:T(8,128)(2,1)S(1)} all-gather(bf16[256,256]{1,0:T(8,128)(2,1)S(1)} %bitcast.112), channel_id=1, replica_groups=mesh['ctx'=64,'y'=4,'zh'=2] {'y'}, dimensions={1}, use_global_device_ids=true | all-gather | bytes 655360 | tf_op jit(solution)/shard_map/all_gather | solution.py:128
  273.2 8.2 %collective-permute-start = (bf16[256,256]{1,0:T(8,128)(2,1)S(1)}, bf16[256,256]{1,0:T(8,128)(2,1)S(1)}, u32[]{:S(2)}, u32[]{:S(2)}) collective-permute-start(bf16[256,256]{1,0:T(8,128)(2,1)S(1)} %bitcast.113), channel_id=1, source_target_pairs={{0,1},{1,0},{2,3},{3,2},{4,5},{5,4},{6,7},{7,6},{8,9},{9,8},{10,11... | collective-permute-start | bytes 393224 | tf_op jit(solution)/shard_map/ppermute | solution.py:129
  281.7 14.0 %collective-permute-done = bf16[256,256]{1,0:T(8,128)(2,1)S(1)} collective-permute-done((bf16[256,256]{1,0:T(8,128)(2,1)S(1)}, bf16[256,256]{1,0:T(8,128)(2,1)S(1)}, u32[]{:S(2)}, u32[]{:S(2)}) %collective-permute-start) | collective-permute-done | bytes 131104 | tf_op jit(solution)/shard_map/ppermute | solution.py:129
  295.8 12.8 %all_gather.7 = bf16[256,1024]{1,0:T(8,128)(2,1)S(1)} all-gather(bf16[256,256]{1,0:T(8,128)(2,1)S(1)} %collective-permute-done), channel_id=1, replica_groups=mesh['ctx'=64,'y'=4,'zh'=2] {'y'}, dimensions={1}, use_global_device_ids=true | all-gather | bytes 655360 | tf_op jit(solution)/shard_map/all_gather | solution.py:130
  (67 shorter events, 11.1 us)
Async XLA Ops:
  0.0 117.4 %copy-start = (bf16[256,256]{1,0:T(8,128)(2,1)S(1)}, bf16[256,256]{1,0:T(8,128)(2,1)}, u32[]{:S(2)}) copy-start(bf16[256,256]{1,0:T(8,128)(2,1)} %param.6) | copy-start | bytes 393220
  1.4 0.6 copy-start.10
  6.0 110.8 %all-to-all-start = ((bf16[64,2,2,32,128]{4,3,1,2,0:T(8,128)(2,1)}), bf16[64,2,2,32,128]{4,3,1,2,0:T(8,128)(2,1)S(1)}, u32[]{:S(2)}, u32[]{:S(2)}) async-start(bf16[64,2,2,32,128]{4,3,1,2,0:T(8,128)(2,1)} %copy.71), calls=%async_computation | async-start | bytes 4194304 | tf_op jit(solution)/shard_map/all_to_all | solution.py:75
  118.6 3.2 %copy-start.1 = (f32[2,4096,256]{1,2,0:T(8,128)}, f32[2,4096,256]{1,2,0:T(8,128)S(1)}, u32[]{:S(2)}) copy-start(f32[2,4096,256]{1,2,0:T(8,128)S(1)} %get-tuple-element.18) | copy-start | bytes 25165828
  118.6 3.7 %copy-start.12 = (bf16[256,256]{1,0:T(8,128)(2,1)S(1)}, bf16[256,256]{1,0:T(8,128)(2,1)}, u32[]{:S(2)}) copy-start(bf16[256,256]{1,0:T(8,128)(2,1)} %param.7) | copy-start | bytes 393220
  127.9 11.8 %copy-start.6 = (bf16[256,256]{1,0:T(8,128)(2,1)S(1)}, bf16[256,256]{1,0:T(8,128)(2,1)}, u32[]{:S(2)}) copy-start(bf16[256,256]{1,0:T(8,128)(2,1)} %param.5) | copy-start | bytes 393220
  129.9 115.3 %all-to-all-start.1 = ((bf16[64,144,128]{2,1,0:T(8,128)(2,1)}), bf16[64,144,128]{2,1,0:T(8,128)(2,1)S(1)}, u32[]{:S(2)}, u32[]{:S(2)}) async-start(bf16[64,144,128]{2,1,0:T(8,128)(2,1)} %maximum_maximum_fusion), calls=%async_computation.1 | async-start | bytes 4718592 | tf_op jit(solution)/shard_map/all_to_all | solution.py:104
  140.0 0.8 copy-start.2
  140.9 0.6 copy-start.9
  141.1 108.1 %copy-start.8 = (pred[2,8,2]{1,2,0:T(4,128)(4,1)}, pred[2,8,2]{1,2,0:T(4,128)(4,1)S(1)}, u32[]{:S(2)}) copy-start(pred[2,8,2]{1,2,0:T(4,128)(4,1)S(1)} %copy.68) | copy-start | bytes 100
  253.9 3.1 copy-start.11
  256.7 0.8 copy-start.7
  256.7 2.1 copy-start.3
  256.7 2.1 copy-start.4
  256.7 2.1 copy-start.5
  273.2 22.6 %collective-permute-start = (bf16[256,256]{1,0:T(8,128)(2,1)S(1)}, bf16[256,256]{1,0:T(8,128)(2,1)S(1)}, u32[]{:S(2)}, u32[]{:S(2)}) collective-permute-start(bf16[256,256]{1,0:T(8,128)(2,1)S(1)} %bitcast.113), channel_id=1, source_target_pairs={{0,1},{1,0},{2,3},{3,2},{4,5},{5,4},{6,7},{7,6},{8,9},{9,8},{10,11... | collective-permute-start | bytes 393224 | tf_op jit(solution)/shard_map/ppermute | solution.py:129

commit v9 on v8

--- a/solution.py
+++ b/solution.py
@@ -1,6 +1,10 @@
+import functools
+
 import jax
 import jax.numpy as jnp
 from jax import lax
+from jax.experimental import pallas as pl
+from jax.experimental.pallas import tpu as pltpu
 from jax.sharding import Mesh, PartitionSpec as P
 
 CAP = 2
@@ -29,6 +33,57 @@
         "hrk,khd->hrd", prob.astype(jnp.bfloat16), vals, preferred_element_type=jnp.float32
     )
     return part / total[..., None], top + jnp.log(total)
+
+
+def owner_kernel(scale, q_ref, k_ref, v_ref, part_ref, lse_ref):
+    groups = q_ref.shape[0]
+    slots = q_ref.shape[1]
+    rows = q_ref.shape[2]
+    width = q_ref.shape[3]
+    heads = k_ref.shape[1] // width
+    nt = (((1,), (1,)), ((), ()))
+    for j in range(slots):
+        cols = pl.ds((j % heads) * width, width)
+        q = q_ref[:, j].reshape(groups * rows, width)
+        k = k_ref[:, cols]
+        v = v_ref[:, cols]
+        s = lax.dot_general(q, k, nt, preferred_element_type=jnp.float32) * scale
+        top = jnp.max(s, axis=1, keepdims=True)
+        prob = jnp.exp(s - top)
+        total = jnp.sum(prob, axis=1, keepdims=True)
+        out = jnp.dot(prob.astype(jnp.bfloat16), v, preferred_element_type=jnp.float32) / total
+        part_ref[:, j] = out.reshape(groups, rows, width).astype(part_ref.dtype)
+        s_t = lax.dot_general(k, q, nt, preferred_element_type=jnp.float32) * scale
+        top_t = jnp.max(s_t, axis=0, keepdims=True)
+        total_t = jnp.sum(jnp.exp(s_t - top_t), axis=0, keepdims=True)
+        lse_ref[pl.ds(j, 1), :] = top_t + jnp.log(total_t)
+
+
+def owner_attention(got, keys, values, scale):
+    sources, slots, rows, width = got.shape
+    step = 8
+    return pl.pallas_call(
+        functools.partial(owner_kernel, scale),
+        grid=(sources // step,),
+        in_specs=[
+            pl.BlockSpec((step, slots, rows, width), lambda i: (i, 0, 0, 0)),
+            pl.BlockSpec(keys.shape, lambda i: (0, 0)),
+            pl.BlockSpec(values.shape, lambda i: (0, 0)),
+        ],
+        out_specs=[
+            pl.BlockSpec((step, slots, rows, width), lambda i: (i, 0, 0, 0)),
+            pl.BlockSpec((slots, step * rows), lambda i: (0, i)),
+        ],
+        out_shape=[
+            jax.ShapeDtypeStruct(got.shape, jnp.bfloat16),
+            jax.ShapeDtypeStruct((slots, sources * rows), jnp.float32),
+        ],
+        cost_estimate=pl.CostEstimate(
+            flops=6 * sources * slots * rows * keys.shape[0] * width,
+            transcendentals=2 * sources * slots * rows * keys.shape[0],
+            bytes_accessed=2 * got.size * 2 + 4 * slots * sources * rows,
+        ),
+    )(got, keys, values)
 
 
 def local(queries, keys, values, selected, out_weight):
@@ -74,21 +129,15 @@
     send_q = send_q.reshape(sources, CAP, heads_loc, tile_rows, width)
     got_rows = lax.all_to_all(send_q, "ctx", split_axis=0, concat_axis=0, tiled=True)
 
-    got_q = jnp.transpose(got_rows, (2, 0, 1, 3, 4)).reshape(
-        heads_loc, sources * CAP * tile_rows, width
-    )
-    got_scores = (
-        jnp.einsum("hrd,khd->hrk", got_q, keys_three, preferred_element_type=jnp.float32) * scale
-    )
-    part, lse = softmax_pv(got_scores, vals_three)
-    part = jnp.transpose(
-        part.reshape(heads_loc, sources, CAP, tile_rows, width), (1, 2, 0, 3, 4)
-    ).reshape(sources, CAP * heads_loc * tile_rows, width)
-    pieces = split_bf16(lse.reshape(heads_loc, sources, CAP, tile_rows))
+    part, lse = owner_attention(
+        got_rows.reshape(sources, CAP * heads_loc, tile_rows, width), keys, values, scale
+    )
+    part = part.reshape(sources, CAP * heads_loc * tile_rows, width)
+    pieces = split_bf16(lse.reshape(CAP, heads_loc, sources, tile_rows))
     pieces = jnp.concatenate(
         [pieces, jnp.zeros((LANE_ROWS - 3,) + pieces.shape[1:], pieces.dtype)], axis=0
     )
-    lse_rows = jnp.transpose(pieces, (2, 3, 1, 0, 4)).reshape(
+    lse_rows = jnp.transpose(pieces, (3, 1, 2, 0, 4)).reshape(
         sources, CAP * heads_loc, LANE_ROWS * tile_rows
     )
     rows_part = CAP * heads_loc * tile_rows

time: 311 us -> 304 us (0.977)
  Pallas kernels: 0 us -> 11.4 us
  local copies, waits for them, and re-layouts: 18.4 us -> 10.5 us
  matrix products: 13.4 us -> 5.59 us
    pallas_call x0 -> x1, Pallas kernels: none -> 11.4 us  [owner_attention(): pl.pallas_call(functools.partial(owner_kernel, scale), grid=(sources // s...]
    dot_general x2 -> x1, matrix products: 7.14 us -> 1.91 us  [softmax_pv(): jnp.einsum('hrk,khd->hrd', prob.astype(jnp.bfloat16), vals, preferred_ele...]
where the time goes in v9:
time: 304 us; the launch traced here: 303 us
  waiting for transfers between devices  209 us (69%)
  starting transfers between devices  34.4 us (11%)
  blocking collectives  26.8 us (9%)
  Pallas kernels  11.4 us (4%)
  local copies, waits for them, and re-layouts  10.5 us (3%)
  matrix products  5.59 us (2%)
  other arithmetic  4.54 us (1%)
    all_to_all x1, waiting for transfers between devices, local(): lax.all_to_all(back, 'ctx', split_axis=0, concat_axis=0, tiled=True)  101 us
    all_to_all x1, waiting for transfers between devices, local(): lax.all_to_all(send_q, 'ctx', split_axis=0, concat_axis=0, tiled=True)  94.5 us
    all_to_all x1, starting transfers between devices, local(): lax.all_to_all(send_q, 'ctx', split_axis=0, concat_axis=0, tiled=True)  16.2 us
    ppermute x1, waiting for transfers between devices, local(): partner = lax.ppermute(attention, 'zh', [(0, 1), (1, 0)])  14 us
    all_gather x1, blocking collectives, local(): own_rows = lax.all_gather(attention, 'y', axis=1, tiled=True)  14 us
    all_gather x1, blocking collectives, local(): partner_rows = lax.all_gather(partner, 'y', axis=1, tiled=True)  12.8 us
    pallas_call x1, Pallas kernels, owner_attention(): pl.pallas_call(functools.partial(owner_kernel, scale), grid=(sources // s...  11.4 us
    all_to_all x1, starting transfers between devices, local(): lax.all_to_all(back, 'ctx', split_axis=0, concat_axis=0, tiled=True)  9.91 us
  transfers between devices with their start and end apart: 3, of which 3 were waited for; matrix products, arithmetic and copies ran while one was open for 1% of the time, Pallas kernels for 0%

profile of v9, /device:TPU:6, one launch (start us, length us, event | category | flops | bytes accessed | tf_op | source)
XLA Modules:
  0.0 302.8 jit_solution(8630671374349250780)
XLA Ops:
  0.0 0.7 slice.18
  1.4 1.0 reshape_reshape.3
  2.4 0.7 convolution_convert_fusion
  3.1 0.5 copy.70
  3.6 1.9 copy.40
  5.5 16.2 %all-to-all-start = ((bf16[64,2,2,32,128]{4,3,2,1,0:T(8,128)(2,1)}), bf16[64,2,2,32,128]{4,3,2,1,0:T(8,128)(2,1)S(1)}, u32[]{:S(2)}, u32[]{:S(2)}) async-start(bf16[64,2,2,32,128]{4,3,2,1,0:T(8,128)(2,1)} %copy.40), calls=%async_computation | async-start | bytes 4194304 | tf_op jit(solution)/shard_map/all_to_all | solution.py:130
  21.8 94.5 %all-to-all-done = bf16[64,2,2,32,128]{4,3,2,1,0:T(8,128)(2,1)S(1)} async-done(((bf16[64,2,2,32,128]{4,3,2,1,0:T(8,128)(2,1)}), bf16[64,2,2,32,128]{4,3,2,1,0:T(8,128)(2,1)S(1)}, u32[]{:S(2)}, u32[]{:S(2)}) %all-to-all-start) | async-done | bytes 2097184 | tf_op jit(solution)/shard_map/all_to_all | solution.py:130
  116.3 1.3 copy-done
  117.7 11.4 %shard_map.55 = (bf16[64,4,32,128]{3,2,1,0:T(8,128)(2,1)}, f32[4,2048]{1,0:T(4,128)}) custom-call(bf16[64,4,32,128]{3,2,1,0:T(8,128)(2,1)} %bitcast.88, bf16[256,256]{1,0:T(8,128)(2,1)} %k_ref.1, bf16[256,256]{1,0:T(8,128)(2,1)} %v_ref.1), custom_call_target="tpu_custom_call" | custom-call | flops 1610612736 | bytes 4227072 | tf_op jit(solution)/shard_map/pallas_call | solution.py:65
  129.1 0.9 reshape.187
  130.3 3.5 %maximum_maximum_fusion = bf16[64,144,128]{2,1,0:T(8,128)(2,1)} fusion(bf16[64,4,128]{2,1,0:T(4,128)(2,1)S(1)} %copy.42, bf16[64,128,128]{2,1,0:T(8,128)(2,1)} %bitcast.87, bf16[144]{0:T(256)(128)(2,1)S(1)} %pad.3.clone), kind=kLoop, calls=%fused_computation.1 | loop fusion | flops 7077888 | bytes 4522272 | tf_op jit(solution)/shard_map/concatenate | solution.py:145
  133.9 9.9 %all-to-all-start.1 = ((bf16[64,144,128]{2,1,0:T(8,128)(2,1)}), bf16[64,144,128]{2,1,0:T(8,128)(2,1)S(1)}, u32[]{:S(2)}, u32[]{:S(2)}) async-start(bf16[64,144,128]{2,1,0:T(8,128)(2,1)} %maximum_maximum_fusion), calls=%async_computation.1 | async-start | bytes 4718592 | tf_op jit(solution)/shard_map/all_to_all | solution.py:153
  144.1 0.8 copy-done.1
  145.2 1.3 constant_dynamic-slice_fusion.1
  146.5 1.9 convolution_divide_fusion
  148.5 100.9 %all-to-all-done.1 = bf16[64,144,128]{2,1,0:T(8,128)(2,1)S(1)} async-done(((bf16[64,144,128]{2,1,0:T(8,128)(2,1)}), bf16[64,144,128]{2,1,0:T(8,128)(2,1)S(1)}, u32[]{:S(2)}, u32[]{:S(2)}) %all-to-all-start.1) | async-done | bytes 2359328 | tf_op jit(solution)/shard_map/all_to_all | solution.py:153
  250.4 0.4 copy-done.6
  250.8 1.2 fusion.6
  252.5 14.0 %all_gather.6 = bf16[256,1024]{1,0:T(8,128)(2,1)S(1)} all-gather(bf16[256,256]{1,0:T(8,128)(2,1)S(1)} %bitcast.93), channel_id=1, replica_groups=mesh['ctx'=64,'y'=4,'zh'=2] {'y'}, dimensions={1}, use_global_device_ids=true | all-gather | bytes 655360 | tf_op jit(solution)/shard_map/all_gather | solution.py:177
  266.5 8.2 %collective-permute-start = (bf16[256,256]{1,0:T(8,128)(2,1)S(1)}, bf16[256,256]{1,0:T(8,128)(2,1)S(1)}, u32[]{:S(2)}, u32[]{:S(2)}) collective-permute-start(bf16[256,256]{1,0:T(8,128)(2,1)S(1)} %bitcast.94), channel_id=1, source_target_pairs={{0,1},{1,0},{2,3},{3,2},{4,5},{5,4},{6,7},{7,6},{8,9},{9,8},{10,11... | collective-permute-start | bytes 393224 | tf_op jit(solution)/shard_map/ppermute | solution.py:178
  274.7 0.3 fusion.49
  275.0 14.0 %collective-permute-done = bf16[256,256]{1,0:T(8,128)(2,1)S(1)} collective-permute-done((bf16[256,256]{1,0:T(8,128)(2,1)S(1)}, bf16[256,256]{1,0:T(8,128)(2,1)S(1)}, u32[]{:S(2)}, u32[]{:S(2)}) %collective-permute-start) | collective-permute-done | bytes 131104 | tf_op jit(solution)/shard_map/ppermute | solution.py:178
  289.0 12.8 %all_gather.7 = bf16[256,1024]{1,0:T(8,128)(2,1)S(1)} all-gather(bf16[256,256]{1,0:T(8,128)(2,1)S(1)} %collective-permute-done), channel_id=1, replica_groups=mesh['ctx'=64,'y'=4,'zh'=2] {'y'}, dimensions={1}, use_global_device_ids=true | all-gather | bytes 655360 | tf_op jit(solution)/shard_map/all_gather | solution.py:179
  301.8 1.0 fusion.9
  (51 shorter events, 3.2 us)
Async XLA Ops:
  1.3 248.0 %copy-start.5 = (s32[2,8,2]{1,2,0:T(2,128)}, s32[2,8,2]{1,2,0:T(2,128)S(1)}, u32[]{:S(2)}) copy-start(s32[2,8,2]{1,2,0:T(2,128)S(1)} %copy.38) | copy-start | bytes 388
  5.5 110.8 %all-to-all-start = ((bf16[64,2,2,32,128]{4,3,2,1,0:T(8,128)(2,1)}), bf16[64,2,2,32,128]{4,3,2,1,0:T(8,128)(2,1)S(1)}, u32[]{:S(2)}, u32[]{:S(2)}) async-start(bf16[64,2,2,32,128]{4,3,2,1,0:T(8,128)(2,1)} %copy.40), calls=%async_computation | async-start | bytes 4194304 | tf_op jit(solution)/shard_map/all_to_all | solution.py:130
  116.3 1.4 copy-start
  133.8 10.0 %copy-start.4 = (bf16[256,256]{1,0:T(8,128)(2,1)S(1)}, bf16[256,256]{1,0:T(8,128)(2,1)}, u32[]{:S(2)}) copy-start(bf16[256,256]{1,0:T(8,128)(2,1)} %param.5) | copy-start | bytes 393220
  133.8 10.0 %copy-start.7 = (bf16[256,256]{1,0:T(8,128)(2,1)S(1)}, bf16[256,256]{1,0:T(8,128)(2,1)}, u32[]{:S(2)}) copy-start(bf16[256,256]{1,0:T(8,128)(2,1)} %k_ref.1) | copy-start | bytes 393220
  133.9 115.5 %all-to-all-start.1 = ((bf16[64,144,128]{2,1,0:T(8,128)(2,1)}), bf16[64,144,128]{2,1,0:T(8,128)(2,1)S(1)}, u32[]{:S(2)}, u32[]{:S(2)}) async-start(bf16[64,144,128]{2,1,0:T(8,128)(2,1)} %maximum_maximum_fusion), calls=%async_computation.1 | async-start | bytes 4718592 | tf_op jit(solution)/shard_map/all_to_all | solution.py:153
  144.1 0.8 copy-start.1
  145.2 1.4 copy-start.2
  250.1 0.7 copy-start.6
  250.4 1.6 copy-start.3
  266.5 22.6 %collective-permute-start = (bf16[256,256]{1,0:T(8,128)(2,1)S(1)}, bf16[256,256]{1,0:T(8,128)(2,1)S(1)}, u32[]{:S(2)}, u32[]{:S(2)}) collective-permute-start(bf16[256,256]{1,0:T(8,128)(2,1)S(1)} %bitcast.94), channel_id=1, source_target_pairs={{0,1},{1,0},{2,3},{3,2},{4,5},{5,4},{6,7},{7,6},{8,9},{9,8},{10,11... | collective-permute-start | bytes 393224 | tf_op jit(solution)/shard_map/ppermute | solution.py:178

commit v10 on v9

--- a/solution.py
+++ b/solution.py
@@ -42,26 +42,26 @@
     width = q_ref.shape[3]
     heads = k_ref.shape[1] // width
     nt = (((1,), (1,)), ((), ()))
+    tn = (((0,), (0,)), ((), ()))
     for j in range(slots):
         cols = pl.ds((j % heads) * width, width)
         q = q_ref[:, j].reshape(groups * rows, width)
         k = k_ref[:, cols]
         v = v_ref[:, cols]
-        s = lax.dot_general(q, k, nt, preferred_element_type=jnp.float32) * scale
-        top = jnp.max(s, axis=1, keepdims=True)
-        prob = jnp.exp(s - top)
-        total = jnp.sum(prob, axis=1, keepdims=True)
-        out = jnp.dot(prob.astype(jnp.bfloat16), v, preferred_element_type=jnp.float32) / total
-        part_ref[:, j] = out.reshape(groups, rows, width).astype(part_ref.dtype)
         s_t = lax.dot_general(k, q, nt, preferred_element_type=jnp.float32) * scale
         top_t = jnp.max(s_t, axis=0, keepdims=True)
-        total_t = jnp.sum(jnp.exp(s_t - top_t), axis=0, keepdims=True)
+        prob_t = jnp.exp(s_t - top_t)
+        total_t = jnp.sum(prob_t, axis=0, keepdims=True)
+        out_t = lax.dot_general(
+            v, prob_t.astype(jnp.bfloat16), tn, preferred_element_type=jnp.float32
+        ) / total_t
+        part_ref[:, j] = out_t.T.reshape(groups, rows, width).astype(part_ref.dtype)
         lse_ref[pl.ds(j, 1), :] = top_t + jnp.log(total_t)
 
 
 def owner_attention(got, keys, values, scale):
     sources, slots, rows, width = got.shape
-    step = 8
+    step = 16
     return pl.pallas_call(
         functools.partial(owner_kernel, scale),
         grid=(sources // step,),

time: 304 us -> 301 us (level)
  no operation moved by 1% of the time
where the time goes in v10:
time: 301 us; the launch traced here: 300 us
  waiting for transfers between devices  209 us (69%)
  starting transfers between devices  34.3 us (11%)
  blocking collectives  26.8 us (9%)
  local copies, waits for them, and re-layouts  10.5 us (3%)
  Pallas kernels  8.62 us (3%)
  matrix products  5.59 us (2%)
  other arithmetic  4.54 us (2%)
    all_to_all x1, waiting for transfers between devices, local(): lax.all_to_all(back, 'ctx', split_axis=0, concat_axis=0, tiled=True)  101 us
    all_to_all x1, waiting for transfers between devices, local(): lax.all_to_all(send_q, 'ctx', split_axis=0, concat_axis=0, tiled=True)  94.5 us
    all_to_all x1, starting transfers between devices, local(): lax.all_to_all(send_q, 'ctx', split_axis=0, concat_axis=0, tiled=True)  16.2 us
    ppermute x1, waiting for transfers between devices, local(): partner = lax.ppermute(attention, 'zh', [(0, 1), (1, 0)])  14 us
    all_gather x1, blocking collectives, local(): own_rows = lax.all_gather(attention, 'y', axis=1, tiled=True)  14 us
    all_gather x1, blocking collectives, local(): partner_rows = lax.all_gather(partner, 'y', axis=1, tiled=True)  12.8 us
    all_to_all x1, starting transfers between devices, local(): lax.all_to_all(back, 'ctx', split_axis=0, concat_axis=0, tiled=True)  9.91 us
    pallas_call x1, Pallas kernels, owner_attention(): pl.pallas_call(functools.partial(owner_kernel, scale), grid=(sources // s...  8.62 us
  transfers between devices with their start and end apart: 3, of which 3 were waited for; matrix products, arithmetic and copies ran while one was open for 1% of the time, Pallas kernels for 0%

profile of v10, /device:TPU:6, one launch (start us, length us, event | category | flops | bytes accessed | tf_op | source)
XLA Modules:
  0.0 300.0 jit_solution(1811320393948233517)
XLA Ops:
  0.0 0.7 slice.18
  1.4 1.0 reshape_reshape.3
  2.4 0.7 convolution_convert_fusion
  3.1 0.5 copy.70
  3.6 1.9 copy.40
  5.5 16.2 %all-to-all-start = ((bf16[64,2,2,32,128]{4,3,2,1,0:T(8,128)(2,1)}), bf16[64,2,2,32,128]{4,3,2,1,0:T(8,128)(2,1)S(1)}, u32[]{:S(2)}, u32[]{:S(2)}) async-start(bf16[64,2,2,32,128]{4,3,2,1,0:T(8,128)(2,1)} %copy.40), calls=%async_computation | async-start | bytes 4194304 | tf_op jit(solution)/shard_map/all_to_all | solution.py:130
  21.8 94.5 %all-to-all-done = bf16[64,2,2,32,128]{4,3,2,1,0:T(8,128)(2,1)S(1)} async-done(((bf16[64,2,2,32,128]{4,3,2,1,0:T(8,128)(2,1)}), bf16[64,2,2,32,128]{4,3,2,1,0:T(8,128)(2,1)S(1)}, u32[]{:S(2)}, u32[]{:S(2)}) %all-to-all-start) | async-done | bytes 2097184 | tf_op jit(solution)/shard_map/all_to_all | solution.py:130
  116.3 1.3 copy-done
  117.7 8.6 %shard_map.55 = (bf16[64,4,32,128]{3,2,1,0:T(8,128)(2,1)}, f32[4,2048]{1,0:T(4,128)}) custom-call(bf16[64,4,32,128]{3,2,1,0:T(8,128)(2,1)} %bitcast.88, bf16[256,256]{1,0:T(8,128)(2,1)} %k_ref.1, bf16[256,256]{1,0:T(8,128)(2,1)} %v_ref.1), custom_call_target="tpu_custom_call" | custom-call | flops 1610612736 | bytes 4227072 | tf_op jit(solution)/shard_map/pallas_call | solution.py:65
  126.3 0.9 reshape.187
  127.5 3.5 %maximum_maximum_fusion = bf16[64,144,128]{2,1,0:T(8,128)(2,1)} fusion(bf16[64,4,128]{2,1,0:T(4,128)(2,1)S(1)} %copy.42, bf16[64,128,128]{2,1,0:T(8,128)(2,1)} %bitcast.87, bf16[144]{0:T(256)(128)(2,1)S(1)} %pad.3.clone), kind=kLoop, calls=%fused_computation.1 | loop fusion | flops 7077888 | bytes 4522272 | tf_op jit(solution)/shard_map/concatenate | solution.py:145
  131.1 9.9 %all-to-all-start.1 = ((bf16[64,144,128]{2,1,0:T(8,128)(2,1)}), bf16[64,144,128]{2,1,0:T(8,128)(2,1)S(1)}, u32[]{:S(2)}, u32[]{:S(2)}) async-start(bf16[64,144,128]{2,1,0:T(8,128)(2,1)} %maximum_maximum_fusion), calls=%async_computation.1 | async-start | bytes 4718592 | tf_op jit(solution)/shard_map/all_to_all | solution.py:153
  141.3 0.8 copy-done.1
  142.4 1.3 constant_dynamic-slice_fusion.1
  143.8 1.9 convolution_divide_fusion
  145.7 100.9 %all-to-all-done.1 = bf16[64,144,128]{2,1,0:T(8,128)(2,1)S(1)} async-done(((bf16[64,144,128]{2,1,0:T(8,128)(2,1)}), bf16[64,144,128]{2,1,0:T(8,128)(2,1)S(1)}, u32[]{:S(2)}, u32[]{:S(2)}) %all-to-all-start.1) | async-done | bytes 2359328 | tf_op jit(solution)/shard_map/all_to_all | solution.py:153
  247.7 0.4 copy-done.6
  248.0 1.2 fusion.6
  249.7 14.0 %all_gather.6 = bf16[256,1024]{1,0:T(8,128)(2,1)S(1)} all-gather(bf16[256,256]{1,0:T(8,128)(2,1)S(1)} %bitcast.93), channel_id=1, replica_groups=mesh['ctx'=64,'y'=4,'zh'=2] {'y'}, dimensions={1}, use_global_device_ids=true | all-gather | bytes 655360 | tf_op jit(solution)/shard_map/all_gather | solution.py:177
  263.7 8.2 %collective-permute-start = (bf16[256,256]{1,0:T(8,128)(2,1)S(1)}, bf16[256,256]{1,0:T(8,128)(2,1)S(1)}, u32[]{:S(2)}, u32[]{:S(2)}) collective-permute-start(bf16[256,256]{1,0:T(8,128)(2,1)S(1)} %bitcast.94), channel_id=1, source_target_pairs={{0,1},{1,0},{2,3},{3,2},{4,5},{5,4},{6,7},{7,6},{8,9},{9,8},{10,11... | collective-permute-start | bytes 393224 | tf_op jit(solution)/shard_map/ppermute | solution.py:178
  271.9 0.3 fusion.49
  272.2 14.0 %collective-permute-done = bf16[256,256]{1,0:T(8,128)(2,1)S(1)} collective-permute-done((bf16[256,256]{1,0:T(8,128)(2,1)S(1)}, bf16[256,256]{1,0:T(8,128)(2,1)S(1)}, u32[]{:S(2)}, u32[]{:S(2)}) %collective-permute-start) | collective-permute-done | bytes 131104 | tf_op jit(solution)/shard_map/ppermute | solution.py:178
  286.3 12.8 %all_gather.7 = bf16[256,1024]{1,0:T(8,128)(2,1)S(1)} all-gather(bf16[256,256]{1,0:T(8,128)(2,1)S(1)} %collective-permute-done), channel_id=1, replica_groups=mesh['ctx'=64,'y'=4,'zh'=2] {'y'}, dimensions={1}, use_global_device_ids=true | all-gather | bytes 655360 | tf_op jit(solution)/shard_map/all_gather | solution.py:179
  299.0 1.0 fusion.9
  (51 shorter events, 3.2 us)
Async XLA Ops:
  1.3 245.3 %copy-start.5 = (s32[2,8,2]{1,2,0:T(2,128)}, s32[2,8,2]{1,2,0:T(2,128)S(1)}, u32[]{:S(2)}) copy-start(s32[2,8,2]{1,2,0:T(2,128)S(1)} %copy.38) | copy-start | bytes 388
  5.5 110.8 %all-to-all-start = ((bf16[64,2,2,32,128]{4,3,2,1,0:T(8,128)(2,1)}), bf16[64,2,2,32,128]{4,3,2,1,0:T(8,128)(2,1)S(1)}, u32[]{:S(2)}, u32[]{:S(2)}) async-start(bf16[64,2,2,32,128]{4,3,2,1,0:T(8,128)(2,1)} %copy.40), calls=%async_computation | async-start | bytes 4194304 | tf_op jit(solution)/shard_map/all_to_all | solution.py:130
  116.3 1.4 copy-start
  131.1 10.0 %copy-start.4 = (bf16[256,256]{1,0:T(8,128)(2,1)S(1)}, bf16[256,256]{1,0:T(8,128)(2,1)}, u32[]{:S(2)}) copy-start(bf16[256,256]{1,0:T(8,128)(2,1)} %param.5) | copy-start | bytes 393220
  131.1 10.0 %copy-start.7 = (bf16[256,256]{1,0:T(8,128)(2,1)S(1)}, bf16[256,256]{1,0:T(8,128)(2,1)}, u32[]{:S(2)}) copy-start(bf16[256,256]{1,0:T(8,128)(2,1)} %k_ref.1) | copy-start | bytes 393220
  131.1 115.5 %all-to-all-start.1 = ((bf16[64,144,128]{2,1,0:T(8,128)(2,1)}), bf16[64,144,128]{2,1,0:T(8,128)(2,1)S(1)}, u32[]{:S(2)}, u32[]{:S(2)}) async-start(bf16[64,144,128]{2,1,0:T(8,128)(2,1)} %maximum_maximum_fusion), calls=%async_computation.1 | async-start | bytes 4718592 | tf_op jit(solution)/shard_map/all_to_all | solution.py:153
  141.3 0.8 copy-start.1
  142.4 1.4 copy-start.2
  247.4 0.7 copy-start.6
  247.7 1.6 copy-start.3
  263.7 22.6 %collective-permute-start = (bf16[256,256]{1,0:T(8,128)(2,1)S(1)}, bf16[256,256]{1,0:T(8,128)(2,1)S(1)}, u32[]{:S(2)}, u32[]{:S(2)}) collective-permute-start(bf16[256,256]{1,0:T(8,128)(2,1)S(1)} %bitcast.94), channel_id=1, source_target_pairs={{0,1},{1,0},{2,3},{3,2},{4,5},{5,4},{6,7},{7,6},{8,9},{9,8},{10,11... | collective-permute-start | bytes 393224 | tf_op jit(solution)/shard_map/ppermute | solution.py:178

commit v11 on v10

--- a/solution.py
+++ b/solution.py
@@ -43,6 +43,8 @@
     heads = k_ref.shape[1] // width
     nt = (((1,), (1,)), ((), ()))
     tn = (((0,), (0,)), ((), ()))
+    tail = part_ref.shape[1] - slots * rows
+    part_ref[:, pl.ds(slots * rows, tail)] = jnp.zeros((groups, tail, width), part_ref.dtype)
     for j in range(slots):
         cols = pl.ds((j % heads) * width, width)
         q = q_ref[:, j].reshape(groups * rows, width)
@@ -55,13 +57,16 @@
         out_t = lax.dot_general(
             v, prob_t.astype(jnp.bfloat16), tn, preferred_element_type=jnp.float32
         ) / total_t
-        part_ref[:, j] = out_t.T.reshape(groups, rows, width).astype(part_ref.dtype)
+        part_ref[:, pl.ds(j * rows, rows)] = out_t.T.reshape(groups, rows, width).astype(
+            part_ref.dtype
+        )
         lse_ref[pl.ds(j, 1), :] = top_t + jnp.log(total_t)
 
 
-def owner_attention(got, keys, values, scale):
+def owner_attention(got, keys, values, scale, extra):
     sources, slots, rows, width = got.shape
     step = 16
+    packed = (sources, slots * rows + extra, width)
     return pl.pallas_call(
         functools.partial(owner_kernel, scale),
         grid=(sources // step,),
@@ -71,11 +76,11 @@
             pl.BlockSpec(values.shape, lambda i: (0, 0)),
         ],
         out_specs=[
-            pl.BlockSpec((step, slots, rows, width), lambda i: (i, 0, 0, 0)),
+            pl.BlockSpec((step,) + packed[1:], lambda i: (i, 0, 0)),
             pl.BlockSpec((slots, step * rows), lambda i: (0, i)),
         ],
         out_shape=[
-            jax.ShapeDtypeStruct(got.shape, jnp.bfloat16),
+            jax.ShapeDtypeStruct(packed, jnp.bfloat16),
             jax.ShapeDtypeStruct((slots, sources * rows), jnp.float32),
         ],
         cost_estimate=pl.CostEstimate(
@@ -129,10 +134,11 @@
     send_q = send_q.reshape(sources, CAP, heads_loc, tile_rows, width)
     got_rows = lax.all_to_all(send_q, "ctx", split_axis=0, concat_axis=0, tiled=True)
 
-    part, lse = owner_attention(
-        got_rows.reshape(sources, CAP * heads_loc, tile_rows, width), keys, values, scale
-    )
-    part = part.reshape(sources, CAP * heads_loc * tile_rows, width)
+    rows_part = CAP * heads_loc * tile_rows
+    extra = -(rows_part + CAP * heads_loc) % 16 + CAP * heads_loc
+    back, lse = owner_attention(
+        got_rows.reshape(sources, CAP * heads_loc, tile_rows, width), keys, values, scale, extra
+    )
     pieces = split_bf16(lse.reshape(CAP, heads_loc, sources, tile_rows))
     pieces = jnp.concatenate(
         [pieces, jnp.zeros((LANE_ROWS - 3,) + pieces.shape[1:], pieces.dtype)], axis=0
@@ -140,16 +146,7 @@
     lse_rows = jnp.transpose(pieces, (3, 1, 2, 0, 4)).reshape(
         sources, CAP * heads_loc, LANE_ROWS * tile_rows
     )
-    rows_part = CAP * heads_loc * tile_rows
-    pad = -(rows_part + CAP * heads_loc) % 16
-    back = jnp.concatenate(
-        [
-            part.astype(jnp.bfloat16),
-            lse_rows,
-            jnp.zeros((sources, pad, width), jnp.bfloat16),
-        ],
-        axis=1,
-    )
+    back = lax.dynamic_update_slice_in_dim(back, lse_rows, rows_part, axis=1)
     got_back = lax.all_to_all(back, "ctx", split_axis=0, concat_axis=0, tiled=True)
     got_out = got_back[:, :rows_part].reshape(sources * CAP, heads_loc, tile_rows, width)
     got_lse = got_back[:, rows_part : rows_part + CAP * heads_loc].reshape(

time: 301 us -> 295 us (0.980)
  blocking collectives: 26.8 us -> 138 us
  waiting for transfers between devices: 209 us -> 115 us
  starting transfers between devices: 34.3 us -> 18.1 us
  other arithmetic: 4.54 us -> 1 us
    all_to_all x0 -> x1, blocking collectives: none -> 111 us  [local(): lax.all_to_all(send_q, 'ctx', split_axis=0, concat_axis=0, tiled=True)]
    all_to_all x1 -> x0, waiting for transfers between devices: 94.5 us -> none  [local(): lax.all_to_all(send_q, 'ctx', split_axis=0, concat_axis=0, tiled=True)]
    all_to_all x1 -> x0, starting transfers between devices: 16.2 us -> none  [local(): lax.all_to_all(send_q, 'ctx', split_axis=0, concat_axis=0, tiled=True)]
    concatenate x1 -> x0, other arithmetic: 3.54 us -> none  [local(): jnp.concatenate([part.astype(jnp.bfloat16), lse_rows, jnp.zeros((sources,...]
  transfers between devices with their start and end apart: 3 -> 2, of which waited for: 3 -> 2; matrix products, arithmetic and copies ran while one was open for 1% -> 1% of each run, Pallas kernels for 0% -> 0%
where the time goes in v11:
time: 295 us; the launch traced here: 294 us
  blocking collectives  138 us (47%)
  waiting for transfers between devices  115 us (39%)
  starting transfers between devices  18.1 us (6%)
  Pallas kernels  8.65 us (3%)
  local copies, waits for them, and re-layouts  8.39 us (3%)
  matrix products  5.58 us (2%)
    all_to_all x1, blocking collectives, local(): lax.all_to_all(send_q, 'ctx', split_axis=0, concat_axis=0, tiled=True)  111 us
    all_to_all x1, waiting for transfers between devices, local(): lax.all_to_all(back, 'ctx', split_axis=0, concat_axis=0, tiled=True)  101 us
    ppermute x1, waiting for transfers between devices, local(): partner = lax.ppermute(attention, 'zh', [(0, 1), (1, 0)])  14 us
    all_gather x1, blocking collectives, local(): own_rows = lax.all_gather(attention, 'y', axis=1, tiled=True)  14 us
    all_gather x1, blocking collectives, local(): partner_rows = lax.all_gather(partner, 'y', axis=1, tiled=True)  12.8 us
    all_to_all x1, starting transfers between devices, local(): lax.all_to_all(back, 'ctx', split_axis=0, concat_axis=0, tiled=True)  9.9 us
    pallas_call x1, Pallas kernels, owner_attention(): pl.pallas_call(functools.partial(owner_kernel, scale), grid=(sources // s...  8.65 us
    ppermute x1, starting transfers between devices, local(): partner = lax.ppermute(attention, 'zh', [(0, 1), (1, 0)])  8.21 us
  transfers between devices with their start and end apart: 2, of which 2 were waited for; matrix products, arithmetic and copies ran while one was open for 1% of the time, Pallas kernels for 0%

profile of v11, /device:TPU:6, one launch (start us, length us, event | category | flops | bytes accessed | tf_op | source)
XLA Modules:
  0.0 294.4 jit_solution(13955638980446748346)
XLA Ops:
  0.0 0.7 slice.18
  1.4 1.0 reshape_reshape.3
  2.4 0.7 convolution_convert_fusion
  3.1 0.5 copy.73
  3.6 0.6 copy.43
  4.2 110.7 %all_to_all.10 = bf16[64,2,2,32,128]{4,3,2,1,0:T(8,128)(2,1)} all-to-all(bf16[64,2,2,32,128]{4,3,2,1,0:T(8,128)(2,1)S(1)} %copy.43), channel_id=1, replica_groups=mesh['ctx'=64,'y'=4,'zh'=2] {'ctx'}, dimensions={0} | all-to-all | bytes 4194304 | tf_op jit(solution)/shard_map/all_to_all | solution.py:135
  114.9 8.6 %shard_map.55 = (bf16[64,144,128]{2,1,0:T(8,128)(2,1)}, f32[4,2048]{1,0:T(4,128)}) custom-call(bf16[64,4,32,128]{3,2,1,0:T(8,128)(2,1)} %bitcast.86, bf16[256,256]{1,0:T(8,128)(2,1)} %k_ref.1, bf16[256,256]{1,0:T(8,128)(2,1)} %v_ref.1), custom_call_target="tpu_custom_call" | custom-call | flops 1610612736 | bytes 4227072 | tf_op jit(solution)/shard_map/pallas_call | solution.py:70
  123.6 0.9 reshape.183
  124.8 0.7 constant_dynamic-update-slice_fusion
  125.5 9.9 %all-to-all-start.1 = ((bf16[64,144,128]{2,1,0:T(8,128)(2,1)}), bf16[64,144,128]{2,1,0:T(8,128)(2,1)S(1)}, u32[]{:S(2)}, u32[]{:S(2)}) async-start(bf16[64,144,128]{2,1,0:T(8,128)(2,1)} %constant_dynamic-update-slice_fusion), calls=%async_computation.1 | async-start | bytes 4718592 | tf_op jit(solution)/shard_map/all_to_all | solution.py:150
  135.4 0.2 fusion.48
  135.7 0.8 copy-done
  136.8 1.3 constant_dynamic-slice_fusion.1
  138.1 1.9 convolution_divide_fusion
  140.0 100.9 %all-to-all-done.1 = bf16[64,144,128]{2,1,0:T(8,128)(2,1)S(1)} async-done(((bf16[64,144,128]{2,1,0:T(8,128)(2,1)}), bf16[64,144,128]{2,1,0:T(8,128)(2,1)S(1)}, u32[]{:S(2)}, u32[]{:S(2)}) %all-to-all-start.1) | async-done | bytes 2359328 | tf_op jit(solution)/shard_map/all_to_all | solution.py:150
  241.7 0.3 slice.28
  242.0 0.4 copy-done.5
  242.4 1.2 fusion.6
  244.1 14.0 %all_gather.6 = bf16[256,1024]{1,0:T(8,128)(2,1)S(1)} all-gather(bf16[256,256]{1,0:T(8,128)(2,1)S(1)} %bitcast.91), channel_id=1, replica_groups=mesh['ctx'=64,'y'=4,'zh'=2] {'y'}, dimensions={1}, use_global_device_ids=true | all-gather | bytes 655360 | tf_op jit(solution)/shard_map/all_gather | solution.py:174
  258.1 8.2 %collective-permute-start = (bf16[256,256]{1,0:T(8,128)(2,1)S(1)}, bf16[256,256]{1,0:T(8,128)(2,1)S(1)}, u32[]{:S(2)}, u32[]{:S(2)}) collective-permute-start(bf16[256,256]{1,0:T(8,128)(2,1)S(1)} %bitcast.92), channel_id=1, source_target_pairs={{0,1},{1,0},{2,3},{3,2},{4,5},{5,4},{6,7},{7,6},{8,9},{9,8},{10,11... | collective-permute-start | bytes 393224 | tf_op jit(solution)/shard_map/ppermute | solution.py:175
  266.3 0.3 fusion.49
  266.6 14.0 %collective-permute-done = bf16[256,256]{1,0:T(8,128)(2,1)S(1)} collective-permute-done((bf16[256,256]{1,0:T(8,128)(2,1)S(1)}, bf16[256,256]{1,0:T(8,128)(2,1)S(1)}, u32[]{:S(2)}, u32[]{:S(2)}) %collective-permute-start) | collective-permute-done | bytes 131104 | tf_op jit(solution)/shard_map/ppermute | solution.py:175
  280.6 12.8 %all_gather.7 = bf16[256,1024]{1,0:T(8,128)(2,1)S(1)} all-gather(bf16[256,256]{1,0:T(8,128)(2,1)S(1)} %collective-permute-done), channel_id=1, replica_groups=mesh['ctx'=64,'y'=4,'zh'=2] {'y'}, dimensions={1}, use_global_device_ids=true | all-gather | bytes 655360 | tf_op jit(solution)/shard_map/all_gather | solution.py:176
  293.4 1.0 fusion.9
  (46 shorter events, 2.6 us)
Async XLA Ops:
  1.3 239.6 %copy-start.4 = (s32[2,8,2]{1,2,0:T(2,128)}, s32[2,8,2]{1,2,0:T(2,128)S(1)}, u32[]{:S(2)}) copy-start(s32[2,8,2]{1,2,0:T(2,128)S(1)} %copy.41) | copy-start | bytes 388
  125.5 10.0 %copy-start.3 = (bf16[256,256]{1,0:T(8,128)(2,1)S(1)}, bf16[256,256]{1,0:T(8,128)(2,1)}, u32[]{:S(2)}) copy-start(bf16[256,256]{1,0:T(8,128)(2,1)} %param.5) | copy-start | bytes 393220
  125.5 10.0 %copy-start.6 = (bf16[256,256]{1,0:T(8,128)(2,1)S(1)}, bf16[256,256]{1,0:T(8,128)(2,1)}, u32[]{:S(2)}) copy-start(bf16[256,256]{1,0:T(8,128)(2,1)} %k_ref.1) | copy-start | bytes 393220
  125.5 115.5 %all-to-all-start.1 = ((bf16[64,144,128]{2,1,0:T(8,128)(2,1)}), bf16[64,144,128]{2,1,0:T(8,128)(2,1)S(1)}, u32[]{:S(2)}, u32[]{:S(2)}) async-start(bf16[64,144,128]{2,1,0:T(8,128)(2,1)} %constant_dynamic-update-slice_fusion), calls=%async_computation.1 | async-start | bytes 4718592 | tf_op jit(solution)/shard_map/all_to_all | solution.py:150
  135.7 0.8 copy-start
  136.8 1.4 copy-start.1
  241.7 0.7 copy-start.5
  242.0 1.6 copy-start.2
  258.1 22.6 %collective-permute-start = (bf16[256,256]{1,0:T(8,128)(2,1)S(1)}, bf16[256,256]{1,0:T(8,128)(2,1)S(1)}, u32[]{:S(2)}, u32[]{:S(2)}) collective-permute-start(bf16[256,256]{1,0:T(8,128)(2,1)S(1)} %bitcast.92), channel_id=1, source_target_pairs={{0,1},{1,0},{2,3},{3,2},{4,5},{5,4},{6,7},{7,6},{8,9},{9,8},{10,11... | collective-permute-start | bytes 393224 | tf_op jit(solution)/shard_map/ppermute | solution.py:175

commit v12 on v11

--- a/solution.py
+++ b/solution.py
@@ -171,17 +171,17 @@
     attention = attention.astype(jnp.bfloat16)
     pair = lax.axis_size("zh")
     mine_zh = lax.axis_index("zh")
-    own_rows = lax.all_gather(attention, "y", axis=1, tiled=True)
+    ring = lax.axis_size("y")
     partner = lax.ppermute(attention, "zh", [(0, 1), (1, 0)])
-    partner_rows = lax.all_gather(partner, "y", axis=1, tiled=True)
-    groups = out_weight.reshape(-1, pair, heads_loc * width, out_weight.shape[1])
+    both = jnp.stack([attention, partner])
+    spread = jnp.broadcast_to(both[None], (ring,) + both.shape)
+    got_both = lax.all_to_all(spread, "y", split_axis=0, concat_axis=0, tiled=True)
+    groups = out_weight.reshape(ring, pair, heads_loc * width, out_weight.shape[1])
     own_w = lax.dynamic_index_in_dim(groups, mine_zh, axis=1, keepdims=False)
     partner_w = lax.dynamic_index_in_dim(groups, 1 - mine_zh, axis=1, keepdims=False)
-    projected = jnp.dot(
-        own_rows, own_w.reshape(-1, out_weight.shape[1]), preferred_element_type=jnp.float32
-    ) + jnp.dot(
-        partner_rows, partner_w.reshape(-1, out_weight.shape[1]), preferred_element_type=jnp.float32
-    )
+    projected = jnp.einsum(
+        "yrc,ycn->rn", got_both[:, 0], own_w, preferred_element_type=jnp.float32
+    ) + jnp.einsum("yrc,ycn->rn", got_both[:, 1], partner_w, preferred_element_type=jnp.float32)
     return projected.astype(jnp.bfloat16)
 
 

time: 295 us -> 293 us (level)
  blocking collectives: 138 us -> 111 us
  waiting for transfers between devices: 115 us -> 132 us
  starting transfers between devices: 18.1 us -> 22.6 us
    all_gather x2 -> x0, blocking collectives: 26.8 us -> none  [the longest x1 14 us: local(): own_rows = lax.all_gather(attention, 'y', axis=1, tiled=True)]
    all_to_all x0 -> x1, waiting for transfers between devices: none -> 15.7 us  [local(): lax.all_to_all(spread, 'y', split_axis=0, concat_axis=0, tiled=True)]
    all_to_all x0 -> x1, starting transfers between devices: none -> 4.47 us  [local(): lax.all_to_all(spread, 'y', split_axis=0, concat_axis=0, tiled=True)]
  transfers between devices with their start and end apart: 2 -> 3, of which waited for: 2 -> 3; matrix products, arithmetic and copies ran while one was open for 1% -> 2% of each run, Pallas kernels for 0% -> 0%
where the time goes in v12:
time: 293 us; the launch traced here: 292 us
  waiting for transfers between devices  132 us (45%)
  blocking collectives  111 us (38%)
  starting transfers between devices  22.6 us (8%)
  local copies, waits for them, and re-layouts  8.94 us (3%)
  Pallas kernels  8.65 us (3%)
  matrix products  6.69 us (2%)
    all_to_all x1, blocking collectives, local(): lax.all_to_all(send_q, 'ctx', split_axis=0, concat_axis=0, tiled=True)  111 us
    all_to_all x1, waiting for transfers between devices, local(): lax.all_to_all(back, 'ctx', split_axis=0, concat_axis=0, tiled=True)  99.9 us
    ppermute x1, waiting for transfers between devices, local(): partner = lax.ppermute(attention, 'zh', [(0, 1), (1, 0)])  16.5 us
    all_to_all x1, waiting for transfers between devices, local(): lax.all_to_all(spread, 'y', split_axis=0, concat_axis=0, tiled=True)  15.7 us
    all_to_all x1, starting transfers between devices, local(): lax.all_to_all(back, 'ctx', split_axis=0, concat_axis=0, tiled=True)  9.91 us
    pallas_call x1, Pallas kernels, owner_attention(): pl.pallas_call(functools.partial(owner_kernel, scale), grid=(sources // s...  8.65 us
    ppermute x1, starting transfers between devices, local(): partner = lax.ppermute(attention, 'zh', [(0, 1), (1, 0)])  8.22 us
  transfers between devices with their start and end apart: 3, of which 3 were waited for; matrix products, arithmetic and copies ran while one was open for 2% of the time, Pallas kernels for 0%

profile of v12, /device:TPU:6, one launch (start us, length us, event | category | flops | bytes accessed | tf_op | source)
XLA Modules:
  0.0 292.2 jit_solution(12358873538184799901)
XLA Ops:
  0.0 0.8 slice.24
  1.5 1.0 reshape_reshape.3
  2.5 0.7 convolution_convert_fusion
  3.2 0.5 copy.86
  3.7 0.6 copy.47
  4.3 110.7 %all_to_all.15 = bf16[64,2,2,32,128]{4,3,2,1,0:T(8,128)(2,1)} all-to-all(bf16[64,2,2,32,128]{4,3,2,1,0:T(8,128)(2,1)S(1)} %copy.47), channel_id=1, replica_groups=mesh['ctx'=64,'y'=4,'zh'=2] {'ctx'}, dimensions={0} | all-to-all | bytes 4194304 | tf_op jit(solution)/shard_map/all_to_all | solution.py:135
  115.0 8.7 %shard_map.55 = (bf16[64,144,128]{2,1,0:T(8,128)(2,1)}, f32[4,2048]{1,0:T(4,128)}) custom-call(bf16[64,4,32,128]{3,2,1,0:T(8,128)(2,1)} %bitcast.111, bf16[256,256]{1,0:T(8,128)(2,1)} %k_ref.1, bf16[256,256]{1,0:T(8,128)(2,1)} %v_ref.1), custom_call_target="tpu_custom_call" | custom-call | flops 1610612736 | bytes 4227072 | tf_op jit(solution)/shard_map/pallas_call | solution.py:70
  123.6 0.9 reshape.187
  124.9 0.7 constant_dynamic-update-slice_fusion
  125.6 9.9 %all-to-all-start.1 = ((bf16[64,144,128]{2,1,0:T(8,128)(2,1)}), bf16[64,144,128]{2,1,0:T(8,128)(2,1)S(1)}, u32[]{:S(2)}, u32[]{:S(2)}) async-start(bf16[64,144,128]{2,1,0:T(8,128)(2,1)} %constant_dynamic-update-slice_fusion), calls=%async_computation.1 | async-start | bytes 4718592 | tf_op jit(solution)/shard_map/all_to_all | solution.py:150
  135.5 0.6 broadcast_compare_fusion
  136.1 0.8 copy.44
  136.9 1.2 fusion.55
  138.0 0.8 copy-done.1
  139.0 2.1 convolution_divide_fusion
  141.1 99.9 %all-to-all-done.1 = bf16[64,144,128]{2,1,0:T(8,128)(2,1)S(1)} async-done(((bf16[64,144,128]{2,1,0:T(8,128)(2,1)}), bf16[64,144,128]{2,1,0:T(8,128)(2,1)S(1)}, u32[]{:S(2)}, u32[]{:S(2)}) %all-to-all-start.1) | async-done | bytes 2359328 | tf_op jit(solution)/shard_map/all_to_all | solution.py:150
  241.5 0.8 fusion.52
  243.2 1.3 fusion.6
  244.9 8.2 %collective-permute-start = (bf16[256,256]{1,0:T(8,128)(2,1)S(1)}, bf16[256,256]{1,0:T(8,128)(2,1)S(1)}, u32[]{:S(2)}, u32[]{:S(2)}) collective-permute-start(bf16[256,256]{1,0:T(8,128)(2,1)S(1)} %bitcast.123), channel_id=1, source_target_pairs={{0,1},{1,0},{2,3},{3,2},{4,5},{5,4},{6,7},{7,6},{8,9},{9,8},{10,11... | collective-permute-start | bytes 393224 | tf_op jit(solution)/shard_map/ppermute | solution.py:175
  253.2 16.5 %collective-permute-done = bf16[256,256]{1,0:T(8,128)(2,1)S(1)} collective-permute-done((bf16[256,256]{1,0:T(8,128)(2,1)S(1)}, bf16[256,256]{1,0:T(8,128)(2,1)S(1)}, u32[]{:S(2)}, u32[]{:S(2)}) %collective-permute-start) | collective-permute-done | bytes 131104 | tf_op jit(solution)/shard_map/ppermute | solution.py:175
  269.7 1.1 broadcast_in_dim.69
  270.7 4.5 %all-to-all-start.2 = ((bf16[4,2,256,256]{3,2,1,0:T(8,128)(2,1)}), bf16[4,2,256,256]{3,2,1,0:T(8,128)(2,1)S(1)}, u32[]{:S(2)}, u32[]{:S(2)}) async-start(bf16[4,2,256,256]{3,2,1,0:T(8,128)(2,1)} %broadcast_in_dim.69), calls=%async_computation.2 | async-start | bytes 2097152 | tf_op jit(solution)/shard_map/all_to_all | solution.py:178
  275.2 15.7 %all-to-all-done.2 = bf16[4,2,256,256]{3,2,1,0:T(8,128)(2,1)S(1)} async-done(((bf16[4,2,256,256]{3,2,1,0:T(8,128)(2,1)}), bf16[4,2,256,256]{3,2,1,0:T(8,128)(2,1)S(1)}, u32[]{:S(2)}, u32[]{:S(2)}) %all-to-all-start.2) | async-done | bytes 1048608 | tf_op jit(solution)/shard_map/all_to_all | solution.py:178
  291.3 1.0 fusion.10
  (48 shorter events, 3.4 us)
Async XLA Ops:
  0.0 290.9 %copy-start = (bf16[2048,256]{1,0:T(8,128)(2,1)S(1)}, bf16[2048,256]{1,0:T(8,128)(2,1)}, u32[]{:S(2)}) copy-start(bf16[2048,256]{1,0:T(8,128)(2,1)} %param.9) | copy-start | bytes 3145732
  1.4 239.6 %copy-start.5 = (s32[2,8,2]{1,2,0:T(2,128)}, s32[2,8,2]{1,2,0:T(2,128)S(1)}, u32[]{:S(2)}) copy-start(s32[2,8,2]{1,2,0:T(2,128)S(1)} %copy.45) | copy-start | bytes 388
  125.6 11.3 %copy-start.3 = (bf16[256,256]{1,0:T(8,128)(2,1)S(1)}, bf16[256,256]{1,0:T(8,128)(2,1)}, u32[]{:S(2)}) copy-start(bf16[256,256]{1,0:T(8,128)(2,1)} %param.5) | copy-start | bytes 393220
  125.6 115.5 %all-to-all-start.1 = ((bf16[64,144,128]{2,1,0:T(8,128)(2,1)}), bf16[64,144,128]{2,1,0:T(8,128)(2,1)S(1)}, u32[]{:S(2)}, u32[]{:S(2)}) async-start(bf16[64,144,128]{2,1,0:T(8,128)(2,1)} %constant_dynamic-update-slice_fusion), calls=%async_computation.1 | async-start | bytes 4718592 | tf_op jit(solution)/shard_map/all_to_all | solution.py:150
  136.8 104.6 %copy-start.4 = (pred[2,8,2]{1,2,0:T(4,128)(4,1)}, pred[2,8,2]{1,2,0:T(4,128)(4,1)S(1)}, u32[]{:S(2)}) copy-start(pred[2,8,2]{1,2,0:T(4,128)(4,1)S(1)} %copy.44) | copy-start | bytes 100
  138.0 0.8 copy-start.1
  242.5 0.7 copy-start.6
  242.8 1.7 copy-start.2
  244.9 24.8 %collective-permute-start = (bf16[256,256]{1,0:T(8,128)(2,1)S(1)}, bf16[256,256]{1,0:T(8,128)(2,1)S(1)}, u32[]{:S(2)}, u32[]{:S(2)}) collective-permute-start(bf16[256,256]{1,0:T(8,128)(2,1)S(1)} %bitcast.123), channel_id=1, source_target_pairs={{0,1},{1,0},{2,3},{3,2},{4,5},{5,4},{6,7},{7,6},{8,9},{9,8},{10,11... | collective-permute-start | bytes 393224 | tf_op jit(solution)/shard_map/ppermute | solution.py:175
  270.7 20.2 %all-to-all-start.2 = ((bf16[4,2,256,256]{3,2,1,0:T(8,128)(2,1)}), bf16[4,2,256,256]{3,2,1,0:T(8,128)(2,1)S(1)}, u32[]{:S(2)}, u32[]{:S(2)}) async-start(bf16[4,2,256,256]{3,2,1,0:T(8,128)(2,1)} %broadcast_in_dim.69), calls=%async_computation.2 | async-start | bytes 2097152 | tf_op jit(solution)/shard_map/all_to_all | solution.py:178

commit v13 on v12

--- a/solution.py
+++ b/solution.py
@@ -173,15 +173,26 @@
     mine_zh = lax.axis_index("zh")
     ring = lax.axis_size("y")
     partner = lax.ppermute(attention, "zh", [(0, 1), (1, 0)])
-    both = jnp.stack([attention, partner])
-    spread = jnp.broadcast_to(both[None], (ring,) + both.shape)
-    got_both = lax.all_to_all(spread, "y", split_axis=0, concat_axis=0, tiled=True)
+    got_own = lax.all_to_all(
+        jnp.broadcast_to(attention[None], (ring,) + attention.shape),
+        "y",
+        split_axis=0,
+        concat_axis=0,
+        tiled=True,
+    )
+    got_partner = lax.all_to_all(
+        jnp.broadcast_to(partner[None], (ring,) + partner.shape),
+        "y",
+        split_axis=0,
+        concat_axis=0,
+        tiled=True,
+    )
     groups = out_weight.reshape(ring, pair, heads_loc * width, out_weight.shape[1])
     own_w = lax.dynamic_index_in_dim(groups, mine_zh, axis=1, keepdims=False)
     partner_w = lax.dynamic_index_in_dim(groups, 1 - mine_zh, axis=1, keepdims=False)
     projected = jnp.einsum(
-        "yrc,ycn->rn", got_both[:, 0], own_w, preferred_element_type=jnp.float32
-    ) + jnp.einsum("yrc,ycn->rn", got_both[:, 1], partner_w, preferred_element_type=jnp.float32)
+        "yrc,ycn->rn", got_own, own_w, preferred_element_type=jnp.float32
+    ) + jnp.einsum("yrc,ycn->rn", got_partner, partner_w, preferred_element_type=jnp.float32)
     return projected.astype(jnp.bfloat16)
 
 

time: 293 us -> 292 us (level)
  waiting for transfers between devices: 132 us -> 126 us
  starting transfers between devices: 22.6 us -> 27.7 us
    all_to_all x1 -> x2, waiting for transfers between devices: 15.7 us -> 9.4 us  [the longest x1 9.4 us: local(): lax.all_to_all(jnp.broadcast_to(partner[None], (ring,) + partner.shape),...]
    all_to_all x1 -> x2, starting transfers between devices: 4.47 us -> 9.54 us  [the longest x1 5.08 us: local(): lax.all_to_all(jnp.broadcast_to(partner[None], (ring,) + partner.shape),...]
  transfers between devices with their start and end apart: 3 -> 4, of which waited for: 3 -> 3; matrix products, arithmetic and copies ran while one was open for 2% -> 2% of each run, Pallas kernels for 0% -> 0%
where the time goes in v13:
time: 292 us
  waiting for transfers between devices  126 us (43%)
  blocking collectives  111 us (38%)
  starting transfers between devices  27.7 us (9%)
  local copies, waits for them, and re-layouts  9.44 us (3%)
  Pallas kernels  8.65 us (3%)
  matrix products  6.68 us (2%)
    all_to_all x1, blocking collectives, local(): lax.all_to_all(send_q, 'ctx', split_axis=0, concat_axis=0, tiled=True)  111 us
    all_to_all x1, waiting for transfers between devices, local(): lax.all_to_all(back, 'ctx', split_axis=0, concat_axis=0, tiled=True)  99.9 us
    ppermute x1, waiting for transfers between devices, local(): partner = lax.ppermute(attention, 'zh', [(0, 1), (1, 0)])  16.8 us
    all_to_all x1, starting transfers between devices, local(): lax.all_to_all(back, 'ctx', split_axis=0, concat_axis=0, tiled=True)  9.91 us
    all_to_all x1, waiting for transfers between devices, local(): lax.all_to_all(jnp.broadcast_to(partner[None], (ring,) + partner.shape),...  9.4 us
    pallas_call x1, Pallas kernels, owner_attention(): pl.pallas_call(functools.partial(owner_kernel, scale), grid=(sources // s...  8.65 us
    ppermute x1, starting transfers between devices, local(): partner = lax.ppermute(attention, 'zh', [(0, 1), (1, 0)])  8.21 us
  transfers between devices with their start and end apart: 4, of which 3 were waited for; matrix products, arithmetic and copies ran while one was open for 2% of the time, Pallas kernels for 0%

profile of v13, /device:TPU:6, one launch (start us, length us, event | category | flops | bytes accessed | tf_op | source)
XLA Modules:
  0.0 291.8 jit_solution(16745069336023234962)
XLA Ops:
  0.0 0.8 slice.18
  1.5 1.0 reshape_reshape.3
  2.5 0.7 convolution_convert_fusion
  4.3 110.7 %all_to_all.20 = bf16[64,2,2,32,128]{4,3,2,1,0:T(8,128)(2,1)} all-to-all(bf16[64,2,2,32,128]{4,3,2,1,0:T(8,128)(2,1)S(1)} %copy.47), channel_id=1, replica_groups=mesh['ctx'=64,'y'=4,'zh'=2] {'ctx'}, dimensions={0} | all-to-all | bytes 4194304 | tf_op jit(solution)/shard_map/all_to_all | solution.py:135
  115.0 8.7 %shard_map.55 = (bf16[64,144,128]{2,1,0:T(8,128)(2,1)}, f32[4,2048]{1,0:T(4,128)}) custom-call(bf16[64,4,32,128]{3,2,1,0:T(8,128)(2,1)} %bitcast.102, bf16[256,256]{1,0:T(8,128)(2,1)} %k_ref.1, bf16[256,256]{1,0:T(8,128)(2,1)} %v_ref.1), custom_call_target="tpu_custom_call" | custom-call | flops 1610612736 | bytes 4227072 | tf_op jit(solution)/shard_map/pallas_call | solution.py:70
  123.6 0.9 reshape.181
  124.9 0.7 constant_dynamic-update-slice_fusion
  125.6 9.9 %all-to-all-start.1 = ((bf16[64,144,128]{2,1,0:T(8,128)(2,1)}), bf16[64,144,128]{2,1,0:T(8,128)(2,1)S(1)}, u32[]{:S(2)}, u32[]{:S(2)}) async-start(bf16[64,144,128]{2,1,0:T(8,128)(2,1)} %constant_dynamic-update-slice_fusion), calls=%async_computation.1 | async-start | bytes 4718592 | tf_op jit(solution)/shard_map/all_to_all | solution.py:150
  135.5 0.6 broadcast_compare_fusion
  136.1 0.8 copy.44
  136.9 1.1 fusion.55
  138.0 0.8 copy-done.1
  139.0 2.1 convolution_divide_fusion
  141.1 99.9 %all-to-all-done.1 = bf16[64,144,128]{2,1,0:T(8,128)(2,1)S(1)} async-done(((bf16[64,144,128]{2,1,0:T(8,128)(2,1)}), bf16[64,144,128]{2,1,0:T(8,128)(2,1)S(1)}, u32[]{:S(2)}, u32[]{:S(2)}) %all-to-all-start.1) | async-done | bytes 2359328 | tf_op jit(solution)/shard_map/all_to_all | solution.py:150
  241.5 0.8 fusion.52
  243.2 1.3 fusion.6
  244.9 0.8 broadcast_in_dim.52
  245.7 4.5 %all-to-all-start.2 = ((bf16[4,256,256]{2,1,0:T(8,128)(2,1)}), bf16[4,256,256]{2,1,0:T(8,128)(2,1)S(1)}, u32[]{:S(2)}, u32[]{:S(2)}) async-start(bf16[4,256,256]{2,1,0:T(8,128)(2,1)} %broadcast_in_dim.52), calls=%async_computation.2 | async-start | bytes 1048576 | tf_op jit(solution)/shard_map/all_to_all | solution.py:176
  250.1 8.2 %collective-permute-start = (bf16[256,256]{1,0:T(8,128)(2,1)S(1)}, bf16[256,256]{1,0:T(8,128)(2,1)S(1)}, u32[]{:S(2)}, u32[]{:S(2)}) collective-permute-start(bf16[256,256]{1,0:T(8,128)(2,1)S(1)} %bitcast.105), channel_id=1, source_target_pairs={{0,1},{1,0},{2,3},{3,2},{4,5},{5,4},{6,7},{7,6},{8,9},{9,8},{10,11... | collective-permute-start | bytes 393224 | tf_op jit(solution)/shard_map/ppermute | solution.py:175
  258.4 16.8 %collective-permute-done = bf16[256,256]{1,0:T(8,128)(2,1)S(1)} collective-permute-done((bf16[256,256]{1,0:T(8,128)(2,1)S(1)}, bf16[256,256]{1,0:T(8,128)(2,1)S(1)}, u32[]{:S(2)}, u32[]{:S(2)}) %collective-permute-start) | collective-permute-done | bytes 131104 | tf_op jit(solution)/shard_map/ppermute | solution.py:175
  275.2 0.8 broadcast_in_dim.76
  276.0 5.1 %all-to-all-start.3 = ((bf16[4,256,256]{2,1,0:T(8,128)(2,1)}), bf16[4,256,256]{2,1,0:T(8,128)(2,1)S(1)}, u32[]{:S(2)}, u32[]{:S(2)}) async-start(bf16[4,256,256]{2,1,0:T(8,128)(2,1)} %broadcast_in_dim.76), calls=%async_computation.3 | async-start | bytes 1048576 | tf_op jit(solution)/shard_map/all_to_all | solution.py:183
  281.4 9.4 %all-to-all-done.3 = bf16[4,256,256]{2,1,0:T(8,128)(2,1)S(1)} async-done(((bf16[4,256,256]{2,1,0:T(8,128)(2,1)}), bf16[4,256,256]{2,1,0:T(8,128)(2,1)S(1)}, u32[]{:S(2)}, u32[]{:S(2)}) %all-to-all-start.3) | async-done | bytes 524320 | tf_op jit(solution)/shard_map/all_to_all | solution.py:183
  290.8 1.0 fusion.10
  (49 shorter events, 4.4 us)
Async XLA Ops:
  0.0 281.1 %copy-start = (bf16[2048,256]{1,0:T(8,128)(2,1)S(1)}, bf16[2048,256]{1,0:T(8,128)(2,1)}, u32[]{:S(2)}) copy-start(bf16[2048,256]{1,0:T(8,128)(2,1)} %param.9) | copy-start | bytes 3145732
  1.4 239.6 %copy-start.5 = (s32[2,8,2]{1,2,0:T(2,128)}, s32[2,8,2]{1,2,0:T(2,128)S(1)}, u32[]{:S(2)}) copy-start(s32[2,8,2]{1,2,0:T(2,128)S(1)} %copy.45) | copy-start | bytes 388
  125.6 11.3 %copy-start.3 = (bf16[256,256]{1,0:T(8,128)(2,1)S(1)}, bf16[256,256]{1,0:T(8,128)(2,1)}, u32[]{:S(2)}) copy-start(bf16[256,256]{1,0:T(8,128)(2,1)} %param.5) | copy-start | bytes 393220
  125.6 115.5 %all-to-all-start.1 = ((bf16[64,144,128]{2,1,0:T(8,128)(2,1)}), bf16[64,144,128]{2,1,0:T(8,128)(2,1)S(1)}, u32[]{:S(2)}, u32[]{:S(2)}) async-start(bf16[64,144,128]{2,1,0:T(8,128)(2,1)} %constant_dynamic-update-slice_fusion), calls=%async_computation.1 | async-start | bytes 4718592 | tf_op jit(solution)/shard_map/all_to_all | solution.py:150
  136.8 104.6 %copy-start.4 = (pred[2,8,2]{1,2,0:T(4,128)(4,1)}, pred[2,8,2]{1,2,0:T(4,128)(4,1)S(1)}, u32[]{:S(2)}) copy-start(pred[2,8,2]{1,2,0:T(4,128)(4,1)S(1)} %copy.44) | copy-start | bytes 100
  138.0 0.8 copy-start.1
  242.5 0.7 copy-start.6
  242.8 1.7 copy-start.2
  245.7 29.5 %all-to-all-start.2 = ((bf16[4,256,256]{2,1,0:T(8,128)(2,1)}), bf16[4,256,256]{2,1,0:T(8,128)(2,1)S(1)}, u32[]{:S(2)}, u32[]{:S(2)}) async-start(bf16[4,256,256]{2,1,0:T(8,128)(2,1)} %broadcast_in_dim.52), calls=%async_computation.2 | async-start | bytes 1048576 | tf_op jit(solution)/shard_map/all_to_all | solution.py:176
  250.1 25.1 %collective-permute-start = (bf16[256,256]{1,0:T(8,128)(2,1)S(1)}, bf16[256,256]{1,0:T(8,128)(2,1)S(1)}, u32[]{:S(2)}, u32[]{:S(2)}) collective-permute-start(bf16[256,256]{1,0:T(8,128)(2,1)S(1)} %bitcast.105), channel_id=1, source_target_pairs={{0,1},{1,0},{2,3},{3,2},{4,5},{5,4},{6,7},{7,6},{8,9},{9,8},{10,11... | collective-permute-start | bytes 393224 | tf_op jit(solution)/shard_map/ppermute | solution.py:175
  276.0 14.8 %all-to-all-start.3 = ((bf16[4,256,256]{2,1,0:T(8,128)(2,1)}), bf16[4,256,256]{2,1,0:T(8,128)(2,1)S(1)}, u32[]{:S(2)}, u32[]{:S(2)}) async-start(bf16[4,256,256]{2,1,0:T(8,128)(2,1)} %broadcast_in_dim.76), calls=%async_computation.3 | async-start | bytes 1048576 | tf_op jit(solution)/shard_map/all_to_all | solution.py:183

commit v14 on v12

--- a/solution.py
+++ b/solution.py
@@ -170,18 +170,27 @@
     )
     attention = attention.astype(jnp.bfloat16)
     pair = lax.axis_size("zh")
-    mine_zh = lax.axis_index("zh")
     ring = lax.axis_size("y")
-    partner = lax.ppermute(attention, "zh", [(0, 1), (1, 0)])
-    both = jnp.stack([attention, partner])
-    spread = jnp.broadcast_to(both[None], (ring,) + both.shape)
-    got_both = lax.all_to_all(spread, "y", split_axis=0, concat_axis=0, tiled=True)
-    groups = out_weight.reshape(ring, pair, heads_loc * width, out_weight.shape[1])
-    own_w = lax.dynamic_index_in_dim(groups, mine_zh, axis=1, keepdims=False)
-    partner_w = lax.dynamic_index_in_dim(groups, 1 - mine_zh, axis=1, keepdims=False)
+    both = lax.all_to_all(
+        jnp.broadcast_to(attention[None], (pair,) + attention.shape),
+        "zh",
+        split_axis=0,
+        concat_axis=0,
+        tiled=True,
+    )
+    every = lax.all_to_all(
+        jnp.broadcast_to(both[None], (ring,) + both.shape),
+        "y",
+        split_axis=0,
+        concat_axis=0,
+        tiled=True,
+    )
     projected = jnp.einsum(
-        "yrc,ycn->rn", got_both[:, 0], own_w, preferred_element_type=jnp.float32
-    ) + jnp.einsum("yrc,ycn->rn", got_both[:, 1], partner_w, preferred_element_type=jnp.float32)
+        "yzrc,yzcn->rn",
+        every,
+        out_weight.reshape(ring, pair, heads_loc * width, out_weight.shape[1]),
+        preferred_element_type=jnp.float32,
+    )
     return projected.astype(jnp.bfloat16)
 
 

time: 293 us -> 293 us (level); the launches traced: 292 us -> 287 us
  blocking collectives: 111 us -> 152 us
  waiting for transfers between devices: 132 us -> 99.9 us
  starting transfers between devices: 22.6 us -> 9.91 us
    all_to_all x0 -> x2, blocking collectives: none -> 41.1 us  [the longest x1 22.4 us: local(): lax.all_to_all(jnp.broadcast_to(attention[None], (pair,) + attention.shap...]
    ppermute x1 -> x0, waiting for transfers between devices: 16.5 us -> none  [local(): partner = lax.ppermute(attention, 'zh', [(0, 1), (1, 0)])]
    all_to_all x1 -> x0, waiting for transfers between devices: 15.7 us -> none  [local(): lax.all_to_all(spread, 'y', split_axis=0, concat_axis=0, tiled=True)]
    ppermute x1 -> x0, starting transfers between devices: 8.22 us -> none  [local(): partner = lax.ppermute(attention, 'zh', [(0, 1), (1, 0)])]
    all_to_all x1 -> x0, starting transfers between devices: 4.47 us -> none  [local(): lax.all_to_all(spread, 'y', split_axis=0, concat_axis=0, tiled=True)]
  transfers between devices with their start and end apart: 3 -> 1, of which waited for: 3 -> 1; matrix products, arithmetic and copies ran while one was open for 2% -> 2% of each run, Pallas kernels for 0% -> 0%
where the time goes in v14:
time: 293 us; the launch traced here: 287 us
  blocking collectives  152 us (52%)
  waiting for transfers between devices  99.9 us (34%)
  starting transfers between devices  9.91 us (3%)
  Pallas kernels  8.65 us (3%)
  local copies, waits for them, and re-layouts  7.88 us (3%)
  matrix products  6.52 us (2%)
    all_to_all x1, blocking collectives, local(): lax.all_to_all(send_q, 'ctx', split_axis=0, concat_axis=0, tiled=True)  111 us
    all_to_all x1, waiting for transfers between devices, local(): lax.all_to_all(back, 'ctx', split_axis=0, concat_axis=0, tiled=True)  99.9 us
    all_to_all x1, blocking collectives, local(): lax.all_to_all(jnp.broadcast_to(attention[None], (pair,) + attention.shap...  22.4 us
    all_to_all x1, blocking collectives, local(): lax.all_to_all(jnp.broadcast_to(both[None], (ring,) + both.shape), 'y', s...  18.7 us
    all_to_all x1, starting transfers between devices, local(): lax.all_to_all(back, 'ctx', split_axis=0, concat_axis=0, tiled=True)  9.91 us
    pallas_call x1, Pallas kernels, owner_attention(): pl.pallas_call(functools.partial(owner_kernel, scale), grid=(sources // s...  8.65 us
  transfers between devices with their start and end apart: 1, of which 1 were waited for; matrix products, arithmetic and copies ran while one was open for 2% of the time, Pallas kernels for 0%

profile of v14, /device:TPU:6, one launch (start us, length us, event | category | flops | bytes accessed | tf_op | source)
XLA Modules:
  0.0 287.2 jit_solution(10051887341561363886)
XLA Ops:
  0.0 0.8 slice.18
  1.5 1.0 reshape_reshape.3
  2.5 0.7 convolution_convert_fusion
  3.2 0.5 copy.74
  3.7 0.6 copy.43
  4.3 110.7 %all_to_all.20 = bf16[64,2,2,32,128]{4,3,2,1,0:T(8,128)(2,1)} all-to-all(bf16[64,2,2,32,128]{4,3,2,1,0:T(8,128)(2,1)S(1)} %copy.43), channel_id=1, replica_groups=mesh['ctx'=64,'y'=4,'zh'=2] {'ctx'}, dimensions={0} | all-to-all | bytes 4194304 | tf_op jit(solution)/shard_map/all_to_all | solution.py:135
  115.0 8.7 %shard_map.55 = (bf16[64,144,128]{2,1,0:T(8,128)(2,1)}, f32[4,2048]{1,0:T(4,128)}) custom-call(bf16[64,4,32,128]{3,2,1,0:T(8,128)(2,1)} %bitcast.89, bf16[256,256]{1,0:T(8,128)(2,1)} %k_ref.1, bf16[256,256]{1,0:T(8,128)(2,1)} %v_ref.1), custom_call_target="tpu_custom_call" | custom-call | flops 1610612736 | bytes 4227072 | tf_op jit(solution)/shard_map/pallas_call | solution.py:70
  123.6 0.9 reshape.181
  124.9 0.7 constant_dynamic-update-slice_fusion
  125.6 9.9 %all-to-all-start.1 = ((bf16[64,144,128]{2,1,0:T(8,128)(2,1)}), bf16[64,144,128]{2,1,0:T(8,128)(2,1)S(1)}, u32[]{:S(2)}, u32[]{:S(2)}) async-start(bf16[64,144,128]{2,1,0:T(8,128)(2,1)} %constant_dynamic-update-slice_fusion), calls=%async_computation.1 | async-start | bytes 4718592 | tf_op jit(solution)/shard_map/all_to_all | solution.py:150
  135.5 0.6 broadcast_compare_fusion
  136.1 0.8 copy.40
  136.9 1.2 fusion.48
  138.0 0.8 copy-done.1
  139.0 2.1 convolution_divide_fusion
  141.1 99.9 %all-to-all-done.1 = bf16[64,144,128]{2,1,0:T(8,128)(2,1)S(1)} async-done(((bf16[64,144,128]{2,1,0:T(8,128)(2,1)}), bf16[64,144,128]{2,1,0:T(8,128)(2,1)S(1)}, u32[]{:S(2)}, u32[]{:S(2)}) %all-to-all-start.1) | async-done | bytes 2359328 | tf_op jit(solution)/shard_map/all_to_all | solution.py:150
  241.5 0.8 fusion.45
  242.5 0.3 slice.28
  242.8 0.4 copy-done.6
  243.2 1.3 fusion.6
  244.5 0.2 fusion.32
  244.9 22.4 %all_to_all.21 = bf16[2,256,256]{2,1,0:T(8,128)(2,1)S(1)} all-to-all(bf16[2,256,256]{2,1,0:T(8,128)(2,1)S(1)} %broadcast_in_dim.52), channel_id=1, replica_groups=mesh['ctx'=64,'y'=4,'zh'=2] {'zh'}, dimensions={0} | all-to-all | bytes 524288 | tf_op jit(solution)/shard_map/all_to_all | solution.py:174
  267.4 18.7 %all_to_all.22 = bf16[4,2,256,256]{3,2,1,0:T(8,128)(2,1)S(1)} all-to-all(bf16[4,2,256,256]{3,2,1,0:T(8,128)(2,1)S(1)} %broadcast_in_dim.76), channel_id=1, replica_groups=mesh['ctx'=64,'y'=4,'zh'=2] {'y'}, dimensions={0} | all-to-all | bytes 2097152 | tf_op jit(solution)/shard_map/all_to_all | solution.py:181
  286.1 1.1 fusion.9
  (44 shorter events, 2.2 us)
Async XLA Ops:
  0.0 286.1 %copy-start = (bf16[2048,256]{1,0:T(8,128)(2,1)S(1)}, bf16[2048,256]{1,0:T(8,128)(2,1)}, u32[]{:S(2)}) copy-start(bf16[2048,256]{1,0:T(8,128)(2,1)} %param.9) | copy-start | bytes 3145732
  1.4 239.6 %copy-start.5 = (s32[2,8,2]{1,2,0:T(2,128)}, s32[2,8,2]{1,2,0:T(2,128)S(1)}, u32[]{:S(2)}) copy-start(s32[2,8,2]{1,2,0:T(2,128)S(1)} %copy.41) | copy-start | bytes 388
  125.6 11.3 %copy-start.3 = (bf16[256,256]{1,0:T(8,128)(2,1)S(1)}, bf16[256,256]{1,0:T(8,128)(2,1)}, u32[]{:S(2)}) copy-start(bf16[256,256]{1,0:T(8,128)(2,1)} %param.5) | copy-start | bytes 393220
  125.6 115.5 %all-to-all-start.1 = ((bf16[64,144,128]{2,1,0:T(8,128)(2,1)}), bf16[64,144,128]{2,1,0:T(8,128)(2,1)S(1)}, u32[]{:S(2)}, u32[]{:S(2)}) async-start(bf16[64,144,128]{2,1,0:T(8,128)(2,1)} %constant_dynamic-update-slice_fusion), calls=%async_computation.1 | async-start | bytes 4718592 | tf_op jit(solution)/shard_map/all_to_all | solution.py:150
  136.8 104.6 %copy-start.4 = (pred[2,8,2]{1,2,0:T(4,128)(4,1)}, pred[2,8,2]{1,2,0:T(4,128)(4,1)S(1)}, u32[]{:S(2)}) copy-start(pred[2,8,2]{1,2,0:T(4,128)(4,1)S(1)} %copy.40) | copy-start | bytes 100
  138.0 0.8 copy-start.1
  242.5 0.7 copy-start.6
  242.8 1.7 copy-start.2

commit v15 on v12

--- a/solution.py
+++ b/solution.py
@@ -65,7 +65,7 @@
 
 def owner_attention(got, keys, values, scale, extra):
     sources, slots, rows, width = got.shape
-    step = 16
+    step = 32
     packed = (sources, slots * rows + extra, width)
     return pl.pallas_call(
         functools.partial(owner_kernel, scale),

time: 293 us -> 291 us (level)
  no operation moved by 1% of the time
where the time goes in v15:
time: 291 us
  waiting for transfers between devices  132 us (45%)
  blocking collectives  111 us (38%)
  starting transfers between devices  22.6 us (8%)
  local copies, waits for them, and re-layouts  8.94 us (3%)
  Pallas kernels  7.13 us (2%)
  matrix products  6.69 us (2%)
    all_to_all x1, blocking collectives, local(): lax.all_to_all(send_q, 'ctx', split_axis=0, concat_axis=0, tiled=True)  111 us
    all_to_all x1, waiting for transfers between devices, local(): lax.all_to_all(back, 'ctx', split_axis=0, concat_axis=0, tiled=True)  99.9 us
    ppermute x1, waiting for transfers between devices, local(): partner = lax.ppermute(attention, 'zh', [(0, 1), (1, 0)])  16.5 us
    all_to_all x1, waiting for transfers between devices, local(): lax.all_to_all(spread, 'y', split_axis=0, concat_axis=0, tiled=True)  15.7 us
    all_to_all x1, starting transfers between devices, local(): lax.all_to_all(back, 'ctx', split_axis=0, concat_axis=0, tiled=True)  9.91 us
    ppermute x1, starting transfers between devices, local(): partner = lax.ppermute(attention, 'zh', [(0, 1), (1, 0)])  8.22 us
    pallas_call x1, Pallas kernels, owner_attention(): pl.pallas_call(functools.partial(owner_kernel, scale), grid=(sources // s...  7.13 us
  transfers between devices with their start and end apart: 3, of which 3 were waited for; matrix products, arithmetic and copies ran while one was open for 2% of the time, Pallas kernels for 0%

profile of v15, /device:TPU:6, one launch (start us, length us, event | category | flops | bytes accessed | tf_op | source)
XLA Modules:
  0.0 290.7 jit_solution(16585199136665800317)
XLA Ops:
  0.0 0.8 slice.24
  1.5 1.0 reshape_reshape.3
  2.5 0.7 convolution_convert_fusion
  3.2 0.5 copy.86
  3.7 0.6 copy.47
  4.3 110.7 %all_to_all.15 = bf16[64,2,2,32,128]{4,3,2,1,0:T(8,128)(2,1)} all-to-all(bf16[64,2,2,32,128]{4,3,2,1,0:T(8,128)(2,1)S(1)} %copy.47), channel_id=1, replica_groups=mesh['ctx'=64,'y'=4,'zh'=2] {'ctx'}, dimensions={0} | all-to-all | bytes 4194304 | tf_op jit(solution)/shard_map/all_to_all | solution.py:135
  115.0 7.1 %shard_map.55 = (bf16[64,144,128]{2,1,0:T(8,128)(2,1)}, f32[4,2048]{1,0:T(4,128)}) custom-call(bf16[64,4,32,128]{3,2,1,0:T(8,128)(2,1)} %bitcast.111, bf16[256,256]{1,0:T(8,128)(2,1)} %k_ref.1, bf16[256,256]{1,0:T(8,128)(2,1)} %v_ref.1), custom_call_target="tpu_custom_call" | custom-call | flops 1610612736 | bytes 4227072 | tf_op jit(solution)/shard_map/pallas_call | solution.py:70
  122.1 0.9 reshape.187
  123.4 0.7 constant_dynamic-update-slice_fusion
  124.0 9.9 %all-to-all-start.1 = ((bf16[64,144,128]{2,1,0:T(8,128)(2,1)}), bf16[64,144,128]{2,1,0:T(8,128)(2,1)S(1)}, u32[]{:S(2)}, u32[]{:S(2)}) async-start(bf16[64,144,128]{2,1,0:T(8,128)(2,1)} %constant_dynamic-update-slice_fusion), calls=%async_computation.1 | async-start | bytes 4718592 | tf_op jit(solution)/shard_map/all_to_all | solution.py:150
  133.9 0.6 broadcast_compare_fusion
  134.5 0.8 copy.44
  135.4 1.1 fusion.55
  136.5 0.8 copy-done.1
  137.5 2.1 convolution_divide_fusion
  139.6 99.9 %all-to-all-done.1 = bf16[64,144,128]{2,1,0:T(8,128)(2,1)S(1)} async-done(((bf16[64,144,128]{2,1,0:T(8,128)(2,1)}), bf16[64,144,128]{2,1,0:T(8,128)(2,1)S(1)}, u32[]{:S(2)}, u32[]{:S(2)}) %all-to-all-start.1) | async-done | bytes 2359328 | tf_op jit(solution)/shard_map/all_to_all | solution.py:150
  240.0 0.8 fusion.52
  241.7 1.3 fusion.6
  243.3 8.2 %collective-permute-start = (bf16[256,256]{1,0:T(8,128)(2,1)S(1)}, bf16[256,256]{1,0:T(8,128)(2,1)S(1)}, u32[]{:S(2)}, u32[]{:S(2)}) collective-permute-start(bf16[256,256]{1,0:T(8,128)(2,1)S(1)} %bitcast.123), channel_id=1, source_target_pairs={{0,1},{1,0},{2,3},{3,2},{4,5},{5,4},{6,7},{7,6},{8,9},{9,8},{10,11... | collective-permute-start | bytes 393224 | tf_op jit(solution)/shard_map/ppermute | solution.py:175
  251.7 16.5 %collective-permute-done = bf16[256,256]{1,0:T(8,128)(2,1)S(1)} collective-permute-done((bf16[256,256]{1,0:T(8,128)(2,1)S(1)}, bf16[256,256]{1,0:T(8,128)(2,1)S(1)}, u32[]{:S(2)}, u32[]{:S(2)}) %collective-permute-start) | collective-permute-done | bytes 131104 | tf_op jit(solution)/shard_map/ppermute | solution.py:175
  268.2 1.1 broadcast_in_dim.69
  269.2 4.5 %all-to-all-start.2 = ((bf16[4,2,256,256]{3,2,1,0:T(8,128)(2,1)}), bf16[4,2,256,256]{3,2,1,0:T(8,128)(2,1)S(1)}, u32[]{:S(2)}, u32[]{:S(2)}) async-start(bf16[4,2,256,256]{3,2,1,0:T(8,128)(2,1)} %broadcast_in_dim.69), calls=%async_computation.2 | async-start | bytes 2097152 | tf_op jit(solution)/shard_map/all_to_all | solution.py:178
  273.7 15.7 %all-to-all-done.2 = bf16[4,2,256,256]{3,2,1,0:T(8,128)(2,1)S(1)} async-done(((bf16[4,2,256,256]{3,2,1,0:T(8,128)(2,1)}), bf16[4,2,256,256]{3,2,1,0:T(8,128)(2,1)S(1)}, u32[]{:S(2)}, u32[]{:S(2)}) %all-to-all-start.2) | async-done | bytes 1048608 | tf_op jit(solution)/shard_map/all_to_all | solution.py:178
  289.7 1.0 fusion.10
  (48 shorter events, 3.4 us)
Async XLA Ops:
  0.0 289.4 %copy-start = (bf16[2048,256]{1,0:T(8,128)(2,1)S(1)}, bf16[2048,256]{1,0:T(8,128)(2,1)}, u32[]{:S(2)}) copy-start(bf16[2048,256]{1,0:T(8,128)(2,1)} %param.9) | copy-start | bytes 3145732
  1.4 238.1 %copy-start.5 = (s32[2,8,2]{1,2,0:T(2,128)}, s32[2,8,2]{1,2,0:T(2,128)S(1)}, u32[]{:S(2)}) copy-start(s32[2,8,2]{1,2,0:T(2,128)S(1)} %copy.45) | copy-start | bytes 388
  124.0 11.3 %copy-start.3 = (bf16[256,256]{1,0:T(8,128)(2,1)S(1)}, bf16[256,256]{1,0:T(8,128)(2,1)}, u32[]{:S(2)}) copy-start(bf16[256,256]{1,0:T(8,128)(2,1)} %param.5) | copy-start | bytes 393220
  124.0 115.5 %all-to-all-start.1 = ((bf16[64,144,128]{2,1,0:T(8,128)(2,1)}), bf16[64,144,128]{2,1,0:T(8,128)(2,1)S(1)}, u32[]{:S(2)}, u32[]{:S(2)}) async-start(bf16[64,144,128]{2,1,0:T(8,128)(2,1)} %constant_dynamic-update-slice_fusion), calls=%async_computation.1 | async-start | bytes 4718592 | tf_op jit(solution)/shard_map/all_to_all | solution.py:150
  135.3 104.6 %copy-start.4 = (pred[2,8,2]{1,2,0:T(4,128)(4,1)}, pred[2,8,2]{1,2,0:T(4,128)(4,1)S(1)}, u32[]{:S(2)}) copy-start(pred[2,8,2]{1,2,0:T(4,128)(4,1)S(1)} %copy.44) | copy-start | bytes 100
  136.5 0.8 copy-start.1
  241.0 0.7 copy-start.6
  241.3 1.7 copy-start.2
  243.3 24.8 %collective-permute-start = (bf16[256,256]{1,0:T(8,128)(2,1)S(1)}, bf16[256,256]{1,0:T(8,128)(2,1)S(1)}, u32[]{:S(2)}, u32[]{:S(2)}) collective-permute-start(bf16[256,256]{1,0:T(8,128)(2,1)S(1)} %bitcast.123), channel_id=1, source_target_pairs={{0,1},{1,0},{2,3},{3,2},{4,5},{5,4},{6,7},{7,6},{8,9},{9,8},{10,11... | collective-permute-start | bytes 393224 | tf_op jit(solution)/shard_map/ppermute | solution.py:175
  269.2 20.2 %all-to-all-start.2 = ((bf16[4,2,256,256]{3,2,1,0:T(8,128)(2,1)}), bf16[4,2,256,256]{3,2,1,0:T(8,128)(2,1)S(1)}, u32[]{:S(2)}, u32[]{:S(2)}) async-start(bf16[4,2,256,256]{3,2,1,0:T(8,128)(2,1)} %broadcast_in_dim.69), calls=%async_computation.2 | async-start | bytes 2097152 | tf_op jit(solution)/shard_map/all_to_all | solution.py:178

commit v16 on v15

--- a/solution.py
+++ b/solution.py
@@ -65,7 +65,7 @@
 
 def owner_attention(got, keys, values, scale, extra):
     sources, slots, rows, width = got.shape
-    step = 32
+    step = 64
     packed = (sources, slots * rows + extra, width)
     return pl.pallas_call(
         functools.partial(owner_kernel, scale),

time: 291 us -> 291 us (level)
  no operation moved by 1% of the time
where the time goes in v16:
time: 291 us
  waiting for transfers between devices  132 us (45%)
  blocking collectives  111 us (38%)
  starting transfers between devices  22.6 us (8%)
  local copies, waits for them, and re-layouts  8.94 us (3%)
  Pallas kernels  7.14 us (2%)
  matrix products  6.68 us (2%)
    all_to_all x1, blocking collectives, local(): lax.all_to_all(send_q, 'ctx', split_axis=0, concat_axis=0, tiled=True)  111 us
    all_to_all x1, waiting for transfers between devices, local(): lax.all_to_all(back, 'ctx', split_axis=0, concat_axis=0, tiled=True)  99.9 us
    ppermute x1, waiting for transfers between devices, local(): partner = lax.ppermute(attention, 'zh', [(0, 1), (1, 0)])  16.5 us
    all_to_all x1, waiting for transfers between devices, local(): lax.all_to_all(spread, 'y', split_axis=0, concat_axis=0, tiled=True)  15.7 us
    all_to_all x1, starting transfers between devices, local(): lax.all_to_all(back, 'ctx', split_axis=0, concat_axis=0, tiled=True)  9.91 us
    ppermute x1, starting transfers between devices, local(): partner = lax.ppermute(attention, 'zh', [(0, 1), (1, 0)])  8.22 us
    pallas_call x1, Pallas kernels, owner_attention(): pl.pallas_call(functools.partial(owner_kernel, scale), grid=(sources // s...  7.14 us
  transfers between devices with their start and end apart: 3, of which 3 were waited for; matrix products, arithmetic and copies ran while one was open for 2% of the time, Pallas kernels for 0%

profile of v16, /device:TPU:6, one launch (start us, length us, event | category | flops | bytes accessed | tf_op | source)
XLA Modules:
  0.0 290.7 jit_solution(5557250507490958118)
XLA Ops:
  0.0 0.8 slice.24
  1.5 1.0 reshape_reshape.3
  2.5 0.7 convolution_convert_fusion
  3.2 0.5 copy.86
  3.7 0.6 copy.47
  4.3 110.7 %all_to_all.15 = bf16[64,2,2,32,128]{4,3,2,1,0:T(8,128)(2,1)} all-to-all(bf16[64,2,2,32,128]{4,3,2,1,0:T(8,128)(2,1)S(1)} %copy.47), channel_id=1, replica_groups=mesh['ctx'=64,'y'=4,'zh'=2] {'ctx'}, dimensions={0} | all-to-all | bytes 4194304 | tf_op jit(solution)/shard_map/all_to_all | solution.py:135
  115.0 7.1 %shard_map.55 = (bf16[64,144,128]{2,1,0:T(8,128)(2,1)}, f32[4,2048]{1,0:T(4,128)}) custom-call(bf16[64,4,32,128]{3,2,1,0:T(8,128)(2,1)} %bitcast.111, bf16[256,256]{1,0:T(8,128)(2,1)} %k_ref.1, bf16[256,256]{1,0:T(8,128)(2,1)} %v_ref.1), custom_call_target="tpu_custom_call" | custom-call | flops 1610612736 | bytes 4227072 | tf_op jit(solution)/shard_map/pallas_call | solution.py:70
  122.1 0.9 reshape.187
  123.4 0.7 constant_dynamic-update-slice_fusion
  124.0 9.9 %all-to-all-start.1 = ((bf16[64,144,128]{2,1,0:T(8,128)(2,1)}), bf16[64,144,128]{2,1,0:T(8,128)(2,1)S(1)}, u32[]{:S(2)}, u32[]{:S(2)}) async-start(bf16[64,144,128]{2,1,0:T(8,128)(2,1)} %constant_dynamic-update-slice_fusion), calls=%async_computation.1 | async-start | bytes 4718592 | tf_op jit(solution)/shard_map/all_to_all | solution.py:150
  134.0 0.6 broadcast_compare_fusion
  134.5 0.8 copy.44
  135.4 1.1 fusion.55
  136.5 0.8 copy-done.1
  137.5 2.1 convolution_divide_fusion
  139.6 99.9 %all-to-all-done.1 = bf16[64,144,128]{2,1,0:T(8,128)(2,1)S(1)} async-done(((bf16[64,144,128]{2,1,0:T(8,128)(2,1)}), bf16[64,144,128]{2,1,0:T(8,128)(2,1)S(1)}, u32[]{:S(2)}, u32[]{:S(2)}) %all-to-all-start.1) | async-done | bytes 2359328 | tf_op jit(solution)/shard_map/all_to_all | solution.py:150
  240.0 0.8 fusion.52
  241.7 1.3 fusion.6
  243.3 8.2 %collective-permute-start = (bf16[256,256]{1,0:T(8,128)(2,1)S(1)}, bf16[256,256]{1,0:T(8,128)(2,1)S(1)}, u32[]{:S(2)}, u32[]{:S(2)}) collective-permute-start(bf16[256,256]{1,0:T(8,128)(2,1)S(1)} %bitcast.123), channel_id=1, source_target_pairs={{0,1},{1,0},{2,3},{3,2},{4,5},{5,4},{6,7},{7,6},{8,9},{9,8},{10,11... | collective-permute-start | bytes 393224 | tf_op jit(solution)/shard_map/ppermute | solution.py:175
  251.7 16.5 %collective-permute-done = bf16[256,256]{1,0:T(8,128)(2,1)S(1)} collective-permute-done((bf16[256,256]{1,0:T(8,128)(2,1)S(1)}, bf16[256,256]{1,0:T(8,128)(2,1)S(1)}, u32[]{:S(2)}, u32[]{:S(2)}) %collective-permute-start) | collective-permute-done | bytes 131104 | tf_op jit(solution)/shard_map/ppermute | solution.py:175
  268.2 1.1 broadcast_in_dim.69
  269.2 4.5 %all-to-all-start.2 = ((bf16[4,2,256,256]{3,2,1,0:T(8,128)(2,1)}), bf16[4,2,256,256]{3,2,1,0:T(8,128)(2,1)S(1)}, u32[]{:S(2)}, u32[]{:S(2)}) async-start(bf16[4,2,256,256]{3,2,1,0:T(8,128)(2,1)} %broadcast_in_dim.69), calls=%async_computation.2 | async-start | bytes 2097152 | tf_op jit(solution)/shard_map/all_to_all | solution.py:178
  273.7 15.7 %all-to-all-done.2 = bf16[4,2,256,256]{3,2,1,0:T(8,128)(2,1)S(1)} async-done(((bf16[4,2,256,256]{3,2,1,0:T(8,128)(2,1)}), bf16[4,2,256,256]{3,2,1,0:T(8,128)(2,1)S(1)}, u32[]{:S(2)}, u32[]{:S(2)}) %all-to-all-start.2) | async-done | bytes 1048608 | tf_op jit(solution)/shard_map/all_to_all | solution.py:178
  289.7 1.0 fusion.10
  (48 shorter events, 3.4 us)
Async XLA Ops:
  0.0 289.4 %copy-start = (bf16[2048,256]{1,0:T(8,128)(2,1)S(1)}, bf16[2048,256]{1,0:T(8,128)(2,1)}, u32[]{:S(2)}) copy-start(bf16[2048,256]{1,0:T(8,128)(2,1)} %param.9) | copy-start | bytes 3145732
  1.4 238.1 %copy-start.5 = (s32[2,8,2]{1,2,0:T(2,128)}, s32[2,8,2]{1,2,0:T(2,128)S(1)}, u32[]{:S(2)}) copy-start(s32[2,8,2]{1,2,0:T(2,128)S(1)} %copy.45) | copy-start | bytes 388
  124.0 11.3 %copy-start.3 = (bf16[256,256]{1,0:T(8,128)(2,1)S(1)}, bf16[256,256]{1,0:T(8,128)(2,1)}, u32[]{:S(2)}) copy-start(bf16[256,256]{1,0:T(8,128)(2,1)} %param.5) | copy-start | bytes 393220
  124.0 115.5 %all-to-all-start.1 = ((bf16[64,144,128]{2,1,0:T(8,128)(2,1)}), bf16[64,144,128]{2,1,0:T(8,128)(2,1)S(1)}, u32[]{:S(2)}, u32[]{:S(2)}) async-start(bf16[64,144,128]{2,1,0:T(8,128)(2,1)} %constant_dynamic-update-slice_fusion), calls=%async_computation.1 | async-start | bytes 4718592 | tf_op jit(solution)/shard_map/all_to_all | solution.py:150
  135.3 104.6 %copy-start.4 = (pred[2,8,2]{1,2,0:T(4,128)(4,1)}, pred[2,8,2]{1,2,0:T(4,128)(4,1)S(1)}, u32[]{:S(2)}) copy-start(pred[2,8,2]{1,2,0:T(4,128)(4,1)S(1)} %copy.44) | copy-start | bytes 100
  136.5 0.8 copy-start.1
  241.0 0.7 copy-start.6
  241.3 1.7 copy-start.2
  243.3 24.8 %collective-permute-start = (bf16[256,256]{1,0:T(8,128)(2,1)S(1)}, bf16[256,256]{1,0:T(8,128)(2,1)S(1)}, u32[]{:S(2)}, u32[]{:S(2)}) collective-permute-start(bf16[256,256]{1,0:T(8,128)(2,1)S(1)} %bitcast.123), channel_id=1, source_target_pairs={{0,1},{1,0},{2,3},{3,2},{4,5},{5,4},{6,7},{7,6},{8,9},{9,8},{10,11... | collective-permute-start | bytes 393224 | tf_op jit(solution)/shard_map/ppermute | solution.py:175
  269.2 20.2 %all-to-all-start.2 = ((bf16[4,2,256,256]{3,2,1,0:T(8,128)(2,1)}), bf16[4,2,256,256]{3,2,1,0:T(8,128)(2,1)S(1)}, u32[]{:S(2)}, u32[]{:S(2)}) async-start(bf16[4,2,256,256]{3,2,1,0:T(8,128)(2,1)} %broadcast_in_dim.69), calls=%async_computation.2 | async-start | bytes 2097152 | tf_op jit(solution)/shard_map/all_to_all | solution.py:178

commit v17 on v16

--- a/solution.py
+++ b/solution.py
@@ -121,15 +121,15 @@
     flat_hot = onehot.reshape(heads_loc, tiles * 2, sources)
     before = jnp.cumsum(flat_hot, axis=1) - flat_hot
     slot = jnp.sum(before * flat_hot, axis=-1).reshape(heads_loc, tiles, 2)
-    query_src = jnp.transpose(
-        quer_three.reshape(tiles, tile_rows, heads_loc, width), (2, 0, 1, 3)
-    ).reshape(heads_loc, tiles, tile_rows * width)
     flat_slot = target * CAP + slot
     route = (
         flat_slot[..., None] == jnp.arange(sources * CAP, dtype=jnp.int32)
     ).astype(jnp.bfloat16)
     send_q = jnp.einsum(
-        "htep,htx->phx", route, query_src, preferred_element_type=jnp.float32
+        "htep,trhd->phrd",
+        route,
+        quer_three.reshape(tiles, tile_rows, heads_loc, width),
+        preferred_element_type=jnp.float32,
     ).astype(jnp.bfloat16)
     send_q = send_q.reshape(sources, CAP, heads_loc, tile_rows, width)
     got_rows = lax.all_to_all(send_q, "ctx", split_axis=0, concat_axis=0, tiled=True)

time: 291 us -> 292 us (level)
  transfers between devices with their start and end apart: 3 -> 3, of which waited for: 3 -> 3; matrix products, arithmetic and copies ran while one was open for 2% -> 1% of each run, Pallas kernels for 0% -> 0%
where the time goes in v17:
time: 292 us; the launch traced here: 291 us
  waiting for transfers between devices  133 us (46%)
  blocking collectives  111 us (38%)
  starting transfers between devices  22.6 us (8%)
  local copies, waits for them, and re-layouts  9.64 us (3%)
  Pallas kernels  7.14 us (2%)
  matrix products  6.68 us (2%)
    all_to_all x1, blocking collectives, local(): lax.all_to_all(send_q, 'ctx', split_axis=0, concat_axis=0, tiled=True)  111 us
    all_to_all x1, waiting for transfers between devices, local(): lax.all_to_all(back, 'ctx', split_axis=0, concat_axis=0, tiled=True)  101 us
    ppermute x1, waiting for transfers between devices, local(): partner = lax.ppermute(attention, 'zh', [(0, 1), (1, 0)])  16.5 us
    all_to_all x1, waiting for transfers between devices, local(): lax.all_to_all(spread, 'y', split_axis=0, concat_axis=0, tiled=True)  15.7 us
    all_to_all x1, starting transfers between devices, local(): lax.all_to_all(back, 'ctx', split_axis=0, concat_axis=0, tiled=True)  9.92 us
    ppermute x1, starting transfers between devices, local(): partner = lax.ppermute(attention, 'zh', [(0, 1), (1, 0)])  8.22 us
    pallas_call x1, Pallas kernels, owner_attention(): pl.pallas_call(functools.partial(owner_kernel, scale), grid=(sources // s...  7.14 us
  transfers between devices with their start and end apart: 3, of which 3 were waited for; matrix products, arithmetic and copies ran while one was open for 1% of the time, Pallas kernels for 0%

profile of v17, /device:TPU:6, one launch (start us, length us, event | category | flops | bytes accessed | tf_op | source)
XLA Modules:
  0.0 291.4 jit_solution(14169765825788717154)
XLA Ops:
  0.0 0.8 slice.24
  1.5 1.0 reshape_reshape.3
  2.5 0.7 convolution_convert_fusion
  3.2 2.4 copy.47
  5.7 110.7 %all_to_all.15 = bf16[64,2,2,32,128]{4,3,2,1,0:T(8,128)(2,1)} all-to-all(bf16[64,2,2,32,128]{4,3,2,1,0:T(8,128)(2,1)S(1)} %copy.47), channel_id=1, replica_groups=mesh['ctx'=64,'y'=4,'zh'=2] {'ctx'}, dimensions={0} | all-to-all | bytes 4194304 | tf_op jit(solution)/shard_map/all_to_all | solution.py:135
  116.4 7.1 %shard_map.55 = (bf16[64,144,128]{2,1,0:T(8,128)(2,1)}, f32[4,2048]{1,0:T(4,128)}) custom-call(bf16[64,4,32,128]{3,2,1,0:T(8,128)(2,1)} %bitcast.106, bf16[256,256]{1,0:T(8,128)(2,1)} %k_ref.1, bf16[256,256]{1,0:T(8,128)(2,1)} %v_ref.1), custom_call_target="tpu_custom_call" | custom-call | flops 1610612736 | bytes 4227072 | tf_op jit(solution)/shard_map/pallas_call | solution.py:70
  123.5 0.9 reshape.183
  124.8 0.7 constant_dynamic-update-slice_fusion
  125.4 9.9 %all-to-all-start.1 = ((bf16[64,144,128]{2,1,0:T(8,128)(2,1)}), bf16[64,144,128]{2,1,0:T(8,128)(2,1)S(1)}, u32[]{:S(2)}, u32[]{:S(2)}) async-start(bf16[64,144,128]{2,1,0:T(8,128)(2,1)} %constant_dynamic-update-slice_fusion), calls=%async_computation.1 | async-start | bytes 4718592 | tf_op jit(solution)/shard_map/all_to_all | solution.py:150
  135.5 1.1 fusion.55
  136.7 0.8 copy-done.1
  137.6 2.1 convolution_divide_fusion
  139.7 101.2 %all-to-all-done.1 = bf16[64,144,128]{2,1,0:T(8,128)(2,1)S(1)} async-done(((bf16[64,144,128]{2,1,0:T(8,128)(2,1)}), bf16[64,144,128]{2,1,0:T(8,128)(2,1)S(1)}, u32[]{:S(2)}, u32[]{:S(2)}) %all-to-all-start.1) | async-done | bytes 2359328 | tf_op jit(solution)/shard_map/all_to_all | solution.py:150
  241.7 0.3 slice.36
  242.0 0.4 copy-done.5
  242.4 1.3 fusion.6
  243.6 0.2 fusion.36
  244.0 8.2 %collective-permute-start = (bf16[256,256]{1,0:T(8,128)(2,1)S(1)}, bf16[256,256]{1,0:T(8,128)(2,1)S(1)}, u32[]{:S(2)}, u32[]{:S(2)}) collective-permute-start(bf16[256,256]{1,0:T(8,128)(2,1)S(1)} %bitcast.117), channel_id=1, source_target_pairs={{0,1},{1,0},{2,3},{3,2},{4,5},{5,4},{6,7},{7,6},{8,9},{9,8},{10,11... | collective-permute-start | bytes 393224 | tf_op jit(solution)/shard_map/ppermute | solution.py:175
  252.4 16.5 %collective-permute-done = bf16[256,256]{1,0:T(8,128)(2,1)S(1)} collective-permute-done((bf16[256,256]{1,0:T(8,128)(2,1)S(1)}, bf16[256,256]{1,0:T(8,128)(2,1)S(1)}, u32[]{:S(2)}, u32[]{:S(2)}) %collective-permute-start) | collective-permute-done | bytes 131104 | tf_op jit(solution)/shard_map/ppermute | solution.py:175
  268.9 1.1 broadcast_in_dim.69
  269.9 4.5 %all-to-all-start.2 = ((bf16[4,2,256,256]{3,2,1,0:T(8,128)(2,1)}), bf16[4,2,256,256]{3,2,1,0:T(8,128)(2,1)S(1)}, u32[]{:S(2)}, u32[]{:S(2)}) async-start(bf16[4,2,256,256]{3,2,1,0:T(8,128)(2,1)} %broadcast_in_dim.69), calls=%async_computation.2 | async-start | bytes 2097152 | tf_op jit(solution)/shard_map/all_to_all | solution.py:178
  274.4 15.7 %all-to-all-done.2 = bf16[4,2,256,256]{3,2,1,0:T(8,128)(2,1)S(1)} async-done(((bf16[4,2,256,256]{3,2,1,0:T(8,128)(2,1)}), bf16[4,2,256,256]{3,2,1,0:T(8,128)(2,1)S(1)}, u32[]{:S(2)}, u32[]{:S(2)}) %all-to-all-start.2) | async-done | bytes 1048608 | tf_op jit(solution)/shard_map/all_to_all | solution.py:178
  290.1 0.3 convolution_bitcast_fusion
  290.4 1.0 fusion.10
  (45 shorter events, 2.4 us)
Async XLA Ops:
  0.0 290.1 %copy-start = (bf16[2048,256]{1,0:T(8,128)(2,1)S(1)}, bf16[2048,256]{1,0:T(8,128)(2,1)}, u32[]{:S(2)}) copy-start(bf16[2048,256]{1,0:T(8,128)(2,1)} %param.9) | copy-start | bytes 3145732
  1.4 239.5 %copy-start.4 = (s32[2,8,2]{1,2,0:T(2,128)}, s32[2,8,2]{1,2,0:T(2,128)S(1)}, u32[]{:S(2)}) copy-start(s32[2,8,2]{1,2,0:T(2,128)S(1)} %copy.45) | copy-start | bytes 388
  125.4 10.1 %copy-start.3 = (bf16[256,256]{1,0:T(8,128)(2,1)S(1)}, bf16[256,256]{1,0:T(8,128)(2,1)}, u32[]{:S(2)}) copy-start(bf16[256,256]{1,0:T(8,128)(2,1)} %param.5) | copy-start | bytes 393220
  125.4 115.5 %all-to-all-start.1 = ((bf16[64,144,128]{2,1,0:T(8,128)(2,1)}), bf16[64,144,128]{2,1,0:T(8,128)(2,1)S(1)}, u32[]{:S(2)}, u32[]{:S(2)}) async-start(bf16[64,144,128]{2,1,0:T(8,128)(2,1)} %constant_dynamic-update-slice_fusion), calls=%async_computation.1 | async-start | bytes 4718592 | tf_op jit(solution)/shard_map/all_to_all | solution.py:150
  136.7 0.8 copy-start.1
  241.7 0.7 copy-start.5
  242.0 1.7 copy-start.2
  244.0 24.8 %collective-permute-start = (bf16[256,256]{1,0:T(8,128)(2,1)S(1)}, bf16[256,256]{1,0:T(8,128)(2,1)S(1)}, u32[]{:S(2)}, u32[]{:S(2)}) collective-permute-start(bf16[256,256]{1,0:T(8,128)(2,1)S(1)} %bitcast.117), channel_id=1, source_target_pairs={{0,1},{1,0},{2,3},{3,2},{4,5},{5,4},{6,7},{7,6},{8,9},{9,8},{10,11... | collective-permute-start | bytes 393224 | tf_op jit(solution)/shard_map/ppermute | solution.py:175
  269.9 20.2 %all-to-all-start.2 = ((bf16[4,2,256,256]{3,2,1,0:T(8,128)(2,1)}), bf16[4,2,256,256]{3,2,1,0:T(8,128)(2,1)S(1)}, u32[]{:S(2)}, u32[]{:S(2)}) async-start(bf16[4,2,256,256]{3,2,1,0:T(8,128)(2,1)} %broadcast_in_dim.69), calls=%async_computation.2 | async-start | bytes 2097152 | tf_op jit(solution)/shard_map/all_to_all | solution.py:178

commit v18 on v16

--- a/solution.py
+++ b/solution.py
@@ -35,19 +35,24 @@
     return part / total[..., None], top + jnp.log(total)
 
 
-def owner_kernel(scale, q_ref, k_ref, v_ref, part_ref, lse_ref):
+def owner_kernel(scale, q_ref, k_ref, v_ref, part_ref):
     groups = q_ref.shape[0]
     slots = q_ref.shape[1]
     rows = q_ref.shape[2]
     width = q_ref.shape[3]
     heads = k_ref.shape[1] // width
+    lanes = groups * rows
     nt = (((1,), (1,)), ((), ()))
     tn = (((0,), (0,)), ((), ()))
     tail = part_ref.shape[1] - slots * rows
     part_ref[:, pl.ds(slots * rows, tail)] = jnp.zeros((groups, tail, width), part_ref.dtype)
+    owner = lax.broadcasted_iota(jnp.int32, (groups, lanes), 1) // rows
+    mask = owner == lax.broadcasted_iota(jnp.int32, (groups, lanes), 0)
+    src_lane = lax.broadcasted_iota(jnp.int32, (lanes, width), 0) % rows
+    dst_lane = lax.broadcasted_iota(jnp.int32, (lanes, width), 1)
     for j in range(slots):
         cols = pl.ds((j % heads) * width, width)
-        q = q_ref[:, j].reshape(groups * rows, width)
+        q = q_ref[:, j].reshape(lanes, width)
         k = k_ref[:, cols]
         v = v_ref[:, cols]
         s_t = lax.dot_general(k, q, nt, preferred_element_type=jnp.float32) * scale
@@ -60,33 +65,40 @@
         part_ref[:, pl.ds(j * rows, rows)] = out_t.T.reshape(groups, rows, width).astype(
             part_ref.dtype
         )
-        lse_ref[pl.ds(j, 1), :] = top_t + jnp.log(total_t)
+        lse = top_t + jnp.log(total_t)
+        hi = lse.astype(jnp.bfloat16)
+        rest = lse - hi.astype(jnp.float32)
+        mid = rest.astype(jnp.bfloat16)
+        lo = (rest - mid.astype(jnp.float32)).astype(jnp.bfloat16)
+        packed = jnp.zeros((groups, width), jnp.float32)
+        for p, piece in enumerate((hi, mid, lo)):
+            spread = jnp.where(mask, jnp.broadcast_to(piece, (groups, lanes)), 0).astype(
+                jnp.bfloat16
+            )
+            place = (dst_lane == src_lane + p * rows).astype(jnp.bfloat16)
+            packed = packed + jnp.dot(spread, place, preferred_element_type=jnp.float32)
+        part_ref[:, pl.ds(slots * rows + j, 1)] = packed.reshape(groups, 1, width).astype(
+            part_ref.dtype
+        )
 
 
 def owner_attention(got, keys, values, scale, extra):
     sources, slots, rows, width = got.shape
-    step = 64
     packed = (sources, slots * rows + extra, width)
     return pl.pallas_call(
         functools.partial(owner_kernel, scale),
-        grid=(sources // step,),
+        grid=(1,),
         in_specs=[
-            pl.BlockSpec((step, slots, rows, width), lambda i: (i, 0, 0, 0)),
+            pl.BlockSpec(got.shape, lambda i: (0, 0, 0, 0)),
             pl.BlockSpec(keys.shape, lambda i: (0, 0)),
             pl.BlockSpec(values.shape, lambda i: (0, 0)),
         ],
-        out_specs=[
-            pl.BlockSpec((step,) + packed[1:], lambda i: (i, 0, 0)),
-            pl.BlockSpec((slots, step * rows), lambda i: (0, i)),
-        ],
-        out_shape=[
-            jax.ShapeDtypeStruct(packed, jnp.bfloat16),
-            jax.ShapeDtypeStruct((slots, sources * rows), jnp.float32),
-        ],
+        out_specs=pl.BlockSpec(packed, lambda i: (0, 0, 0)),
+        out_shape=jax.ShapeDtypeStruct(packed, jnp.bfloat16),
         cost_estimate=pl.CostEstimate(
             flops=6 * sources * slots * rows * keys.shape[0] * width,
             transcendentals=2 * sources * slots * rows * keys.shape[0],
-            bytes_accessed=2 * got.size * 2 + 4 * slots * sources * rows,
+            bytes_accessed=2 * got.size * 2,
         ),
     )(got, keys, values)
 
@@ -136,17 +148,9 @@
 
     rows_part = CAP * heads_loc * tile_rows
     extra = -(rows_part + CAP * heads_loc) % 16 + CAP * heads_loc
-    back, lse = owner_attention(
+    back = owner_attention(
         got_rows.reshape(sources, CAP * heads_loc, tile_rows, width), keys, values, scale, extra
     )
-    pieces = split_bf16(lse.reshape(CAP, heads_loc, sources, tile_rows))
-    pieces = jnp.concatenate(
-        [pieces, jnp.zeros((LANE_ROWS - 3,) + pieces.shape[1:], pieces.dtype)], axis=0
-    )
-    lse_rows = jnp.transpose(pieces, (3, 1, 2, 0, 4)).reshape(
-        sources, CAP * heads_loc, LANE_ROWS * tile_rows
-    )
-    back = lax.dynamic_update_slice_in_dim(back, lse_rows, rows_part, axis=1)
     got_back = lax.all_to_all(back, "ctx", split_axis=0, concat_axis=0, tiled=True)
     got_out = got_back[:, :rows_part].reshape(sources * CAP, heads_loc, tile_rows, width)
     got_lse = got_back[:, rows_part : rows_part + CAP * heads_loc].reshape(

time: 291 us -> 290 us (level)
  transfers between devices with their start and end apart: 3 -> 3, of which waited for: 3 -> 3; matrix products, arithmetic and copies ran while one was open for 2% -> 1% of each run, Pallas kernels for 0% -> 0%
where the time goes in v18:
time: 290 us; the launch traced here: 289 us
  waiting for transfers between devices  133 us (46%)
  blocking collectives  111 us (38%)
  starting transfers between devices  22.6 us (8%)
  Pallas kernels  8.36 us (3%)
  matrix products  6.69 us (2%)
  local copies, waits for them, and re-layouts  6.48 us (2%)
    all_to_all x1, blocking collectives, local(): lax.all_to_all(send_q, 'ctx', split_axis=0, concat_axis=0, tiled=True)  111 us
    all_to_all x1, waiting for transfers between devices, local(): lax.all_to_all(back, 'ctx', split_axis=0, concat_axis=0, tiled=True)  101 us
    ppermute x1, waiting for transfers between devices, local(): partner = lax.ppermute(attention, 'zh', [(0, 1), (1, 0)])  16.5 us
    all_to_all x1, waiting for transfers between devices, local(): lax.all_to_all(spread, 'y', split_axis=0, concat_axis=0, tiled=True)  15.7 us
    all_to_all x1, starting transfers between devices, local(): lax.all_to_all(back, 'ctx', split_axis=0, concat_axis=0, tiled=True)  9.91 us
    pallas_call x1, Pallas kernels, owner_attention(): pl.pallas_call(functools.partial(owner_kernel, scale), grid=(1,), in_spec...  8.36 us
    ppermute x1, starting transfers between devices, local(): partner = lax.ppermute(attention, 'zh', [(0, 1), (1, 0)])  8.22 us
  transfers between devices with their start and end apart: 3, of which 3 were waited for; matrix products, arithmetic and copies ran while one was open for 1% of the time, Pallas kernels for 0%

profile of v18, /device:TPU:6, one launch (start us, length us, event | category | flops | bytes accessed | tf_op | source)
XLA Modules:
  0.0 289.4 jit_solution(7483132586010318061)
XLA Ops:
  0.0 0.8 slice.24
  1.1 0.2 select_reduce_fusion
  1.5 1.0 reshape_reshape.3
  2.5 0.7 convolution_convert_fusion
  3.2 0.5 copy.81
  3.7 0.6 copy.44
  4.3 110.7 %all_to_all.15 = bf16[64,2,2,32,128]{4,3,2,1,0:T(8,128)(2,1)} all-to-all(bf16[64,2,2,32,128]{4,3,2,1,0:T(8,128)(2,1)S(1)} %copy.44), channel_id=1, replica_groups=mesh['ctx'=64,'y'=4,'zh'=2] {'ctx'}, dimensions={0} | all-to-all | bytes 4194304 | tf_op jit(solution)/shard_map/all_to_all | solution.py:147
  115.0 8.4 %shard_map.55 = bf16[64,144,128]{2,1,0:T(8,128)(2,1)} custom-call(bf16[64,4,32,128]{3,2,1,0:T(8,128)(2,1)} %bitcast.109, bf16[256,256]{1,0:T(8,128)(2,1)} %k_ref.1, bf16[256,256]{1,0:T(8,128)(2,1)} %v_ref.1), custom_call_target="tpu_custom_call" | custom-call | flops 1610612736 | bytes 4194304 | tf_op jit(solution)/shard_map/pallas_call | solution.py:88
  123.4 9.9 %all-to-all-start.1 = ((bf16[64,144,128]{2,1,0:T(8,128)(2,1)}), bf16[64,144,128]{2,1,0:T(8,128)(2,1)S(1)}, u32[]{:S(2)}, u32[]{:S(2)}) async-start(bf16[64,144,128]{2,1,0:T(8,128)(2,1)} %shard_map.55), calls=%async_computation.1 | async-start | bytes 4718592 | tf_op jit(solution)/shard_map/all_to_all | solution.py:154
  133.4 1.2 fusion.48
  134.6 0.8 copy-done.1
  135.6 2.1 convolution_divide_fusion
  137.7 101.2 %all-to-all-done.1 = bf16[64,144,128]{2,1,0:T(8,128)(2,1)S(1)} async-done(((bf16[64,144,128]{2,1,0:T(8,128)(2,1)}), bf16[64,144,128]{2,1,0:T(8,128)(2,1)S(1)}, u32[]{:S(2)}, u32[]{:S(2)}) %all-to-all-start.1) | async-done | bytes 2359328 | tf_op jit(solution)/shard_map/all_to_all | solution.py:154
  239.6 0.3 slice.36
  239.9 0.4 copy-done.5
  240.3 1.2 fusion.6
  241.6 0.2 fusion.30
  242.0 8.2 %collective-permute-start = (bf16[256,256]{1,0:T(8,128)(2,1)S(1)}, bf16[256,256]{1,0:T(8,128)(2,1)S(1)}, u32[]{:S(2)}, u32[]{:S(2)}) collective-permute-start(bf16[256,256]{1,0:T(8,128)(2,1)S(1)} %bitcast.119), channel_id=1, source_target_pairs={{0,1},{1,0},{2,3},{3,2},{4,5},{5,4},{6,7},{7,6},{8,9},{9,8},{10,11... | collective-permute-start | bytes 393224 | tf_op jit(solution)/shard_map/ppermute | solution.py:179
  250.3 16.5 %collective-permute-done = bf16[256,256]{1,0:T(8,128)(2,1)S(1)} collective-permute-done((bf16[256,256]{1,0:T(8,128)(2,1)S(1)}, bf16[256,256]{1,0:T(8,128)(2,1)S(1)}, u32[]{:S(2)}, u32[]{:S(2)}) %collective-permute-start) | collective-permute-done | bytes 131104 | tf_op jit(solution)/shard_map/ppermute | solution.py:179
  266.8 1.1 broadcast_in_dim.68
  267.9 4.5 %all-to-all-start.2 = ((bf16[4,2,256,256]{3,2,1,0:T(8,128)(2,1)}), bf16[4,2,256,256]{3,2,1,0:T(8,128)(2,1)S(1)}, u32[]{:S(2)}, u32[]{:S(2)}) async-start(bf16[4,2,256,256]{3,2,1,0:T(8,128)(2,1)} %broadcast_in_dim.68), calls=%async_computation.2 | async-start | bytes 2097152 | tf_op jit(solution)/shard_map/all_to_all | solution.py:182
  272.3 15.7 %all-to-all-done.2 = bf16[4,2,256,256]{3,2,1,0:T(8,128)(2,1)S(1)} async-done(((bf16[4,2,256,256]{3,2,1,0:T(8,128)(2,1)}), bf16[4,2,256,256]{3,2,1,0:T(8,128)(2,1)S(1)}, u32[]{:S(2)}, u32[]{:S(2)}) %all-to-all-start.2) | async-done | bytes 1048608 | tf_op jit(solution)/shard_map/all_to_all | solution.py:182
  288.1 0.3 convolution_bitcast_fusion
  288.4 1.0 fusion.10
  (40 shorter events, 1.9 us)
Async XLA Ops:
  0.0 288.1 %copy-start = (bf16[2048,256]{1,0:T(8,128)(2,1)S(1)}, bf16[2048,256]{1,0:T(8,128)(2,1)}, u32[]{:S(2)}) copy-start(bf16[2048,256]{1,0:T(8,128)(2,1)} %param.9) | copy-start | bytes 3145732
  1.4 237.4 %copy-start.4 = (s32[2,8,2]{1,2,0:T(2,128)}, s32[2,8,2]{1,2,0:T(2,128)S(1)}, u32[]{:S(2)}) copy-start(s32[2,8,2]{1,2,0:T(2,128)S(1)} %copy.42) | copy-start | bytes 388
  123.4 10.1 %copy-start.3 = (bf16[256,256]{1,0:T(8,128)(2,1)S(1)}, bf16[256,256]{1,0:T(8,128)(2,1)}, u32[]{:S(2)}) copy-start(bf16[256,256]{1,0:T(8,128)(2,1)} %param.5) | copy-start | bytes 393220
  123.4 115.5 %all-to-all-start.1 = ((bf16[64,144,128]{2,1,0:T(8,128)(2,1)}), bf16[64,144,128]{2,1,0:T(8,128)(2,1)S(1)}, u32[]{:S(2)}, u32[]{:S(2)}) async-start(bf16[64,144,128]{2,1,0:T(8,128)(2,1)} %shard_map.55), calls=%async_computation.1 | async-start | bytes 4718592 | tf_op jit(solution)/shard_map/all_to_all | solution.py:154
  134.6 0.8 copy-start.1
  239.6 0.7 copy-start.5
  239.9 1.7 copy-start.2
  242.0 24.8 %collective-permute-start = (bf16[256,256]{1,0:T(8,128)(2,1)S(1)}, bf16[256,256]{1,0:T(8,128)(2,1)S(1)}, u32[]{:S(2)}, u32[]{:S(2)}) collective-permute-start(bf16[256,256]{1,0:T(8,128)(2,1)S(1)} %bitcast.119), channel_id=1, source_target_pairs={{0,1},{1,0},{2,3},{3,2},{4,5},{5,4},{6,7},{7,6},{8,9},{9,8},{10,11... | collective-permute-start | bytes 393224 | tf_op jit(solution)/shard_map/ppermute | solution.py:179
  267.9 20.2 %all-to-all-start.2 = ((bf16[4,2,256,256]{3,2,1,0:T(8,128)(2,1)}), bf16[4,2,256,256]{3,2,1,0:T(8,128)(2,1)S(1)}, u32[]{:S(2)}, u32[]{:S(2)}) async-start(bf16[4,2,256,256]{3,2,1,0:T(8,128)(2,1)} %broadcast_in_dim.68), calls=%async_computation.2 | async-start | bytes 2097152 | tf_op jit(solution)/shard_map/all_to_all | solution.py:182
